TPU v7x, 32 devices: a whole 2x2x4 slice. The times are simulated.
32 devices in a mesh: inline: 4 (over x, core), xline: 8 (over z, y).
Axes of the slice: x: 2, y: 2, z: 4, core: 2. Of those that a mesh axis runs over, the one named last changes fastest.
Arguments:
- image: bfloat16 [128, 512, 1024], P('inline', 'xline'), may hold values from -6 to 6
- weights: bfloat16 [4, 8, 2048, 1024], P('inline', 'xline'), may hold values from -0.1875 to 0.1875
- observed: bfloat16 [4096, 2048], P(('inline', 'xline')), may hold values from -6 to 6
- wavelet: float32 [33], replicated, may hold values from -0.375 to 0.375
- taps: float32 [9], replicated, may hold values from 0.1 to 0.6
- aperture: int32 [512, 8], P(('inline', 'xline')), may hold values from 0 to 31, all different within a row; in each aligned block of 16 rows (0 to 15, 16 to 31, ...) at most 8 rows name the same one
- landing: int32 [4096, 8], P(('inline', 'xline')), may hold values from 0 to 2047
Outputs:
- gradient: float32 [128, 512, 1024], P('inline', 'xline')
- residual: float32 [4096, 2048], P(('inline', 'xline'))
Inputs may be any that keep to these rules, and one draw needn't show every extreme that they name: `aperture`: each row names 8 different tiles; within the 16 rows of one device no tile is named more than 8 times, a bound that some block reaches. Tile i * 8 + j is the image tile of inline index i and crossline index j. `landing`: A column index a * 64 + b within a tile.
All inputs are finite; a program needn't handle non-finite values.
Results may differ from a plain program's by a relative error of at most 0.0035.
Values may be sent and summed in bfloat16 or wider, within the bound.
No kernel may reach another device: no remote copies, remote signals or barrier semaphores. Data moves between devices by JAX's collectives and lax.ppermute only.
A program may use at most 128 MiB of HBM per device.

v0:
```python
import jax
import jax.numpy as jnp
from jax import lax
from jax.sharding import PartitionSpec as P


def extended(block, sides, width):
    for axis, dim in sides:
        count = lax.axis_size(axis)
        forward = [(i, i + 1) for i in range(count - 1)]
        backward = [(target, source) for source, target in forward]
        low = lax.ppermute(
            lax.slice_in_dim(block, block.shape[dim] - width, None, axis=dim), axis, forward
        )
        high = lax.ppermute(lax.slice_in_dim(block, 0, width, axis=dim), axis, backward)
        block = jnp.concatenate([low, block, high], axis=dim)
    return block


def convolve(signal, wavelet):
    pad_width = wavelet.shape[0] // 2
    padded = jnp.pad(signal, ((0, 0), (pad_width, pad_width)))
    length = signal.shape[1]
    result = jnp.zeros_like(signal)
    for offset in range(wavelet.shape[0]):
        start = 2 * pad_width - offset
        result = result + wavelet[offset] * padded[:, start : start + length]
    return result


def correlate(signal, wavelet):
    pad_width = wavelet.shape[0] // 2
    padded = jnp.pad(signal, ((0, 0), (pad_width, pad_width)))
    length = signal.shape[1]
    result = jnp.zeros_like(signal)
    for offset in range(wavelet.shape[0]):
        result = result + wavelet[offset] * padded[:, offset : offset + length]
    return result


def filter_padded(padded, taps, axis):
    length = padded.shape[axis] - 8
    shape_out = list(padded.shape)
    shape_out[axis] = length
    result = jnp.zeros(tuple(shape_out), jnp.float32)
    for offset in range(9):
        result = result + taps[offset] * lax.slice_in_dim(
            padded, offset, offset + length, axis=axis
        )
    return result


def traverse(blocks):
    return lax.all_to_all(blocks, ("inline", "xline"), split_axis=0, concat_axis=0, tiled=True)


def local(image, weights, observed, wavelet, taps, aperture, landing):
    device_count = lax.axis_size("inline") * lax.axis_size("xline")
    block_count, aperture_len = aperture.shape
    trace_count, samples = observed.shape
    per_block = trace_count // block_count
    rows_x, rows_y, depth_len = image.shape
    cell_count = rows_x * rows_y
    capacity = 2 * max(1, block_count * aperture_len // device_count)
    item_count = block_count * aperture_len
    target_tile = aperture.reshape(item_count)
    onehot = (target_tile[:, None] == jnp.arange(device_count, dtype=jnp.int32)[None, :]).astype(
        jnp.int32
    )
    before = jnp.cumsum(onehot, axis=0) - onehot
    slot_index = jnp.sum(before * onehot, axis=1)
    target_slot = target_tile * capacity + slot_index
    item_cells = (
        landing.reshape(block_count, per_block, aperture_len)
        .transpose(0, 2, 1)
        .reshape(item_count, per_block)
    )
    cell_send = (
        jnp.zeros((device_count * capacity, per_block), jnp.int32).at[target_slot].set(item_cells)
    )
    cell_recv = lax.all_to_all(
        cell_send.reshape(device_count, capacity * per_block),
        ("inline", "xline"),
        split_axis=0,
        concat_axis=0,
        tiled=True,
    )
    cell_recv = cell_recv.reshape(device_count * capacity * per_block)
    tile_rows = image.reshape(cell_count, depth_len)
    weight_matrix = weights.reshape(samples, depth_len)
    contract = (((1,), (1,)), ((), ()))
    tile_table = lax.dot_general(
        tile_rows, weight_matrix, contract, preferred_element_type=jnp.float32
    )
    predicted = jnp.take(tile_table.astype(jnp.bfloat16), cell_recv, axis=0)
    outgoing = predicted.reshape(device_count, capacity * per_block, samples)
    returned = traverse(outgoing).reshape(device_count * capacity, per_block, samples)
    own_preds = jnp.take(returned, target_slot, axis=0).reshape(
        block_count, aperture_len, per_block, samples
    )
    synthetic = jnp.sum(own_preds.astype(jnp.float32), axis=1).reshape(trace_count, samples)
    modeled = convolve(synthetic, wavelet)
    residual = modeled - observed.astype(jnp.float32)
    adjoint = correlate(residual, wavelet).astype(jnp.bfloat16)
    adjoint_items = jnp.broadcast_to(
        adjoint.reshape(block_count, 1, per_block, samples),
        (block_count, aperture_len, per_block, samples),
    )
    adjoint_items = adjoint_items.reshape(item_count, per_block, samples)
    outbound = (
        jnp.zeros((device_count * capacity, per_block, samples), jnp.bfloat16)
        .at[target_slot]
        .set(adjoint_items)
    )
    arrived = traverse(outbound.reshape(device_count, capacity * per_block, samples))
    arrived = arrived.reshape(device_count * capacity * per_block, samples)
    gathered = jax.ops.segment_sum(arrived.astype(jnp.float32), cell_recv, num_segments=cell_count)
    raw_gradient = jnp.dot(
        gathered, weight_matrix.astype(jnp.float32), precision=lax.Precision.HIGHEST
    )
    raw_gradient = raw_gradient.reshape(rows_x, rows_y, depth_len)
    depth_padded = jnp.pad(raw_gradient, ((0, 0), (0, 0), (4, 4)))
    smooth_z = filter_padded(depth_padded, taps, 2)
    inline_wide = extended(smooth_z, (("inline", 0),), 4)
    smooth_x = filter_padded(inline_wide, taps, 0)
    xline_wide = extended(smooth_x, (("xline", 1),), 4)
    gradient = filter_padded(xline_wide, taps, 1)
    return (gradient, residual)


def solution(mesh):
    return jax.shard_map(
        local,
        mesh=mesh,
        in_specs=(
            P("inline", "xline", None),
            P("inline", "xline", None, None),
            P(("inline", "xline"), None),
            P(),
            P(),
            P(("inline", "xline"), None),
            P(("inline", "xline"), None),
        ),
        out_specs=(P("inline", "xline", None), P(("inline", "xline"), None)),
        check_vma=False,
    )
```

profile of v0, /device:TPU:1, one launch (start us, length us, event | category | flops | bytes accessed | tf_op | source)
XLA Modules:
  0.0 764.1 jit_solution(5605356831083066823)
XLA Ops:
  4.5 7.1 all-to-all-start
  11.6 14.0 %convolution_convert_fusion = bf16[2048,2048]{1,0:T(8,128)(2,1)} fusion(bf16[2048,1024]{1,0:T(8,128)(2,1)} %bitcast.89, bf16[1,1,2048,1024]{3,2,1,0:T(8,128)(2,1)} %param.8), kind=kOutput, calls=%fused_computation.106 | convolution fusion | flops 8594128896 | bytes 16777216 | tf_op jit(solution)/shard_map/dot_general | solution.py:92
  25.7 20.8 %gather_fusion = bf16[2048,2048]{1,0:T(8,128)(2,1)} fusion(bf16[2048,2048]{1,0:T(8,128)(2,1)} %convolution_convert_fusion, s32[2048]{0:T(1024)S(1)} %broadcast_clamp_fusion), kind=kCustom, calls=%fused_computation | custom fusion | bytes 16785408 | tf_op jit(solution)/shard_map/jit(_take)/gather | solution.py:95
  46.5 7.6 broadcast_select_fusion
  54.1 6.4 all-to-all-start.1
  62.0 187.1 %all-to-all-done.1 = bf16[32,64,2048]{2,1,0:T(8,128)(2,1)} async-done(((bf16[32,64,2048]{2,1,0:T(8,128)(2,1)}), bf16[32,64,2048]{2,1,0:T(8,128)(2,1)}, u32[]{:S(2)}, u32[]{:S(2)}) %all-to-all-start.1) | async-done | bytes 8388640 | tf_op jit(solution)/shard_map/all_to_all | solution.py:54
  249.1 6.2 gather_fusion.1
  255.3 3.5 convert_reduce_fusion
  258.8 29.3 %convert_subtract_fusion = f32[128,2048]{1,0:T(8,128)S(1)} fusion(bf16[128,2048]{1,0:T(8,128)(2,1)S(1)} %copy-done.3, f32[128,2048]{1,0:T(8,128)S(1)} %bitcast.84, f32[]{:T(128)} %bitcast.46, f32[]{:T(128)} %bitcast.45, f32[]{:T(128)} %bitcast.44, f32[]{:T(128)} %bitcast.43, f32[]{:T(128)} %bitcast.42, f32[]{:T(128)} %bitcast.41, f32[]{:T(128)} %bitcast.40, ...), kind=kLoop, calls=%fused_computation.155 | loop fusion | flops 17563648 | bytes 2621572 | tf_op jit(solution)/shard_map/sub | solution.py:103
  288.2 29.2 %fusion.124 = bf16[16,8,2048]{2,1,0:T(8,128)(2,1)S(1)} fusion(f32[]{:T(128)} %bitcast.46, f32[]{:T(128)} %bitcast.45, f32[]{:T(128)} %bitcast.44, f32[]{:T(128)} %bitcast.43, f32[]{:T(128)} %bitcast.42, f32[]{:T(128)} %bitcast.41, f32[]{:T(128)} %bitcast.40, f32[]{:T(128)} %bitcast.39, f32[]{:T(128)} %bitcast.38, f32[]{:T(128)} %bitcast.37, f32[]{:T(128)} %bitcast.36, ...), kind=kLoop, calls=%fused_computation.200 | loop fusion | flops 17301504 | bytes 1572996 | tf_op jit(solution)/shard_map/broadcast_in_dim | solution.py:105
  319.8 4.5 broadcast_in_dim.41
  324.3 19.3 %scatter_fusion = bf16[256,8,2048]{2,1,0:T(8,128)(2,1)} fusion(bf16[256,8,2048]{2,1,0:T(8,128)(2,1)} %broadcast_in_dim.41, s32[128]{0:T(128)S(1)} %fusion.128, bf16[128,8,2048]{2,1,0:T(8,128)(2,1)} %bitcast.83), kind=kCustom, calls=%fused_computation.3 | custom fusion | bytes 12583424 | tf_op jit(solution)/shard_map/scatter | solution.py:113
  343.6 4.8 all-to-all-start.2
  350.4 186.9 %all-to-all-done.2 = bf16[32,64,2048]{2,1,0:T(8,128)(2,1)} async-done(((bf16[32,64,2048]{2,1,0:T(8,128)(2,1)}), bf16[32,64,2048]{2,1,0:T(8,128)(2,1)}, u32[]{:S(2)}, u32[]{:S(2)}) %all-to-all-start.2) | async-done | bytes 8388640 | tf_op jit(solution)/shard_map/all_to_all | solution.py:54
  537.2 34.5 %scatter_custom_fusion.2 = f32[2048,2048]{1,0:T(8,128)} fusion(s32[2048]{0:T(1024)S(1)} %reshape.171, bf16[2048,2048]{1,0:T(8,128)(2,1)} %bitcast.61, f32[]{:T(128)} %constant.23.clone.1), kind=kCustom, calls=%fused_computation.11 | custom fusion | flops 8388608 | bytes 25165828 | tf_op jit(solution)/shard_map/scatter-add | solution.py:117
  571.7 31.5 %fusion.63 = f32[32,64,1024]{2,1,0:T(8,128)} fusion(f32[32,64,2048]{2,1,0:T(8,128)} %bitcast.82, bf16[1,1,2048,1024]{3,2,1,0:T(8,128)(2,1)} %param.8), kind=kOutput, calls=%fused_computation.107 | convolution fusion | flops 51539607552 | bytes 29360128 | tf_op jit(solution)/shard_map/dot_general | solution.py:118
  603.2 45.4 %fusion.10 = f32[32,64,1024]{2,1,0:T(8,128)S(1)} fusion(f32[32,64,1024]{2,1,0:T(8,128)} %fusion.63, f32[]{:T(128)} %bitcast.60, f32[]{:T(128)} %bitcast.59, f32[]{:T(128)} %bitcast.58, f32[]{:T(128)} %bitcast.57, f32[]{:T(128)} %bitcast.56, f32[]{:T(128)} %bitcast.55, f32[]{:T(128)} %bitcast.54, f32[]{:T(128)} %bitcast.53, f32[]{:T(128)} %bitcast), kind=kLoop, calls=%fused_computation.47 | loop fusion | flops 35651584 | bytes 16777252 | tf_op jit(solution)/shard_map/add | solution.py:47
  648.6 3.4 copy-done
  652.2 3.1 collective-permute-start
  657.4 9.6 %collective-permute-done = f32[4,64,1024]{2,1,0:T(8,128)S(1)} collective-permute-done((f32[4,64,1024]{2,1,0:T(8,128)S(1)}, f32[4,64,1024]{2,1,0:T(8,128)S(1)}, u32[]{:S(2)}, u32[]{:S(2)}) %collective-permute-start) | collective-permute-done | bytes 1048608 | tf_op jit(solution)/shard_map/ppermute | solution.py:12
  666.9 4.4 collective-permute-done.1
  671.3 34.2 %fusion.41 = f32[32,64,1024]{2,1,0:T(8,128)} fusion(f32[32,64,1024]{2,1,0:T(8,128)} %copy-done, f32[4,64,1024]{2,1,0:T(8,128)S(1)} %collective-permute-done.1, f32[4,64,1024]{2,1,0:T(8,128)S(1)} %collective-permute-done, f32[]{:T(128)} %bitcast.60, f32[]{:T(128)} %bitcast.59, f32[]{:T(128)} %bitcast.58, f32[]{:T(128)} %bitcast.57, f32[]{:T(128)} %bitcast.56, ...), kind=kLoop, calls=%fused_computation.78 | loop fusion | flops 52428800 | bytes 18874404 | tf_op jit(solution)/shard_map/add | solution.py:47
  709.9 10.3 %collective-permute-done.2 = f32[32,4,1024]{2,1,0:T(4,128)S(1)} collective-permute-done((f32[32,4,1024]{2,1,0:T(4,128)S(1)}, f32[32,4,1024]{2,1,0:T(4,128)S(1)}, u32[]{:S(2)}, u32[]{:S(2)}) %collective-permute-start.2) | collective-permute-done | bytes 524320 | tf_op jit(solution)/shard_map/ppermute | solution.py:12
  720.2 43.7 %fusion.21 = f32[32,64,1024]{2,1,0:T(8,128)} fusion(f32[32,64,1024]{2,1,0:T(8,128)} %fusion.41, f32[32,4,1024]{2,1,0:T(4,128)S(1)} %collective-permute-done.3, f32[32,4,1024]{2,1,0:T(4,128)S(1)} %collective-permute-done.2, f32[]{:T(128)} %bitcast.60, f32[]{:T(128)} %bitcast.59, f32[]{:T(128)} %bitcast.58, f32[]{:T(128)} %bitcast.57, f32[]{:T(128)} %bitcast.56, ...), kind=kLoop, calls=%fused_computation.58 | loop fusion | flops 52428800 | bytes 17825828 | tf_op jit(solution)/shard_map/add | solution.py:47
  (41 shorter events, 16.5 us)
Async XLA Ops:
  4.5 21.1 %all-to-all-start = ((s32[32,1,64]{2,1,0:T(1,128)}), s32[32,1,64]{2,1,0:T(1,128)S(1)}, u32[]{:S(2)}, u32[]{:S(2)}) async-start(s32[32,1,64]{2,1,0:T(1,128)} %bitcast.5), calls=%async_computation | async-start | bytes 32768 | tf_op jit(solution)/shard_map/all_to_all | solution.py:81
  54.1 6.5 copy-start.2
  54.1 195.0 %all-to-all-start.1 = ((bf16[32,64,2048]{2,1,0:T(8,128)(2,1)}), bf16[32,64,2048]{2,1,0:T(8,128)(2,1)}, u32[]{:S(2)}, u32[]{:S(2)}) async-start(bf16[32,64,2048]{2,1,0:T(8,128)(2,1)} %broadcast_select_fusion), calls=%async_computation.1 | async-start | bytes 16777216 | tf_op jit(solution)/shard_map/all_to_all | solution.py:54
  60.5 198.4 %copy-start.3 = (bf16[128,2048]{1,0:T(8,128)(2,1)S(1)}, bf16[128,2048]{1,0:T(8,128)(2,1)}, u32[]{:S(2)}) copy-start(bf16[128,2048]{1,0:T(8,128)(2,1)} %param.9) | copy-start | bytes 1572868
  288.1 55.4 %copy-start.1 = (f32[128,2048]{1,0:T(8,128)}, f32[128,2048]{1,0:T(8,128)S(1)}, u32[]{:S(2)}) copy-start(f32[128,2048]{1,0:T(8,128)S(1)} %convert_subtract_fusion) | copy-start | bytes 3145732
  343.6 4.8 copy-start.4
  343.6 193.7 %all-to-all-start.2 = ((bf16[32,64,2048]{2,1,0:T(8,128)(2,1)}), bf16[32,64,2048]{2,1,0:T(8,128)(2,1)}, u32[]{:S(2)}, u32[]{:S(2)}) async-start(bf16[32,64,2048]{2,1,0:T(8,128)(2,1)} %bitcast.80), calls=%async_computation.2 | async-start | bytes 16777216 | tf_op jit(solution)/shard_map/all_to_all | solution.py:54
  648.6 3.4 copy-start
  652.2 14.8 %collective-permute-start = (f32[4,64,1024]{2,1,0:T(8,128)S(1)}, f32[4,64,1024]{2,1,0:T(8,128)S(1)}, u32[]{:S(2)}, u32[]{:S(2)}) collective-permute-start(f32[4,64,1024]{2,1,0:T(8,128)S(1)} %get-tuple-element.4), channel_id=1, source_target_pairs={{0,8},{8,16},{16,24},{1,9},{9,17},{17,25},{2,10},{10,18},{18,26},{... | collective-permute-start | bytes 3145736 | tf_op jit(solution)/shard_map/ppermute | solution.py:12
  655.2 16.1 %collective-permute-start.1 = (f32[4,64,1024]{2,1,0:T(8,128)S(1)}, f32[4,64,1024]{2,1,0:T(8,128)S(1)}, u32[]{:S(2)}, u32[]{:S(2)}) collective-permute-start(f32[4,64,1024]{2,1,0:T(8,128)S(1)} %get-tuple-element.5), channel_id=1, source_target_pairs={{8,0},{16,8},{24,16},{9,1},{17,9},{25,17},{10,2},{18,10},{26,18},{... | collective-permute-start | bytes 3145736 | tf_op jit(solution)/shard_map/ppermute | solution.py:15
  707.3 12.9 %collective-permute-start.2 = (f32[32,4,1024]{2,1,0:T(4,128)S(1)}, f32[32,4,1024]{2,1,0:T(4,128)S(1)}, u32[]{:S(2)}, u32[]{:S(2)}) collective-permute-start(f32[32,4,1024]{2,1,0:T(4,128)S(1)} %get-tuple-element.2), channel_id=1, source_target_pairs={{0,1},{1,2},{2,3},{3,4},{4,5},{5,6},{6,7},{8,9},{9,10},{10,11},{11... | collective-permute-start | bytes 1572872 | tf_op jit(solution)/shard_map/ppermute | solution.py:12
  708.6 11.6 %collective-permute-start.3 = (f32[32,4,1024]{2,1,0:T(4,128)S(1)}, f32[32,4,1024]{2,1,0:T(4,128)S(1)}, u32[]{:S(2)}, u32[]{:S(2)}) collective-permute-start(f32[32,4,1024]{2,1,0:T(4,128)S(1)} %get-tuple-element.3), channel_id=1, source_target_pairs={{1,0},{2,1},{3,2},{4,3},{5,4},{6,5},{7,6},{9,8},{10,9},{11,10},{12... | collective-permute-start | bytes 1572872 | tf_op jit(solution)/shard_map/ppermute | solution.py:15
where the time goes:
time: 772 us; the launch traced here: 764 us
  waiting for transfers between devices  398 us (52%)
  other arithmetic  228 us (30%)
  local copies, waits for them, and re-layouts  64.8 us (8%)
  matrix products  45.5 us (6%)
  starting transfers between devices  26.1 us (3%)
    all_to_all x2, waiting for transfers between devices, traverse(): lax.all_to_all(blocks, ('inline', 'xline'), split_axis=0, concat_axis=0,...  374 us
    add x3, other arithmetic, filter_padded(): result + taps[offset] * lax.slice_in_dim(padded, offset, offset + length,...  123 us
    scatter-add x1, other arithmetic, local(): jax.ops.segment_sum(arrived.astype(jnp.float32), cell_recv, num_segments=...  34.5 us
    dot_general x1, matrix products, local(): jnp.dot(gathered, weight_matrix.astype(jnp.float32), precision=lax.Precis...  31.5 us
    sub x1, other arithmetic, local(): residual = modeled - observed.astype(jnp.float32)  29.3 us
    broadcast_in_dim x1, other arithmetic, local(): jnp.broadcast_to(adjoint.reshape(block_count, 1, per_block, samples), (bl...  29.2 us
    gather x1, local copies, waits for them, and re-layouts, local(): predicted = jnp.take(tile_table.astype(jnp.bfloat16), cell_recv, axis=0)  20.8 us
    ppermute x2, waiting for transfers between devices, extended(): lax.ppermute(lax.slice_in_dim(block, block.shape[dim] - width, None, axis...  19.8 us
  transfers between devices with their start and end apart: 7, of which 5 were waited for; matrix products, arithmetic and copies ran while one was open for 2% of the time, Pallas kernels for 0%

commit v1 on v0

--- a/solution.py
+++ b/solution.py
@@ -2,6 +2,9 @@
 import jax.numpy as jnp
 from jax import lax
 from jax.sharding import PartitionSpec as P
+
+CHUNK = 128
+HALO = 64
 
 
 def extended(block, sides, width):
@@ -17,25 +20,31 @@
     return block
 
 
-def convolve(signal, wavelet):
-    pad_width = wavelet.shape[0] // 2
-    padded = jnp.pad(signal, ((0, 0), (pad_width, pad_width)))
-    length = signal.shape[1]
-    result = jnp.zeros_like(signal)
-    for offset in range(wavelet.shape[0]):
-        start = 2 * pad_width - offset
-        result = result + wavelet[offset] * padded[:, start : start + length]
-    return result
+def toeplitz_block(wavelet, sign):
+    half = wavelet.shape[0] // 2
+    k = jnp.arange(CHUNK + 2 * HALO)[:, None]
+    n = jnp.arange(CHUNK)[None, :]
+    if sign > 0:
+        tap = n - k + HALO + half
+    else:
+        tap = k - n - HALO + half
+    block = jnp.zeros((CHUNK + 2 * HALO, CHUNK), jnp.float32)
+    for j in range(wavelet.shape[0]):
+        block = jnp.where(tap == j, wavelet[j], block)
+    return block
 
 
-def correlate(signal, wavelet):
-    pad_width = wavelet.shape[0] // 2
-    padded = jnp.pad(signal, ((0, 0), (pad_width, pad_width)))
-    length = signal.shape[1]
-    result = jnp.zeros_like(signal)
-    for offset in range(wavelet.shape[0]):
-        result = result + wavelet[offset] * padded[:, offset : offset + length]
-    return result
+def banded(signal, block):
+    rows, length = signal.shape
+    chunks = length // CHUNK
+    padded = jnp.pad(signal, ((0, 0), (HALO, HALO)))
+    pieces = padded.reshape(rows, chunks + 1, CHUNK)
+    windows = jnp.concatenate([pieces[:, :chunks], pieces[:, 1:]], axis=-1)
+    out = jnp.einsum(
+        "tok,kn->ton", windows, block, precision=lax.Precision.HIGHEST,
+        preferred_element_type=jnp.float32,
+    )
+    return out.reshape(rows, length)
 
 
 def filter_padded(padded, taps, axis):
@@ -55,7 +64,9 @@
 
 
 def local(image, weights, observed, wavelet, taps, aperture, landing):
+    axes = ("inline", "xline")
     device_count = lax.axis_size("inline") * lax.axis_size("xline")
+    me = lax.axis_index("inline") * lax.axis_size("xline") + lax.axis_index("xline")
     block_count, aperture_len = aperture.shape
     trace_count, samples = observed.shape
     per_block = trace_count // block_count
@@ -80,7 +91,7 @@
     )
     cell_recv = lax.all_to_all(
         cell_send.reshape(device_count, capacity * per_block),
-        ("inline", "xline"),
+        axes,
         split_axis=0,
         concat_axis=0,
         tiled=True,
@@ -99,24 +110,42 @@
         block_count, aperture_len, per_block, samples
     )
     synthetic = jnp.sum(own_preds.astype(jnp.float32), axis=1).reshape(trace_count, samples)
-    modeled = convolve(synthetic, wavelet)
+    modeled = banded(synthetic, toeplitz_block(wavelet, 1))
     residual = modeled - observed.astype(jnp.float32)
-    adjoint = correlate(residual, wavelet).astype(jnp.bfloat16)
-    adjoint_items = jnp.broadcast_to(
-        adjoint.reshape(block_count, 1, per_block, samples),
-        (block_count, aperture_len, per_block, samples),
+    adjoint = banded(residual, toeplitz_block(wavelet, -1)).astype(jnp.bfloat16)
+
+    adjoint_all = lax.all_gather(adjoint, axes, axis=0, tiled=True)
+    aperture_all = lax.all_gather(aperture, axes, axis=0, tiled=True)
+    landing_all = lax.all_gather(landing, axes, axis=0, tiled=True)
+    all_blocks = aperture_all.shape[0]
+    relevant = capacity * device_count
+    hit = aperture_all == me
+    has = jnp.any(hit, axis=1)
+    entry = jnp.argmax(hit, axis=1).astype(jnp.int32)
+    position = jnp.cumsum(has.astype(jnp.int32)) - 1
+    slot = jnp.where(has, position, relevant)
+    chosen = (
+        jnp.zeros((relevant,), jnp.int32)
+        .at[slot]
+        .set(jnp.arange(all_blocks, dtype=jnp.int32), mode="drop")
     )
-    adjoint_items = adjoint_items.reshape(item_count, per_block, samples)
-    outbound = (
-        jnp.zeros((device_count * capacity, per_block, samples), jnp.bfloat16)
-        .at[target_slot]
-        .set(adjoint_items)
+    found = jnp.sum(has.astype(jnp.int32))
+    cells_all = jnp.take_along_axis(
+        landing_all.reshape(all_blocks, per_block, aperture_len), entry[:, None, None], axis=2
+    )[:, :, 0]
+    cells = jnp.where(
+        (jnp.arange(relevant) < found)[:, None], jnp.take(cells_all, chosen, axis=0), cell_count
     )
-    arrived = traverse(outbound.reshape(device_count, capacity * per_block, samples))
-    arrived = arrived.reshape(device_count * capacity * per_block, samples)
-    gathered = jax.ops.segment_sum(arrived.astype(jnp.float32), cell_recv, num_segments=cell_count)
-    raw_gradient = jnp.dot(
-        gathered, weight_matrix.astype(jnp.float32), precision=lax.Precision.HIGHEST
+    picked = jnp.take(adjoint_all.reshape(all_blocks, per_block, samples), chosen, axis=0)
+    per_trace = jnp.dot(
+        picked.reshape(relevant * per_block, samples),
+        weight_matrix,
+        preferred_element_type=jnp.float32,
+    )
+    raw_gradient = (
+        jnp.zeros((cell_count, depth_len), jnp.float32)
+        .at[cells.reshape(relevant * per_block)]
+        .add(per_trace, mode="drop")
     )
     raw_gradient = raw_gradient.reshape(rows_x, rows_y, depth_len)
     depth_padded = jnp.pad(raw_gradient, ((0, 0), (0, 0), (4, 4)))

time: 772 us -> 707 us (0.916)
  waiting for transfers between devices: 398 us -> 205 us
  blocking collectives: 0 us -> 125 us
  other arithmetic: 228 us -> 163 us
  matrix products: 45.5 us -> 76.1 us
  local copies, waits for them, and re-layouts: 64.8 us -> 81.3 us
  between operations: 1.11 us -> 14.6 us
    all_to_all x2 -> x1, waiting for transfers between devices: 374 us -> 186 us  [traverse(): lax.all_to_all(blocks, ('inline', 'xline'), split_axis=0, concat_axis=0,...]
    all_gather x0 -> x2, blocking collectives: none -> 125 us  [the longest x1 67.2 us: local(): landing_all = lax.all_gather(landing, axes, axis=0, tiled=True)]
    dot_general x1 -> x3, matrix products: 31.5 us -> 62.1 us  [the longest x2 47.3 us: banded(): jnp.einsum('tok,kn->ton', windows, block, precision=lax.Precision.HIGHEST...]
    broadcast_in_dim x1 -> x0, other arithmetic: 29.2 us -> none  [local(): jnp.broadcast_to(adjoint.reshape(block_count, 1, per_block, samples), (bl...]
    sub x1, other arithmetic: 29.3 us -> 1.24 us  [local(): residual = modeled - observed.astype(jnp.float32)]
    gather x0 -> x3, local copies, waits for them, and re-layouts: none -> 20.8 us  [the longest x1 14.5 us: local(): jnp.take(adjoint_all.reshape(all_blocks, per_block, samples), chosen, axi...]
    scatter x1, local copies, waits for them, and re-layouts: 19.3 us -> 2.65 us  [local(): chosen = jnp.zeros((relevant,), jnp.int32).at[slot].set(jnp.arange(all_bl...]
    ppermute x2, waiting for transfers between devices: 19.8 us -> 6.81 us  [extended(): lax.ppermute(lax.slice_in_dim(block, block.shape[dim] - width, None, axis...]
  transfers between devices with their start and end apart: 7 -> 7, of which waited for: 5 -> 5; matrix products, arithmetic and copies ran while one was open for 2% -> 5% of each run, Pallas kernels for 0% -> 0%
where the time goes in v1:
time: 707 us; the launch traced here: 699 us
  waiting for transfers between devices  205 us (29%)
  other arithmetic  163 us (23%)
  blocking collectives  125 us (18%)
  local copies, waits for them, and re-layouts  81.3 us (11%)
  matrix products  76.1 us (11%)
  starting transfers between devices  33.2 us (5%)
  between operations  14.6 us (2%)
    all_to_all x1, waiting for transfers between devices, traverse(): lax.all_to_all(blocks, ('inline', 'xline'), split_axis=0, concat_axis=0,...  186 us
    add x3, other arithmetic, filter_padded(): result + taps[offset] * lax.slice_in_dim(padded, offset, offset + length,...  124 us
    all_gather x1, blocking collectives, local(): landing_all = lax.all_gather(landing, axes, axis=0, tiled=True)  67.2 us
    all_gather x1, blocking collectives, local(): aperture_all = lax.all_gather(aperture, axes, axis=0, tiled=True)  57.7 us
    dot_general x2, matrix products, banded(): jnp.einsum('tok,kn->ton', windows, block, precision=lax.Precision.HIGHEST...  47.3 us
    scatter-add x1, other arithmetic, local(): raw_gradient = jnp.zeros((cell_count, depth_len), jnp.float32).at[cells.r...  23.1 us
    gather x1, local copies, waits for them, and re-layouts, local(): predicted = jnp.take(tile_table.astype(jnp.bfloat16), cell_recv, axis=0)  20.8 us
    dot_general x1, matrix products, local(): jnp.dot(picked.reshape(relevant * per_block, samples), weight_matrix, pre...  14.8 us
  transfers between devices with their start and end apart: 7, of which 5 were waited for; matrix products, arithmetic and copies ran while one was open for 5% of the time, Pallas kernels for 0%

profile of v1, /device:TPU:1, one launch (start us, length us, event | category | flops | bytes accessed | tf_op | source)
XLA Modules:
  0.0 699.1 jit_solution(16067734472219478815)
XLA Ops:
  11.0 7.1 %all-to-all-start = ((s32[32,1,64]{2,1,0:T(1,128)}), s32[32,1,64]{2,1,0:T(1,128)S(1)}, u32[]{:S(2)}, u32[]{:S(2)}) async-start(s32[32,1,64]{2,1,0:T(1,128)} %bitcast.12), calls=%async_computation | async-start | bytes 32768 | tf_op jit(solution)/shard_map/all_to_all | solution.py:92
  18.1 14.0 %convolution_convert_fusion = bf16[2048,2048]{1,0:T(8,128)(2,1)} fusion(bf16[2048,1024]{1,0:T(8,128)(2,1)} %bitcast.113, bf16[1,1,2048,1024]{3,2,1,0:T(8,128)(2,1)} %param.8), kind=kOutput, calls=%fused_computation.110 | convolution fusion | flops 8594128896 | bytes 16777216 | tf_op jit(solution)/shard_map/dot_general | solution.py:103
  33.4 20.8 %gather_fusion.1 = bf16[2048,2048]{1,0:T(8,128)(2,1)} fusion(bf16[2048,2048]{1,0:T(8,128)(2,1)} %convolution_convert_fusion, s32[2048]{0:T(1024)S(1)} %broadcast_clamp_fusion), kind=kCustom, calls=%fused_computation.1 | custom fusion | bytes 16785408 | tf_op jit(solution)/shard_map/jit(_take)/gather | solution.py:106
  54.2 7.6 %broadcast_select_fusion = bf16[32,64,2048]{2,1,0:T(8,128)(2,1)} fusion(bf16[32,64,2048]{2,1,0:T(8,128)(2,1)} %bitcast.98, pred[32,64]{1,0:T(8,128)(4,1)S(1)} %compare_and_fusion), kind=kLoop, calls=%fused_computation.109 | loop fusion | flops 4194304 | bytes 16779264 | tf_op jit(solution)/shard_map/jit(_take)/select_n | solution.py:106
  61.8 5.9 all-to-all-start.1
  70.5 186.4 %all-to-all-done.1 = bf16[32,64,2048]{2,1,0:T(8,128)(2,1)} async-done(((bf16[32,64,2048]{2,1,0:T(8,128)(2,1)}), bf16[32,64,2048]{2,1,0:T(8,128)(2,1)}, u32[]{:S(2)}, u32[]{:S(2)}) %all-to-all-start.1) | async-done | bytes 8388640 | tf_op jit(solution)/shard_map/all_to_all | solution.py:63
  256.9 6.2 gather_fusion.2
  263.1 3.5 convert_reduce_fusion
  267.9 22.9 %fusion.69 = f32[128,16,128]{0,2,1:T(8,128)S(1)} fusion(f32[128,16,128]{2,0,1:T(8,128)S(1)} %copy.76, f32[128,16,128]{2,0,1:T(8,128)S(1)} %copy.75, f32[]{:T(128)} %bitcast.54, f32[]{:T(128)} %bitcast.53, f32[]{:T(128)} %bitcast.52, f32[]{:T(128)} %bitcast.51, f32[]{:T(128)} %bitcast.50, f32[]{:T(128)} %bitcast.49, f32[]{:T(128)} %bitcast.48, ...), kind=kOutput, calls=%fused_computation.116 | convolution fusion | flops 808058880 | bytes 3145860 | tf_op jit(solution)/shard_map/tok,kn->ton/dot_general | solution.py:43
  297.2 24.4 %fusion.77 = bf16[128,16,128]{0,2,1:T(8,128)(2,1)S(1)} fusion(f32[128,16,128]{2,0,1:T(8,128)} %copy.78, f32[128,16,128]{2,0,1:T(8,128)} %copy.77, f32[]{:T(128)} %bitcast.54, f32[]{:T(128)} %bitcast.53, f32[]{:T(128)} %bitcast.52, f32[]{:T(128)} %bitcast.51, f32[]{:T(128)} %bitcast.50, f32[]{:T(128)} %bitcast.49, f32[]{:T(128)} %bitcast.48, f32[]{:T(128)} %bitcast.47, ...), kind=kOutput, calls=%fused_computation.124 | convolution fusion | flops 808321024 | bytes 2621572 | tf_op jit(solution)/shard_map/tok,kn->ton/dot_general | solution.py:43
  322.7 57.7 %all-gather = s32[32,16,8]{1,2,0:T(8,128)S(1)} all-gather(s32[1,16,8]{1,2,0:T(8,128)S(1)} %bitcast.108), channel_id=1, replica_groups=mesh['inline'=4,'xline'=8] {'inline','xline'}, dimensions={0}, use_global_device_ids=true | all-gather | bytes 16896 | tf_op jit(solution)/shard_map/all_gather | solution.py:118
  380.6 67.2 %all_gather.10 = s32[4096,8]{0,1:T(8,128)S(1)} all-gather(s32[128,8]{0,1:T(8,128)S(1)} %copy-done.5), channel_id=1, replica_groups=mesh['inline'=4,'xline'=8] {'inline','xline'}, dimensions={0}, use_global_device_ids=true | all-gather | bytes 135168 | tf_op jit(solution)/shard_map/all_gather | solution.py:119
  450.2 4.2 copy.55
  455.6 5.6 gather_fusion.4
  467.4 14.5 %gather_fusion.3 = bf16[256,8,2048]{2,1,0:T(8,128)(2,1)} fusion(bf16[512,8,2048]{2,1,0:T(8,128)(2,1)} %bitcast.103, s32[1024]{0:T(1024)S(1)} %pad_clamp_fusion.1), kind=kCustom, calls=%fused_computation.3 | custom fusion | bytes 16778240 | tf_op jit(solution)/shard_map/jit(_take)/gather | solution.py:139
  481.8 14.8 %fusion.60 = f32[2048,1024]{1,0:T(8,128)} fusion(bf16[256,8,2048]{2,1,0:T(8,128)(2,1)} %gather_fusion.3, pred[256]{0:T(512)(128)(4,1)S(1)} %compare_and_fusion.3, bf16[1,1,2048,1024]{3,2,1,0:T(8,128)(2,1)} %param.8), kind=kOutput, calls=%fused_computation.104 | convolution fusion | flops 8594128896 | bytes 20971776 | tf_op jit(solution)/shard_map/dot_general | solution.py:140
  496.6 23.1 %scatter_custom_fusion.2 = f32[2048,1024]{1,0:T(8,128)} fusion(s32[2048]{0:T(1024)S(1)} %bitcast.110, f32[2048,1024]{1,0:T(8,128)} %fusion.60, f32[]{:T(128)} %constant.48.clone.1), kind=kCustom, calls=%fused_computation.114 | custom fusion | flops 2097152 | bytes 8389120 | tf_op jit(solution)/shard_map/scatter-add | solution.py:148
  519.7 45.4 %fusion.8 = f32[32,64,1024]{2,1,0:T(8,128)S(1)} fusion(f32[32,64,1024]{2,1,0:T(8,128)} %bitcast.99, f32[]{:T(128)} %bitcast.70, f32[]{:T(128)} %bitcast.69, f32[]{:T(128)} %bitcast.68, f32[]{:T(128)} %bitcast.67, f32[]{:T(128)} %bitcast.66, f32[]{:T(128)} %bitcast.65, f32[]{:T(128)} %bitcast.64, f32[]{:T(128)} %bitcast.63, f32[]{:T(128)} %bitcast), kind=kLoop, calls=%fused_computation.48 | loop fusion | flops 35651584 | bytes 16777252 | tf_op jit(solution)/shard_map/add | solution.py:56
  568.7 11.2 %collective-permute-start.1 = (f32[4,64,1024]{2,1,0:T(8,128)S(1)}, f32[4,64,1024]{2,1,0:T(8,128)S(1)}, u32[]{:S(2)}, u32[]{:S(2)}) collective-permute-start(f32[4,64,1024]{2,1,0:T(8,128)S(1)} %get-tuple-element.17), channel_id=1, source_target_pairs={{8,0},{16,8},{24,16},{9,1},{17,9},{25,17},{10,2},{18,10},{26,18},{... | collective-permute-start | bytes 3145736 | tf_op jit(solution)/shard_map/ppermute | solution.py:18
  582.2 10.5 %collective-permute-done.1 = f32[4,64,1024]{2,1,0:T(8,128)S(1)} collective-permute-done((f32[4,64,1024]{2,1,0:T(8,128)S(1)}, f32[4,64,1024]{2,1,0:T(8,128)S(1)}, u32[]{:S(2)}, u32[]{:S(2)}) %collective-permute-start.1) | collective-permute-done | bytes 1048608 | tf_op jit(solution)/shard_map/ppermute | solution.py:18
  593.9 35.2 %fusion.39 = f32[32,64,1024]{2,1,0:T(8,128)} fusion(f32[32,64,1024]{2,1,0:T(8,128)} %copy-done, f32[4,64,1024]{2,1,0:T(8,128)S(1)} %collective-permute-done.1, f32[4,64,1024]{2,1,0:T(8,128)} %collective-permute-done, f32[]{:T(128)} %bitcast.70, f32[]{:T(128)} %bitcast.69, f32[]{:T(128)} %bitcast.68, f32[]{:T(128)} %bitcast.67, f32[]{:T(128)} %bitcast.66, ...), kind=kLoop, calls=%fused_computation.79 | loop fusion | flops 52428800 | bytes 18874404 | tf_op jit(solution)/shard_map/add | solution.py:56
  632.8 5.3 collective-permute-start.2
  641.5 5.6 collective-permute-done.2
  648.5 43.6 %fusion.19 = f32[32,64,1024]{2,1,0:T(8,128)} fusion(f32[32,64,1024]{2,1,0:T(8,128)} %fusion.39, f32[32,4,1024]{2,1,0:T(4,128)S(1)} %copy.71, f32[32,4,1024]{2,1,0:T(4,128)S(1)} %copy.69, f32[]{:T(128)} %bitcast.70, f32[]{:T(128)} %bitcast.69, f32[]{:T(128)} %bitcast.68, f32[]{:T(128)} %bitcast.67, f32[]{:T(128)} %bitcast.66, f32[]{:T(128)} %bitcast.65, ...), kind=kLoop, calls=%fused_computation.59 | loop fusion | flops 52428800 | bytes 17825828 | tf_op jit(solution)/shard_map/add | solution.py:56
  (93 shorter events, 41.9 us)
Async XLA Ops:
  11.0 21.1 %all-to-all-start = ((s32[32,1,64]{2,1,0:T(1,128)}), s32[32,1,64]{2,1,0:T(1,128)S(1)}, u32[]{:S(2)}, u32[]{:S(2)}) async-start(s32[32,1,64]{2,1,0:T(1,128)} %bitcast.12), calls=%async_computation | async-start | bytes 32768 | tf_op jit(solution)/shard_map/all_to_all | solution.py:92
  61.8 6.2 copy-start.2
  61.8 7.2 %copy-start.1 = (f32[33]{0:T(128)S(1)}, f32[33]{0:T(128)}, u32[]{:S(2)}) copy-start(f32[33]{0:T(128)} %param.10) | copy-start | bytes 400
  61.8 195.0 %all-to-all-start.1 = ((bf16[32,64,2048]{2,1,0:T(8,128)(2,1)}), bf16[32,64,2048]{2,1,0:T(8,128)(2,1)}, u32[]{:S(2)}, u32[]{:S(2)}) async-start(bf16[32,64,2048]{2,1,0:T(8,128)(2,1)} %broadcast_select_fusion), calls=%async_computation.1 | async-start | bytes 16777216 | tf_op jit(solution)/shard_map/all_to_all | solution.py:63
  67.7 399.6 %all-gather.3.cloned.1.call-start = ((), (), s32[]{:S(2)}) async-start(), calls=%async_computation.2 | async-start | bytes 17301504 | tf_op jit(solution)/shard_map/all_gather | solution.py:117
  292.0 30.6 %copy-start.4 = (s32[16,8]{0,1:T(8,128)S(1)}, s32[16,8]{0,1:T(8,128)}, u32[]{:S(2)}) copy-start(s32[16,8]{0,1:T(8,128)} %param.12) | copy-start | bytes 1540
  292.0 88.5 %copy-start.5 = (s32[128,8]{0,1:T(8,128)S(1)}, s32[128,8]{0,1:T(8,128)}, u32[]{:S(2)}) copy-start(s32[128,8]{0,1:T(8,128)} %param.13) | copy-start | bytes 12292
  297.2 169.4 %copy-start.3 = (f32[9]{0:T(128)S(1)}, f32[9]{0:T(128)}, u32[]{:S(2)}) copy-start(f32[9]{0:T(128)} %param.11) | copy-start | bytes 112
  565.2 3.4 copy-start
  568.7 24.0 %collective-permute-start.1 = (f32[4,64,1024]{2,1,0:T(8,128)S(1)}, f32[4,64,1024]{2,1,0:T(8,128)S(1)}, u32[]{:S(2)}, u32[]{:S(2)}) collective-permute-start(f32[4,64,1024]{2,1,0:T(8,128)S(1)} %get-tuple-element.17), channel_id=1, source_target_pairs={{8,0},{16,8},{24,16},{9,1},{17,9},{25,17},{10,2},{18,10},{26,18},{... | collective-permute-start | bytes 3145736 | tf_op jit(solution)/shard_map/ppermute | solution.py:18
  579.9 14.0 %collective-permute-start = (f32[4,64,1024]{2,1,0:T(8,128)S(1)}, f32[4,64,1024]{2,1,0:T(8,128)}, u32[]{:S(2)}, u32[]{:S(2)}) collective-permute-start(f32[4,64,1024]{2,1,0:T(8,128)S(1)} %get-tuple-element.16), channel_id=1, source_target_pairs={{0,8},{8,16},{16,24},{1,9},{9,17},{17,25},{2,10},{10,18},{18,26},{... | collective-permute-start | bytes 3145736 | tf_op jit(solution)/shard_map/ppermute | solution.py:15
  631.2 9.9 %collective-permute-start.3 = (f32[32,4,1024]{2,0,1:T(8,128)S(1)}, f32[32,4,1024]{2,0,1:T(8,128)S(1)}, u32[]{:S(2)}, u32[]{:S(2)}) collective-permute-start(f32[32,4,1024]{2,0,1:T(8,128)S(1)} %copy.70), channel_id=1, source_target_pairs={{1,0},{2,1},{3,2},{4,3},{5,4},{6,5},{7,6},{9,8},{10,9},{11,10},{12... | collective-permute-start | bytes 1572872 | tf_op jit(solution)/shard_map/ppermute | solution.py:18
  632.8 14.3 %collective-permute-start.2 = (f32[32,4,1024]{2,0,1:T(8,128)S(1)}, f32[32,4,1024]{2,0,1:T(8,128)}, u32[]{:S(2)}, u32[]{:S(2)}) collective-permute-start(f32[32,4,1024]{2,0,1:T(8,128)S(1)} %copy.68), channel_id=1, source_target_pairs={{0,1},{1,2},{2,3},{3,4},{4,5},{5,6},{6,7},{8,9},{9,10},{10,11},{11... | collective-permute-start | bytes 1572872 | tf_op jit(solution)/shard_map/ppermute | solution.py:15
Sparse Core Ops, SparseCore 0:
  322.8 113.5 all-gather.2

commit v2 on v1

--- a/solution.py
+++ b/solution.py
@@ -20,29 +20,39 @@
     return block
 
 
-def toeplitz_block(wavelet, sign):
-    half = wavelet.shape[0] // 2
+def band_block(values, centre):
     k = jnp.arange(CHUNK + 2 * HALO)[:, None]
     n = jnp.arange(CHUNK)[None, :]
-    if sign > 0:
-        tap = n - k + HALO + half
-    else:
-        tap = k - n - HALO + half
+    tap = k - n - HALO + centre
     block = jnp.zeros((CHUNK + 2 * HALO, CHUNK), jnp.float32)
-    for j in range(wavelet.shape[0]):
-        block = jnp.where(tap == j, wavelet[j], block)
+    for j in range(values.shape[0]):
+        block = jnp.where(tap == j, values[j], block)
     return block
+
+
+def split(x):
+    high = lax.reduce_precision(x, exponent_bits=8, mantissa_bits=7)
+    return high.astype(jnp.bfloat16), (x - high).astype(jnp.bfloat16)
+
+
+def windows(x):
+    rows, length = x.shape
+    chunks = length // CHUNK
+    padded = jnp.pad(x, ((0, 0), (HALO, HALO)))
+    pieces = padded.reshape(rows, chunks + 1, CHUNK)
+    joined = jnp.concatenate([pieces[:, :chunks], pieces[:, 1:]], axis=-1)
+    return joined.reshape(rows * chunks, CHUNK + 2 * HALO)
 
 
 def banded(signal, block):
     rows, length = signal.shape
-    chunks = length // CHUNK
-    padded = jnp.pad(signal, ((0, 0), (HALO, HALO)))
-    pieces = padded.reshape(rows, chunks + 1, CHUNK)
-    windows = jnp.concatenate([pieces[:, :chunks], pieces[:, 1:]], axis=-1)
-    out = jnp.einsum(
-        "tok,kn->ton", windows, block, precision=lax.Precision.HIGHEST,
-        preferred_element_type=jnp.float32,
+    x_high, x_low = split(signal)
+    b_high, b_low = split(block)
+    w_high, w_low = windows(x_high), windows(x_low)
+    out = (
+        jnp.dot(w_high, b_high, preferred_element_type=jnp.float32)
+        + jnp.dot(w_high, b_low, preferred_element_type=jnp.float32)
+        + jnp.dot(w_low, b_high, preferred_element_type=jnp.float32)
     )
     return out.reshape(rows, length)
 
@@ -74,6 +84,10 @@
     cell_count = rows_x * rows_y
     capacity = 2 * max(1, block_count * aperture_len // device_count)
     item_count = block_count * aperture_len
+    tables = jnp.concatenate(
+        [aperture, landing.reshape(block_count, per_block * aperture_len)], axis=1
+    ).astype(jnp.float32)
+    tables_all = jnp.round(lax.all_gather(tables, axes, axis=0, tiled=True))
     target_tile = aperture.reshape(item_count)
     onehot = (target_tile[:, None] == jnp.arange(device_count, dtype=jnp.int32)[None, :]).astype(
         jnp.int32
@@ -110,14 +124,15 @@
         block_count, aperture_len, per_block, samples
     )
     synthetic = jnp.sum(own_preds.astype(jnp.float32), axis=1).reshape(trace_count, samples)
-    modeled = banded(synthetic, toeplitz_block(wavelet, 1))
+    half = wavelet.shape[0] // 2
+    modeled = banded(synthetic, band_block(wavelet[::-1], half))
     residual = modeled - observed.astype(jnp.float32)
-    adjoint = banded(residual, toeplitz_block(wavelet, -1)).astype(jnp.bfloat16)
+    adjoint = banded(residual, band_block(wavelet, half)).astype(jnp.bfloat16)
 
     adjoint_all = lax.all_gather(adjoint, axes, axis=0, tiled=True)
-    aperture_all = lax.all_gather(aperture, axes, axis=0, tiled=True)
-    landing_all = lax.all_gather(landing, axes, axis=0, tiled=True)
-    all_blocks = aperture_all.shape[0]
+    all_blocks = block_count * device_count
+    aperture_all = tables_all[:, :aperture_len].astype(jnp.int32)
+    landing_all = tables_all[:, aperture_len:].astype(jnp.int32).reshape(all_blocks * per_block, aperture_len)
     relevant = capacity * device_count
     hit = aperture_all == me
     has = jnp.any(hit, axis=1)
@@ -147,9 +162,8 @@
         .at[cells.reshape(relevant * per_block)]
         .add(per_trace, mode="drop")
     )
-    raw_gradient = raw_gradient.reshape(rows_x, rows_y, depth_len)
-    depth_padded = jnp.pad(raw_gradient, ((0, 0), (0, 0), (4, 4)))
-    smooth_z = filter_padded(depth_padded, taps, 2)
+    smooth_z = banded(raw_gradient, band_block(taps, taps.shape[0] // 2))
+    smooth_z = smooth_z.reshape(rows_x, rows_y, depth_len)
     inline_wide = extended(smooth_z, (("inline", 0),), 4)
     smooth_x = filter_padded(inline_wide, taps, 0)
     xline_wide = extended(smooth_x, (("xline", 1),), 4)

time: 707 us -> 856 us (1.21)
  matrix products: 76.1 us -> 189 us
  local copies, waits for them, and re-layouts: 81.3 us -> 162 us
  blocking collectives: 125 us -> 58.9 us
  waiting for transfers between devices: 205 us -> 250 us
  other arithmetic: 163 us -> 148 us
  starting transfers between devices: 33.2 us -> 22.4 us
    dot_general x2 -> x9, matrix products: 47.3 us -> 160 us  [the longest x3 54.9 us: banded(): jnp.dot(w_high, b_high, preferred_element_type=jnp.float32)]
    all_gather x2 -> x1, blocking collectives: 125 us -> 58.9 us  [local(): tables_all = jnp.round(lax.all_gather(tables, axes, axis=0, tiled=True))]
    all_gather x1, waiting for transfers between devices: 0.02 us -> 42.6 us  [local(): adjoint_all = lax.all_gather(adjoint, axes, axis=0, tiled=True)]
    add x3 -> x2, other arithmetic: 124 us -> 83.5 us  [filter_padded(): result + taps[offset] * lax.slice_in_dim(padded, offset, offset + length,...]
    unnamed x21 -> x23, local copies, waits for them, and re-layouts: 11.3 us -> 45.4 us
    concatenate x0 -> x7, local copies, waits for them, and re-layouts: none -> 33.2 us  [the longest x6 30.3 us: windows(): joined = jnp.concatenate([pieces[:, :chunks], pieces[:, 1:]], axis=-1)]
    concatenate x0 -> x6, other arithmetic: none -> 17.4 us  [windows(): joined = jnp.concatenate([pieces[:, :chunks], pieces[:, 1:]], axis=-1)]
    ppermute x2, waiting for transfers between devices: 6.81 us -> 20 us  [extended(): lax.ppermute(lax.slice_in_dim(block, block.shape[dim] - width, None, axis...]
  transfers between devices with their start and end apart: 7 -> 7, of which waited for: 5 -> 3; matrix products, arithmetic and copies ran while one was open for 5% -> 6% of each run, Pallas kernels for 0% -> 0%
where the time goes in v2:
time: 856 us; the launch traced here: 845 us
  waiting for transfers between devices  250 us (29%)
  matrix products  189 us (22%)
  local copies, waits for them, and re-layouts  162 us (19%)
  other arithmetic  148 us (17%)
  blocking collectives  58.9 us (7%)
  starting transfers between devices  22.4 us (3%)
  between operations  15.1 us (2%)
    all_to_all x1, waiting for transfers between devices, traverse(): lax.all_to_all(blocks, ('inline', 'xline'), split_axis=0, concat_axis=0,...  187 us
    add x2, other arithmetic, filter_padded(): result + taps[offset] * lax.slice_in_dim(padded, offset, offset + length,...  83.5 us
    all_gather x1, blocking collectives, local(): tables_all = jnp.round(lax.all_gather(tables, axes, axis=0, tiled=True))  58.9 us
    dot_general x3, matrix products, banded(): jnp.dot(w_high, b_high, preferred_element_type=jnp.float32)  54.9 us
    dot_general x3, matrix products, banded(): jnp.dot(w_low, b_high, preferred_element_type=jnp.float32)  54.5 us
    dot_general x3, matrix products, banded(): jnp.dot(w_high, b_low, preferred_element_type=jnp.float32)  51.1 us
    unnamed x23, local copies, waits for them, and re-layouts  45.4 us
    all_gather x1, waiting for transfers between devices, local(): adjoint_all = lax.all_gather(adjoint, axes, axis=0, tiled=True)  42.6 us
  transfers between devices with their start and end apart: 7, of which 3 were waited for; matrix products, arithmetic and copies ran while one was open for 6% of the time, Pallas kernels for 0%

profile of v2, /device:TPU:1, one launch (start us, length us, event | category | flops | bytes accessed | tf_op | source)
XLA Modules:
  0.0 844.5 jit_solution(14110742262349823207)
XLA Ops:
  18.1 14.0 %convolution_convert_fusion = bf16[2048,2048]{1,0:T(8,128)(2,1)} fusion(bf16[2048,1024]{1,0:T(8,128)(2,1)} %bitcast.134, bf16[1,1,2048,1024]{3,2,1,0:T(8,128)(2,1)} %param.8), kind=kOutput, calls=%fused_computation.83 | convolution fusion | flops 8594128896 | bytes 16777216 | tf_op jit(solution)/shard_map/dot_general | solution.py:117
  33.4 20.8 %gather_fusion.1 = bf16[2048,2048]{1,0:T(8,128)(2,1)} fusion(bf16[2048,2048]{1,0:T(8,128)(2,1)} %convolution_convert_fusion, s32[2048]{0:T(1024)S(1)} %broadcast_clamp_fusion), kind=kCustom, calls=%fused_computation.1 | custom fusion | bytes 16785408 | tf_op jit(solution)/shard_map/jit(_take)/gather | solution.py:120
  69.9 187.0 %all-to-all-done.1 = bf16[32,64,2048]{2,1,0:T(8,128)(2,1)} async-done(((bf16[32,64,2048]{2,1,0:T(8,128)(2,1)}), bf16[32,64,2048]{2,1,0:T(8,128)(2,1)}, u32[]{:S(2)}, u32[]{:S(2)}) %all-to-all-start.1) | async-done | bytes 8388640 | tf_op jit(solution)/shard_map/all_to_all | solution.py:73
  270.6 20.9 %fusion.106 = f32[2048,128]{1,0:T(8,128)S(1)} fusion(bf16[2048,256]{1,0:T(8,128)(2,1)S(1)} %bitcast.123, f32[]{:T(128)} %bitcast.56, f32[]{:T(128)} %bitcast.55, f32[]{:T(128)} %bitcast.54, f32[]{:T(128)} %bitcast.53, f32[]{:T(128)} %bitcast.52, f32[]{:T(128)} %bitcast.51, f32[]{:T(128)} %bitcast.50, f32[]{:T(128)} %bitcast.49, f32[]{:T(128)} %bitcast.48, ...), kind=kOutput, calls=%fused_computation.169 | convolution fusion | flops 136511488 | bytes 2097284 | tf_op jit(solution)/shard_map/dot_general | solution.py:53
  291.6 21.0 %convolution_add_fusion.5 = f32[2048,128]{1,0:T(8,128)S(1)} fusion(f32[2048,128]{1,0:T(8,128)S(1)} %fusion.106, bf16[2048,256]{1,0:T(8,128)(2,1)S(1)} %bitcast.124, f32[]{:T(128)} %bitcast.56, f32[]{:T(128)} %bitcast.55, f32[]{:T(128)} %bitcast.54, f32[]{:T(128)} %bitcast.53, f32[]{:T(128)} %bitcast.52, f32[]{:T(128)} %bitcast.51, f32[]{:T(128)} %bitcast.50, ...), kind=kOutput, calls=%fused_computation.92 | convolution fusion | flops 136806400 | bytes 3145860 | tf_op jit(solution)/shard_map/dot_general | solution.py:54
  312.5 22.2 %convolution_add_fusion.4 = f32[2048,128]{1,0:T(8,128)S(1)} fusion(f32[2048,128]{1,0:T(8,128)S(1)} %convolution_add_fusion.5, bf16[2048,256]{1,0:T(8,128)(2,1)} %bitcast.122, f32[]{:T(128)} %bitcast.56, f32[]{:T(128)} %bitcast.55, f32[]{:T(128)} %bitcast.54, f32[]{:T(128)} %bitcast.53, f32[]{:T(128)} %bitcast.52, f32[]{:T(128)} %bitcast.51, f32[]{:T(128)} %bitcast.50, ...), kind=kOutput, calls=%fused_computation.91 | convolution fusion | flops 136773632 | bytes 3145860 | tf_op jit(solution)/shard_map/dot_general | solution.py:55
  338.8 22.2 %fusion.107 = f32[2048,128]{1,0:T(8,128)S(1)} fusion(bf16[2048,256]{1,0:T(8,128)(2,1)} %bitcast.125, f32[]{:T(128)} %bitcast.24, f32[]{:T(128)} %bitcast.25, f32[]{:T(128)} %bitcast.26, f32[]{:T(128)} %bitcast.27, f32[]{:T(128)} %bitcast.28, f32[]{:T(128)} %bitcast.29, f32[]{:T(128)} %bitcast.30, f32[]{:T(128)} %bitcast.31, f32[]{:T(128)} %bitcast.32, ...), kind=kOutput, calls=%fused_computation.170 | convolution fusion | flops 136511488 | bytes 2097284 | tf_op jit(solution)/shard_map/dot_general | solution.py:53
  361.0 22.2 %convolution_add_fusion.3 = f32[2048,128]{1,0:T(8,128)S(1)} fusion(f32[2048,128]{1,0:T(8,128)S(1)} %fusion.107, bf16[2048,256]{1,0:T(8,128)(2,1)} %bitcast.126, f32[]{:T(128)} %bitcast.56, f32[]{:T(128)} %bitcast.55, f32[]{:T(128)} %bitcast.54, f32[]{:T(128)} %bitcast.53, f32[]{:T(128)} %bitcast.52, f32[]{:T(128)} %bitcast.51, f32[]{:T(128)} %bitcast.50, ...), kind=kOutput, calls=%fused_computation.90 | convolution fusion | flops 136806400 | bytes 3145860 | tf_op jit(solution)/shard_map/dot_general | solution.py:54
  383.2 21.0 %fusion.51 = bf16[2048,128]{1,0:T(8,128)(2,1)S(1)} fusion(f32[2048,128]{1,0:T(8,128)S(1)} %convolution_add_fusion.3, bf16[2048,256]{1,0:T(8,128)(2,1)S(1)} %bitcast.121, f32[]{:T(128)} %bitcast.24, f32[]{:T(128)} %bitcast.25, f32[]{:T(128)} %bitcast.26, f32[]{:T(128)} %bitcast.27, f32[]{:T(128)} %bitcast.28, f32[]{:T(128)} %bitcast.29, f32[]{:T(128)} %bitcast.30, ...), kind=kOutput, calls=%fused_computation.93 | convolution fusion | flops 137035776 | bytes 2621572 | tf_op jit(solution)/shard_map/dot_general | solution.py:55
  405.5 58.9 %all_gather.6 = f32[512,72]{1,0:T(8,128)S(1)} all-gather(f32[16,72]{1,0:T(8,128)S(1)} %add_convert_fusion), channel_id=1, replica_groups=mesh['inline'=4,'xline'=8] {'inline','xline'}, dimensions={0}, use_global_device_ids=true | all-gather | bytes 152064 | tf_op jit(solution)/shard_map/all_gather | solution.py:90
  475.3 42.6 %all-gather.2.cloned.1.call-done = bf16[4096,2048]{1,0:T(8,128)(2,1)} async-done(((bf16[128,2048]{1,0:T(8,128)(2,1)}), bf16[4096,2048]{1,0:T(8,128)(2,1)}) %all-gather.2.cloned.1.call-update) | async-done | bytes 16777232 | tf_op jit(solution)/shard_map/all_gather | solution.py:132
  517.9 14.4 %gather_fusion.3 = bf16[256,8,2048]{2,1,0:T(8,128)(2,1)} fusion(bf16[512,8,2048]{2,1,0:T(8,128)(2,1)} %bitcast.120, s32[1024]{0:T(1024)S(1)} %pad_clamp_fusion.1), kind=kCustom, calls=%fused_computation.3 | custom fusion | bytes 16778240 | tf_op jit(solution)/shard_map/jit(_take)/gather | solution.py:154
  532.4 14.8 %fusion.42 = f32[2048,1024]{1,0:T(8,128)} fusion(bf16[256,8,2048]{2,1,0:T(8,128)(2,1)} %gather_fusion.3, pred[256]{0:T(512)(128)(4,1)S(1)} %compare_and_fusion.3, bf16[1,1,2048,1024]{3,2,1,0:T(8,128)(2,1)} %param.8), kind=kOutput, calls=%fused_computation.77 | convolution fusion | flops 8594128896 | bytes 20971776 | tf_op jit(solution)/shard_map/dot_general | solution.py:155
  547.2 22.9 %scatter_custom_fusion.2 = f32[2048,1024]{1,0:T(8,128)} fusion(s32[2048]{0:T(1024)S(1)} %bitcast.130, f32[2048,1024]{1,0:T(8,128)} %fusion.42, f32[]{:T(128)} %constant.49.clone.1), kind=kCustom, calls=%fused_computation.87 | custom fusion | flops 2097152 | bytes 8389120 | tf_op jit(solution)/shard_map/scatter-add | solution.py:163
  599.8 12.6 %copy.146 = bf16[2048,8,256]{2,1,0:T(8,128)(2,1)} copy(bf16[2048,8,256]{0,2,1:T(8,128)(2,1)} %pad_maximum_fusion.4) | data formatting | bytes 16777216 | tf_op jit(solution)/shard_map/concatenate | solution.py:43
  633.4 12.6 %copy.144 = bf16[2048,8,256]{2,1,0:T(8,128)(2,1)} copy(bf16[2048,8,256]{0,2,1:T(8,128)(2,1)} %pad_maximum_fusion.3) | data formatting | bytes 16777216 | tf_op jit(solution)/shard_map/concatenate | solution.py:43
  646.0 11.8 %fusion.40 = f32[16384,128]{1,0:T(8,128)S(1)} fusion(bf16[2048,8,256]{2,1,0:T(8,128)(2,1)} %copy.144, f32[]{:T(128)} %bitcast, f32[]{:T(128)} %bitcast.74, f32[]{:T(128)} %bitcast.73, f32[]{:T(128)} %bitcast.72, f32[]{:T(128)} %bitcast.71, f32[]{:T(128)} %bitcast.70, f32[]{:T(128)} %bitcast.69, f32[]{:T(128)} %bitcast.68, f32[]{:T(128)} %bitcast.67), kind=kOutput, calls=%fused_computation.75 | convolution fusion | flops 1074462720 | bytes 16777252 | tf_op jit(solution)/shard_map/dot_general | solution.py:53
  665.8 11.3 %convolution_add_fusion = f32[16384,128]{1,0:T(8,128)S(1)} fusion(f32[16384,128]{1,0:T(8,128)S(1)} %convolution_add_fusion.1, bf16[2048,8,256]{2,1,0:T(8,128)(2,1)} %copy.146, f32[]{:T(128)} %bitcast, f32[]{:T(128)} %bitcast.74, f32[]{:T(128)} %bitcast.73, f32[]{:T(128)} %bitcast.72, f32[]{:T(128)} %bitcast.71, f32[]{:T(128)} %bitcast.70, f32[]{:T(128)} %bitcast.69, ...), kind=kOutput, calls=%fused_computation.8 | convolution fusion | flops 1076559872 | bytes 25165860 | tf_op jit(solution)/shard_map/dot_general | solution.py:55
  688.0 9.5 %reshape_reshape.7 = f32[32,64,1024]{2,1,0:T(8,128)} reshape(f32[16384,128]{1,0:T(8,128)} %copy-done.1) | data formatting | bytes 16777216 | tf_op jit(solution)/shard_map/reshape;reshape | solution.py:166
  697.5 14.4 %constant_dynamic-update-slice_fusion = (f32[36,64,1024]{2,0,1:T(8,128)}, f32[32,64,1024]{2,0,1:T(8,128)}) fusion(f32[32,64,1024]{2,1,0:T(8,128)} %reshape_reshape.7), kind=kLoop, calls=%fused_computation.192 | loop fusion | bytes 25165824
  715.4 48.6 %fusion.8 = f32[32,64,1024]{2,0,1:T(8,128)} fusion(f32[32,64,1024]{2,0,1:T(8,128)} %get-tuple-element.25, f32[4,64,1024]{2,0,1:T(4,128)S(1)} %copy.147, f32[36,64,1024]{2,0,1:T(8,128)} %copy_dynamic-update-slice_fusion, f32[]{:T(128)} %bitcast.67, f32[]{:T(128)} %bitcast.68, f32[]{:T(128)} %bitcast.69, f32[]{:T(128)} %bitcast.70, f32[]{:T(128)} %bitcast.71, ...), kind=kLoop, calls=%fused_computation.32 | loop fusion | flops 44040192 | bytes 51380260 | tf_op jit(solution)/shard_map/add | solution.py:66
  770.8 20.0 %collective-permute-done.2 = f32[32,4,1024]{2,0,1:T(8,128)S(1)} collective-permute-done((f32[32,4,1024]{2,0,1:T(8,128)S(1)}, f32[32,4,1024]{2,0,1:T(8,128)S(1)}, u32[]{:S(2)}, u32[]{:S(2)}) %collective-permute-start.2) | collective-permute-done | bytes 524320 | tf_op jit(solution)/shard_map/ppermute | solution.py:15
  790.7 34.8 %fusion.18 = f32[32,64,1024]{2,0,1:T(8,128)} fusion(f32[32,4,1024]{2,0,1:T(8,128)S(1)} %collective-permute-done.3, f32[32,4,1024]{2,0,1:T(8,128)S(1)} %collective-permute-done.2, f32[32,64,1024]{2,0,1:T(8,128)} %fusion.8, f32[]{:T(128)} %bitcast.67, f32[]{:T(128)} %bitcast.68, f32[]{:T(128)} %bitcast.69, f32[]{:T(128)} %bitcast.70, f32[]{:T(128)} %bitcast.71, ...), kind=kLoop, calls=%fused_computation.42 | loop fusion | flops 52428800 | bytes 17825828 | tf_op jit(solution)/shard_map/add | solution.py:66
  825.6 11.6 %copy.152 = f32[32,64,1024]{2,1,0:T(8,128)} copy(f32[32,64,1024]{2,0,1:T(8,128)} %fusion.18) | data formatting | bytes 16777216
  (126 shorter events, 137.3 us)
Async XLA Ops:
  11.0 21.1 %all-to-all-start = ((s32[32,1,64]{2,1,0:T(1,128)}), s32[32,1,64]{2,1,0:T(1,128)S(1)}, u32[]{:S(2)}, u32[]{:S(2)}) async-start(s32[32,1,64]{2,1,0:T(1,128)} %bitcast.13), calls=%async_computation | async-start | bytes 32768 | tf_op jit(solution)/shard_map/all_to_all | solution.py:106
  61.8 6.2 copy-start.3
  61.8 6.6 copy-start.2
  61.8 195.0 %all-to-all-start.1 = ((bf16[32,64,2048]{2,1,0:T(8,128)(2,1)}), bf16[32,64,2048]{2,1,0:T(8,128)(2,1)}, u32[]{:S(2)}, u32[]{:S(2)}) async-start(bf16[32,64,2048]{2,1,0:T(8,128)(2,1)} %broadcast_select_fusion), calls=%async_computation.1 | async-start | bytes 16777216 | tf_op jit(solution)/shard_map/all_to_all | solution.py:73
  67.7 450.2 %all-gather.2.cloned.1.call-start = ((), (), s32[]{:S(2)}) async-start(), calls=%async_computation.2 | async-start | bytes 17301504 | tf_op jit(solution)/shard_map/all_gather | solution.py:132
  337.1 68.1 %copy-start.5 = (s32[128,8]{0,1:T(8,128)S(1)}, s32[128,8]{0,1:T(8,128)}, u32[]{:S(2)}) copy-start(s32[128,8]{0,1:T(8,128)} %param.13) | copy-start | bytes 12292
  383.2 91.4 %copy-start.4 = (f32[9]{0:T(128)S(1)}, f32[9]{0:T(128)}, u32[]{:S(2)}) copy-start(f32[9]{0:T(128)} %param.11) | copy-start | bytes 112
  646.0 11.8 %copy-start = (bf16[2048,8,256]{2,1,0:T(8,128)(2,1)S(1)}, bf16[2048,8,256]{2,1,0:T(8,128)(2,1)}, u32[]{:S(2)}) copy-start(bf16[2048,8,256]{2,1,0:T(8,128)(2,1)} %copy.144) | copy-start | bytes 25165828
  677.1 3.4 copy-start.1
  681.8 30.1 %collective-permute-start = (f32[4,64,1024]{2,1,0:T(8,128)}, f32[4,64,1024]{2,1,0:T(8,128)S(1)}, u32[]{:S(2)}, u32[]{:S(2)}) collective-permute-start(f32[4,64,1024]{2,1,0:T(8,128)} %slice.400), channel_id=1, source_target_pairs={{0,8},{8,16},{16,24},{1,9},{9,17},{17,25},{2,10},{10,18},{18,26},{... | collective-permute-start | bytes 3145736 | tf_op jit(solution)/shard_map/ppermute | solution.py:15
  686.0 26.5 %collective-permute-start.1 = (f32[4,64,1024]{2,1,0:T(8,128)}, f32[4,64,1024]{2,1,0:T(8,128)}, u32[]{:S(2)}, u32[]{:S(2)}) collective-permute-start(f32[4,64,1024]{2,1,0:T(8,128)} %slice.406), channel_id=1, source_target_pairs={{8,0},{16,8},{24,16},{9,1},{17,9},{25,17},{10,2},{18,10},{26,18},{... | collective-permute-start | bytes 3145736 | tf_op jit(solution)/shard_map/ppermute | solution.py:18
  765.3 25.4 %collective-permute-start.2 = (f32[32,4,1024]{2,0,1:T(8,128)S(1)}, f32[32,4,1024]{2,0,1:T(8,128)S(1)}, u32[]{:S(2)}, u32[]{:S(2)}) collective-permute-start(f32[32,4,1024]{2,0,1:T(8,128)S(1)} %get-tuple-element.20), channel_id=1, source_target_pairs={{0,1},{1,2},{2,3},{3,4},{4,5},{5,6},{6,7},{8,9},{9,10},{10,11},{11... | collective-permute-start | bytes 1572872 | tf_op jit(solution)/shard_map/ppermute | solution.py:15
  767.9 22.8 %collective-permute-start.3 = (f32[32,4,1024]{2,0,1:T(8,128)S(1)}, f32[32,4,1024]{2,0,1:T(8,128)S(1)}, u32[]{:S(2)}, u32[]{:S(2)}) collective-permute-start(f32[32,4,1024]{2,0,1:T(8,128)S(1)} %get-tuple-element.21), channel_id=1, source_target_pairs={{1,0},{2,1},{3,2},{4,3},{5,4},{6,5},{7,6},{9,8},{10,9},{11,10},{12... | collective-permute-start | bytes 1572872 | tf_op jit(solution)/shard_map/ppermute | solution.py:18
Sparse Core Ops, SparseCore 0:
  405.3 112.5 all-gather.1

commit v3 on v2

--- a/solution.py
+++ b/solution.py
@@ -47,7 +47,7 @@
 def banded(signal, block):
     rows, length = signal.shape
     x_high, x_low = split(signal)
-    b_high, b_low = split(block)
+    b_high, b_low = lax.optimization_barrier(split(block))
     w_high, w_low = windows(x_high), windows(x_low)
     out = (
         jnp.dot(w_high, b_high, preferred_element_type=jnp.float32)

time: 856 us -> 713 us (0.83)
  matrix products: 189 us -> 46.5 us
  waiting for transfers between devices: 250 us -> 160 us
  other arithmetic: 148 us -> 236 us
    convert_element_type x4 -> x9, other arithmetic: 8.88 us -> 97.7 us  [split(): return (high.astype(jnp.bfloat16), (x - high).astype(jnp.bfloat16))]
    all_to_all x1, waiting for transfers between devices: 187 us -> 104 us  [traverse(): lax.all_to_all(blocks, ('inline', 'xline'), split_axis=0, concat_axis=0,...]
    dot_general x3, matrix products: 54.9 us -> 6.69 us  [banded(): jnp.dot(w_high, b_high, preferred_element_type=jnp.float32)]
    dot_general x3, matrix products: 51.1 us -> 3.21 us  [banded(): jnp.dot(w_high, b_low, preferred_element_type=jnp.float32)]
    dot_general x3, matrix products: 54.5 us -> 7.82 us  [banded(): jnp.dot(w_low, b_high, preferred_element_type=jnp.float32)]
  transfers between devices with their start and end apart: 7 -> 7, of which waited for: 3 -> 3; matrix products, arithmetic and copies ran while one was open for 6% -> 20% of each run, Pallas kernels for 0% -> 0%
where the time goes in v3:
time: 713 us; the launch traced here: 702 us
  other arithmetic  236 us (33%)
  local copies, waits for them, and re-layouts  162 us (23%)
  waiting for transfers between devices  160 us (22%)
  blocking collectives  59.9 us (8%)
  matrix products  46.5 us (7%)
  starting transfers between devices  22 us (3%)
  between operations  15.1 us (2%)
    all_to_all x1, waiting for transfers between devices, traverse(): lax.all_to_all(blocks, ('inline', 'xline'), split_axis=0, concat_axis=0,...  104 us
    convert_element_type x9, other arithmetic, split(): return (high.astype(jnp.bfloat16), (x - high).astype(jnp.bfloat16))  97.7 us
    add x2, other arithmetic, filter_padded(): result + taps[offset] * lax.slice_in_dim(padded, offset, offset + length,...  83.5 us
    all_gather x1, blocking collectives, local(): tables_all = jnp.round(lax.all_gather(tables, axes, axis=0, tiled=True))  59.9 us
    unnamed x23, local copies, waits for them, and re-layouts  46.1 us
    all_gather x1, waiting for transfers between devices, local(): adjoint_all = lax.all_gather(adjoint, axes, axis=0, tiled=True)  36.5 us
    concatenate x6, local copies, waits for them, and re-layouts, windows(): joined = jnp.concatenate([pieces[:, :chunks], pieces[:, 1:]], axis=-1)  29.6 us
    scatter-add x1, other arithmetic, local(): raw_gradient = jnp.zeros((cell_count, depth_len), jnp.float32).at[cells.r...  22.9 us
  transfers between devices with their start and end apart: 7, of which 3 were waited for; matrix products, arithmetic and copies ran while one was open for 20% of the time, Pallas kernels for 0%

profile of v3, /device:TPU:1, one launch (start us, length us, event | category | flops | bytes accessed | tf_op | source)
XLA Modules:
  0.0 701.9 jit_solution(18150177715952923037)
XLA Ops:
  18.1 14.0 %convolution_convert_fusion = bf16[2048,2048]{1,0:T(8,128)(2,1)} fusion(bf16[2048,1024]{1,0:T(8,128)(2,1)} %bitcast.143, bf16[1,1,2048,1024]{3,2,1,0:T(8,128)(2,1)} %param.8), kind=kOutput, calls=%fused_computation.83 | convolution fusion | flops 8594128896 | bytes 16777216 | tf_op jit(solution)/shard_map/dot_general | solution.py:117
  33.4 20.8 %gather_fusion.1 = bf16[2048,2048]{1,0:T(8,128)(2,1)} fusion(bf16[2048,2048]{1,0:T(8,128)(2,1)} %convolution_convert_fusion, s32[2048]{0:T(1024)S(1)} %broadcast_clamp_fusion), kind=kCustom, calls=%fused_computation.1 | custom fusion | bytes 16785408 | tf_op jit(solution)/shard_map/jit(_take)/gather | solution.py:120
  54.2 7.6 %broadcast_select_fusion = bf16[32,64,2048]{2,1,0:T(8,128)(2,1)} fusion(bf16[32,64,2048]{2,1,0:T(8,128)(2,1)} %bitcast.124, pred[32,64]{1,0:T(8,128)(4,1)S(1)} %compare_and_fusion), kind=kLoop, calls=%fused_computation.82 | loop fusion | flops 4194304 | bytes 16779264 | tf_op jit(solution)/shard_map/jit(_take)/select_n | solution.py:120
  69.5 20.5 %fusion.55 = bf16[256,128]{1,0:T(8,128)(2,1)S(1)} fusion(f32[]{:T(128)} %bitcast.24, f32[]{:T(128)} %bitcast.25, f32[]{:T(128)} %bitcast.26, f32[]{:T(128)} %bitcast.27, f32[]{:T(128)} %bitcast.28, f32[]{:T(128)} %bitcast.29, f32[]{:T(128)} %bitcast.30, f32[]{:T(128)} %bitcast.31, f32[]{:T(128)} %bitcast.32, f32[]{:T(128)} %bitcast.33, f32[]{:T(128)} %bitcast.34, ...), kind=kLoop, calls=%fused_computation.113 | loop fusion | flops 2326528 | bytes 65668 | tf_op jit(solution)/shard_map/convert_element_type | solution.py:35
  90.1 20.5 %reduce-precision_convert_fusion.4 = bf16[256,128]{1,0:T(8,128)(2,1)S(1)} fusion(f32[]{:T(128)} %bitcast.24, f32[]{:T(128)} %bitcast.25, f32[]{:T(128)} %bitcast.26, f32[]{:T(128)} %bitcast.27, f32[]{:T(128)} %bitcast.28, f32[]{:T(128)} %bitcast.29, f32[]{:T(128)} %bitcast.30, f32[]{:T(128)} %bitcast.31, f32[]{:T(128)} %bitcast.32, f32[]{:T(128)} %bitcast.33, ...), kind=kLoop, calls=%fused_computation.109 | loop fusion | flops 2293760 | bytes 65668 | tf_op jit(solution)/shard_map/convert_element_type | solution.py:35
  110.6 20.5 %fusion.54 = bf16[256,128]{1,0:T(8,128)(2,1)S(1)} fusion(f32[]{:T(128)} %bitcast.56, f32[]{:T(128)} %bitcast.55, f32[]{:T(128)} %bitcast.54, f32[]{:T(128)} %bitcast.53, f32[]{:T(128)} %bitcast.52, f32[]{:T(128)} %bitcast.51, f32[]{:T(128)} %bitcast.50, f32[]{:T(128)} %bitcast.49, f32[]{:T(128)} %bitcast.48, f32[]{:T(128)} %bitcast.47, f32[]{:T(128)} %bitcast.46, ...), kind=kLoop, calls=%fused_computation.112 | loop fusion | flops 2326528 | bytes 65668 | tf_op jit(solution)/shard_map/convert_element_type | solution.py:35
  131.2 20.5 %reduce-precision_convert_fusion.5 = bf16[256,128]{1,0:T(8,128)(2,1)S(1)} fusion(f32[]{:T(128)} %bitcast.56, f32[]{:T(128)} %bitcast.55, f32[]{:T(128)} %bitcast.54, f32[]{:T(128)} %bitcast.53, f32[]{:T(128)} %bitcast.52, f32[]{:T(128)} %bitcast.51, f32[]{:T(128)} %bitcast.50, f32[]{:T(128)} %bitcast.49, f32[]{:T(128)} %bitcast.48, f32[]{:T(128)} %bitcast.47, ...), kind=kLoop, calls=%fused_computation.111 | loop fusion | flops 2293760 | bytes 65668 | tf_op jit(solution)/shard_map/convert_element_type | solution.py:35
  152.7 104.1 %all-to-all-done.1 = bf16[32,64,2048]{2,1,0:T(8,128)(2,1)} async-done(((bf16[32,64,2048]{2,1,0:T(8,128)(2,1)}), bf16[32,64,2048]{2,1,0:T(8,128)(2,1)}, u32[]{:S(2)}, u32[]{:S(2)}) %all-to-all-start.1) | async-done | bytes 8388640 | tf_op jit(solution)/shard_map/all_to_all | solution.py:73
  286.5 59.9 %all_gather.6 = f32[512,72]{1,0:T(8,128)S(1)} all-gather(f32[16,72]{1,0:T(8,128)S(1)} %add_convert_fusion), channel_id=1, replica_groups=mesh['inline'=4,'xline'=8] {'inline','xline'}, dimensions={0}, use_global_device_ids=true | all-gather | bytes 152064 | tf_op jit(solution)/shard_map/all_gather | solution.py:90
  356.6 36.5 %all-gather.2.cloned.1.call-done = bf16[4096,2048]{1,0:T(8,128)(2,1)} async-done(((bf16[128,2048]{1,0:T(8,128)(2,1)}), bf16[4096,2048]{1,0:T(8,128)(2,1)}) %all-gather.2.cloned.1.call-update) | async-done | bytes 16777232 | tf_op jit(solution)/shard_map/all_gather | solution.py:132
  393.1 14.6 %gather_fusion.3 = bf16[256,8,2048]{2,1,0:T(8,128)(2,1)} fusion(bf16[512,8,2048]{2,1,0:T(8,128)(2,1)} %bitcast.134, s32[1024]{0:T(1024)S(1)} %pad_clamp_fusion.1), kind=kCustom, calls=%fused_computation.3 | custom fusion | bytes 16778240 | tf_op jit(solution)/shard_map/jit(_take)/gather | solution.py:154
  407.6 14.8 %fusion.42 = f32[2048,1024]{1,0:T(8,128)} fusion(bf16[256,8,2048]{2,1,0:T(8,128)(2,1)} %gather_fusion.3, pred[256]{0:T(512)(128)(4,1)S(1)} %compare_and_fusion.3, bf16[1,1,2048,1024]{3,2,1,0:T(8,128)(2,1)} %param.8), kind=kOutput, calls=%fused_computation.77 | convolution fusion | flops 8594128896 | bytes 20971776 | tf_op jit(solution)/shard_map/dot_general | solution.py:155
  422.4 22.9 %scatter_custom_fusion.2 = f32[2048,1024]{1,0:T(8,128)} fusion(s32[2048]{0:T(1024)S(1)} %bitcast.139, f32[2048,1024]{1,0:T(8,128)} %fusion.42, f32[]{:T(128)} %constant.49.clone.1), kind=kCustom, calls=%fused_computation.87 | custom fusion | flops 2097152 | bytes 8389120 | tf_op jit(solution)/shard_map/scatter-add | solution.py:163
  445.3 8.5 %fusion.14 = (bf16[2048,1024]{1,0:T(8,128)(2,1)}, bf16[2048,1024]{1,0:T(8,128)(2,1)}) fusion(f32[2048,1024]{1,0:T(8,128)} %scatter_custom_fusion.2), kind=kLoop, calls=%fused_computation.38 | loop fusion | flops 8388608 | bytes 16777216 | tf_op jit(solution)/shard_map/convert_element_type | solution.py:35
  466.5 8.5 %pad_maximum_fusion.4 = bf16[2048,8,256]{0,2,1:T(8,128)(2,1)} fusion(bf16[2048,8,128]{0,2,1:T(8,128)(2,1)} %get-tuple-element.41, bf16[2048,8,128]{0,2,1:T(8,128)(2,1)} %get-tuple-element.40), kind=kLoop, calls=%fused_computation.72 | loop fusion | flops 16777216 | bytes 16777216 | tf_op jit(solution)/shard_map/concatenate | solution.py:43
  475.0 12.6 %copy.146 = bf16[2048,8,256]{2,1,0:T(8,128)(2,1)} copy(bf16[2048,8,256]{0,2,1:T(8,128)(2,1)} %pad_maximum_fusion.4) | data formatting | bytes 16777216 | tf_op jit(solution)/shard_map/concatenate | solution.py:43
  500.1 8.5 %pad_maximum_fusion.3 = bf16[2048,8,256]{0,2,1:T(8,128)(2,1)} fusion(bf16[2048,8,128]{0,2,1:T(8,128)(2,1)} %get-tuple-element.43, bf16[2048,8,128]{0,2,1:T(8,128)(2,1)} %get-tuple-element.42), kind=kLoop, calls=%fused_computation.71 | loop fusion | flops 16777216 | bytes 16777216 | tf_op jit(solution)/shard_map/concatenate | solution.py:43
  508.7 12.6 %copy.144 = bf16[2048,8,256]{2,1,0:T(8,128)(2,1)} copy(bf16[2048,8,256]{0,2,1:T(8,128)(2,1)} %pad_maximum_fusion.3) | data formatting | bytes 16777216 | tf_op jit(solution)/shard_map/concatenate | solution.py:43
  546.1 9.5 %reshape_reshape.7 = f32[32,64,1024]{2,1,0:T(8,128)} reshape(f32[16384,128]{1,0:T(8,128)} %copy-done.1) | data formatting | bytes 16777216 | tf_op jit(solution)/shard_map/reshape;reshape | solution.py:166
  555.6 14.4 %constant_dynamic-update-slice_fusion = (f32[36,64,1024]{2,0,1:T(8,128)}, f32[32,64,1024]{2,0,1:T(8,128)}) fusion(f32[32,64,1024]{2,1,0:T(8,128)} %reshape_reshape.7), kind=kLoop, calls=%fused_computation.190 | loop fusion | bytes 25165824
  573.6 48.6 %fusion.8 = f32[32,64,1024]{2,0,1:T(8,128)} fusion(f32[32,64,1024]{2,0,1:T(8,128)} %get-tuple-element.37, f32[4,64,1024]{2,0,1:T(4,128)S(1)} %copy.147, f32[36,64,1024]{2,0,1:T(8,128)} %copy_dynamic-update-slice_fusion, f32[]{:T(128)} %bitcast.67, f32[]{:T(128)} %bitcast.68, f32[]{:T(128)} %bitcast.69, f32[]{:T(128)} %bitcast.70, f32[]{:T(128)} %bitcast.71, ...), kind=kLoop, calls=%fused_computation.32 | loop fusion | flops 44040192 | bytes 51380260 | tf_op jit(solution)/shard_map/add | solution.py:66
  628.5 19.6 %collective-permute-done.2 = f32[32,4,1024]{2,0,1:T(8,128)S(1)} collective-permute-done((f32[32,4,1024]{2,0,1:T(8,128)S(1)}, f32[32,4,1024]{2,0,1:T(8,128)S(1)}, u32[]{:S(2)}, u32[]{:S(2)}) %collective-permute-start.2) | collective-permute-done | bytes 524320 | tf_op jit(solution)/shard_map/ppermute | solution.py:15
  648.2 34.8 %fusion.18 = f32[32,64,1024]{2,0,1:T(8,128)} fusion(f32[32,4,1024]{2,0,1:T(8,128)S(1)} %collective-permute-done.3, f32[32,4,1024]{2,0,1:T(8,128)S(1)} %collective-permute-done.2, f32[32,64,1024]{2,0,1:T(8,128)} %fusion.8, f32[]{:T(128)} %bitcast.67, f32[]{:T(128)} %bitcast.68, f32[]{:T(128)} %bitcast.69, f32[]{:T(128)} %bitcast.70, f32[]{:T(128)} %bitcast.71, ...), kind=kLoop, calls=%fused_computation.42 | loop fusion | flops 52428800 | bytes 17825828 | tf_op jit(solution)/shard_map/add | solution.py:66
  683.0 11.6 %copy.152 = f32[32,64,1024]{2,1,0:T(8,128)} copy(f32[32,64,1024]{2,0,1:T(8,128)} %fusion.18) | data formatting | bytes 16777216
  (131 shorter events, 120.2 us)
Async XLA Ops:
  11.0 21.1 %all-to-all-start = ((s32[32,1,64]{2,1,0:T(1,128)}), s32[32,1,64]{2,1,0:T(1,128)S(1)}, u32[]{:S(2)}, u32[]{:S(2)}) async-start(s32[32,1,64]{2,1,0:T(1,128)} %bitcast.13), calls=%async_computation | async-start | bytes 32768 | tf_op jit(solution)/shard_map/all_to_all | solution.py:106
  61.8 6.2 copy-start.2
  61.8 89.9 %copy-start.3 = (bf16[128,2048]{1,0:T(8,128)(2,1)S(1)}, bf16[128,2048]{1,0:T(8,128)(2,1)}, u32[]{:S(2)}) copy-start(bf16[128,2048]{1,0:T(8,128)(2,1)} %param.9) | copy-start | bytes 1572868
  61.8 195.0 %all-to-all-start.1 = ((bf16[32,64,2048]{2,1,0:T(8,128)(2,1)}), bf16[32,64,2048]{2,1,0:T(8,128)(2,1)}, u32[]{:S(2)}, u32[]{:S(2)}) async-start(bf16[32,64,2048]{2,1,0:T(8,128)(2,1)} %broadcast_select_fusion), calls=%async_computation.1 | async-start | bytes 16777216 | tf_op jit(solution)/shard_map/all_to_all | solution.py:73
  67.7 325.3 %all-gather.2.cloned.1.call-start = ((), (), s32[]{:S(2)}) async-start(), calls=%async_computation.2 | async-start | bytes 17301504 | tf_op jit(solution)/shard_map/all_gather | solution.py:132
  275.0 4.9 copy-start.5
  275.0 5.1 copy-start.4
  521.3 5.9 copy-start
  535.3 3.4 copy-start.1
  539.9 30.1 %collective-permute-start = (f32[4,64,1024]{2,1,0:T(8,128)}, f32[4,64,1024]{2,1,0:T(8,128)S(1)}, u32[]{:S(2)}, u32[]{:S(2)}) collective-permute-start(f32[4,64,1024]{2,1,0:T(8,128)} %slice.400), channel_id=1, source_target_pairs={{0,8},{8,16},{16,24},{1,9},{9,17},{17,25},{2,10},{10,18},{18,26},{... | collective-permute-start | bytes 3145736 | tf_op jit(solution)/shard_map/ppermute | solution.py:15
  544.2 26.5 %collective-permute-start.1 = (f32[4,64,1024]{2,1,0:T(8,128)}, f32[4,64,1024]{2,1,0:T(8,128)}, u32[]{:S(2)}, u32[]{:S(2)}) collective-permute-start(f32[4,64,1024]{2,1,0:T(8,128)} %slice.406), channel_id=1, source_target_pairs={{8,0},{16,8},{24,16},{9,1},{17,9},{25,17},{10,2},{18,10},{26,18},{... | collective-permute-start | bytes 3145736 | tf_op jit(solution)/shard_map/ppermute | solution.py:18
  623.5 24.7 %collective-permute-start.2 = (f32[32,4,1024]{2,0,1:T(8,128)S(1)}, f32[32,4,1024]{2,0,1:T(8,128)S(1)}, u32[]{:S(2)}, u32[]{:S(2)}) collective-permute-start(f32[32,4,1024]{2,0,1:T(8,128)S(1)} %get-tuple-element.32), channel_id=1, source_target_pairs={{0,1},{1,2},{2,3},{3,4},{4,5},{5,6},{6,7},{8,9},{9,10},{10,11},{11... | collective-permute-start | bytes 1572872 | tf_op jit(solution)/shard_map/ppermute | solution.py:15
  625.7 22.5 %collective-permute-start.3 = (f32[32,4,1024]{2,0,1:T(8,128)S(1)}, f32[32,4,1024]{2,0,1:T(8,128)S(1)}, u32[]{:S(2)}, u32[]{:S(2)}) collective-permute-start(f32[32,4,1024]{2,0,1:T(8,128)S(1)} %get-tuple-element.33), channel_id=1, source_target_pairs={{1,0},{2,1},{3,2},{4,3},{5,4},{6,5},{7,6},{9,8},{10,9},{11,10},{12... | collective-permute-start | bytes 1572872 | tf_op jit(solution)/shard_map/ppermute | solution.py:18
Sparse Core Ops, SparseCore 0:
  280.0 112.9 all-gather.1

commit v4 on v3

--- a/solution.py
+++ b/solution.py
@@ -162,8 +162,9 @@
         .at[cells.reshape(relevant * per_block)]
         .add(per_trace, mode="drop")
     )
-    smooth_z = banded(raw_gradient, band_block(taps, taps.shape[0] // 2))
-    smooth_z = smooth_z.reshape(rows_x, rows_y, depth_len)
+    raw_gradient = raw_gradient.reshape(rows_x, rows_y, depth_len)
+    depth_padded = jnp.pad(raw_gradient, ((0, 0), (0, 0), (4, 4)))
+    smooth_z = filter_padded(depth_padded, taps, 2)
     inline_wide = extended(smooth_z, (("inline", 0),), 4)
     smooth_x = filter_padded(inline_wide, taps, 0)
     xline_wide = extended(smooth_x, (("xline", 1),), 4)

time: 713 us -> 632 us (0.89)
  local copies, waits for them, and re-layouts: 162 us -> 80.2 us
  matrix products: 46.5 us -> 32.6 us
  other arithmetic: 236 us -> 248 us
    add x2 -> x3, other arithmetic: 83.5 us -> 124 us  [filter_padded(): result + taps[offset] * lax.slice_in_dim(padded, offset, offset + length,...]
    unnamed x23 -> x17, local copies, waits for them, and re-layouts: 46.1 us -> 7.13 us
    concatenate x6 -> x4, local copies, waits for them, and re-layouts: 29.6 us -> 6.3 us  [windows(): joined = jnp.concatenate([pieces[:, :chunks], pieces[:, 1:]], axis=-1)]
    concatenate x6 -> x4, other arithmetic: 17.4 us -> 2.3 us  [windows(): joined = jnp.concatenate([pieces[:, :chunks], pieces[:, 1:]], axis=-1)]
    convert_element_type x9 -> x7, other arithmetic: 97.7 us -> 84.4 us  [split(): return (high.astype(jnp.bfloat16), (x - high).astype(jnp.bfloat16))]
    ppermute x2, waiting for transfers between devices: 0.01 us -> 12.4 us  [extended(): lax.ppermute(lax.slice_in_dim(block, 0, width, axis=dim), axis, backward)]
    ppermute x2, waiting for transfers between devices: 19.6 us -> 7.97 us  [extended(): lax.ppermute(lax.slice_in_dim(block, block.shape[dim] - width, None, axis...]
    another operation x2 -> x1, local copies, waits for them, and re-layouts: 9.62 us -> 0.11 us  [the longest x1 9.51 us: local(): smooth_z = smooth_z.reshape(rows_x, rows_y, depth_len)]
  transfers between devices with their start and end apart: 7 -> 7, of which waited for: 3 -> 6; matrix products, arithmetic and copies ran while one was open for 20% -> 19% of each run, Pallas kernels for 0% -> 0%
where the time goes in v4:
time: 632 us; the launch traced here: 623 us
  other arithmetic  248 us (39%)
  waiting for transfers between devices  163 us (26%)
  local copies, waits for them, and re-layouts  80.2 us (13%)
  blocking collectives  59 us (9%)
  matrix products  32.6 us (5%)
  starting transfers between devices  25.2 us (4%)
  between operations  15.1 us (2%)
    add x3, other arithmetic, filter_padded(): result + taps[offset] * lax.slice_in_dim(padded, offset, offset + length,...  124 us
    all_to_all x1, waiting for transfers between devices, traverse(): lax.all_to_all(blocks, ('inline', 'xline'), split_axis=0, concat_axis=0,...  104 us
    convert_element_type x7, other arithmetic, split(): return (high.astype(jnp.bfloat16), (x - high).astype(jnp.bfloat16))  84.4 us
    all_gather x1, blocking collectives, local(): tables_all = jnp.round(lax.all_gather(tables, axes, axis=0, tiled=True))  59 us
    all_gather x1, waiting for transfers between devices, local(): adjoint_all = lax.all_gather(adjoint, axes, axis=0, tiled=True)  38.3 us
    scatter-add x1, other arithmetic, local(): raw_gradient = jnp.zeros((cell_count, depth_len), jnp.float32).at[cells.r...  23.1 us
    gather x1, local copies, waits for them, and re-layouts, local(): predicted = jnp.take(tile_table.astype(jnp.bfloat16), cell_recv, axis=0)  20.8 us
    dot_general x1, matrix products, local(): jnp.dot(picked.reshape(relevant * per_block, samples), weight_matrix, pre...  14.8 us
  transfers between devices with their start and end apart: 7, of which 6 were waited for; matrix products, arithmetic and copies ran while one was open for 19% of the time, Pallas kernels for 0%

profile of v4, /device:TPU:1, one launch (start us, length us, event | category | flops | bytes accessed | tf_op | source)
XLA Modules:
  0.0 623.4 jit_solution(6601184565456372486)
XLA Ops:
  11.0 7.1 %all-to-all-start = ((s32[32,1,64]{2,1,0:T(1,128)}), s32[32,1,64]{2,1,0:T(1,128)S(1)}, u32[]{:S(2)}, u32[]{:S(2)}) async-start(s32[32,1,64]{2,1,0:T(1,128)} %bitcast.13), calls=%async_computation | async-start | bytes 32768 | tf_op jit(solution)/shard_map/all_to_all | solution.py:106
  18.1 14.0 %convolution_convert_fusion = bf16[2048,2048]{1,0:T(8,128)(2,1)} fusion(bf16[2048,1024]{1,0:T(8,128)(2,1)} %bitcast.128, bf16[1,1,2048,1024]{3,2,1,0:T(8,128)(2,1)} %param.8), kind=kOutput, calls=%fused_computation.110 | convolution fusion | flops 8594128896 | bytes 16777216 | tf_op jit(solution)/shard_map/dot_general | solution.py:117
  33.4 20.8 %gather_fusion.1 = bf16[2048,2048]{1,0:T(8,128)(2,1)} fusion(bf16[2048,2048]{1,0:T(8,128)(2,1)} %convolution_convert_fusion, s32[2048]{0:T(1024)S(1)} %broadcast_clamp_fusion), kind=kCustom, calls=%fused_computation.1 | custom fusion | bytes 16785408 | tf_op jit(solution)/shard_map/jit(_take)/gather | solution.py:120
  54.2 7.6 %broadcast_select_fusion = bf16[32,64,2048]{2,1,0:T(8,128)(2,1)} fusion(bf16[32,64,2048]{2,1,0:T(8,128)(2,1)} %bitcast.108, pred[32,64]{1,0:T(8,128)(4,1)S(1)} %compare_and_fusion), kind=kLoop, calls=%fused_computation.109 | loop fusion | flops 4194304 | bytes 16779264 | tf_op jit(solution)/shard_map/jit(_take)/select_n | solution.py:120
  61.8 5.9 all-to-all-start.1
  69.5 20.5 %reduce-precision_convert_fusion.3 = bf16[256,128]{1,0:T(8,128)(2,1)S(1)} fusion(f32[]{:T(128)} %bitcast.56, f32[]{:T(128)} %bitcast.55, f32[]{:T(128)} %bitcast.54, f32[]{:T(128)} %bitcast.53, f32[]{:T(128)} %bitcast.52, f32[]{:T(128)} %bitcast.51, f32[]{:T(128)} %bitcast.50, f32[]{:T(128)} %bitcast.49, f32[]{:T(128)} %bitcast.48, f32[]{:T(128)} %bitcast.47, ...), kind=kLoop, calls=%fused_computation.135 | loop fusion | flops 2293760 | bytes 65668 | tf_op jit(solution)/shard_map/convert_element_type | solution.py:35
  90.0 20.5 %fusion.72 = bf16[256,128]{1,0:T(8,128)(2,1)S(1)} fusion(f32[]{:T(128)} %bitcast.56, f32[]{:T(128)} %bitcast.55, f32[]{:T(128)} %bitcast.54, f32[]{:T(128)} %bitcast.53, f32[]{:T(128)} %bitcast.52, f32[]{:T(128)} %bitcast.51, f32[]{:T(128)} %bitcast.50, f32[]{:T(128)} %bitcast.49, f32[]{:T(128)} %bitcast.48, f32[]{:T(128)} %bitcast.47, f32[]{:T(128)} %bitcast.46, ...), kind=kLoop, calls=%fused_computation.136 | loop fusion | flops 2326528 | bytes 65668 | tf_op jit(solution)/shard_map/convert_element_type | solution.py:35
  111.6 20.5 %reduce-precision_convert_fusion.2 = bf16[256,128]{1,0:T(8,128)(2,1)S(1)} fusion(f32[]{:T(128)} %bitcast.24, f32[]{:T(128)} %bitcast.25, f32[]{:T(128)} %bitcast.26, f32[]{:T(128)} %bitcast.27, f32[]{:T(128)} %bitcast.28, f32[]{:T(128)} %bitcast.29, f32[]{:T(128)} %bitcast.30, f32[]{:T(128)} %bitcast.31, f32[]{:T(128)} %bitcast.32, f32[]{:T(128)} %bitcast.33, ...), kind=kLoop, calls=%fused_computation.133 | loop fusion | flops 2293760 | bytes 65668 | tf_op jit(solution)/shard_map/convert_element_type | solution.py:35
  132.1 20.5 %fusion.73 = bf16[256,128]{1,0:T(8,128)(2,1)S(1)} fusion(f32[]{:T(128)} %bitcast.24, f32[]{:T(128)} %bitcast.25, f32[]{:T(128)} %bitcast.26, f32[]{:T(128)} %bitcast.27, f32[]{:T(128)} %bitcast.28, f32[]{:T(128)} %bitcast.29, f32[]{:T(128)} %bitcast.30, f32[]{:T(128)} %bitcast.31, f32[]{:T(128)} %bitcast.32, f32[]{:T(128)} %bitcast.33, f32[]{:T(128)} %bitcast.34, ...), kind=kLoop, calls=%fused_computation.137 | loop fusion | flops 2326528 | bytes 65668 | tf_op jit(solution)/shard_map/convert_element_type | solution.py:35
  152.7 104.2 %all-to-all-done.1 = bf16[32,64,2048]{2,1,0:T(8,128)(2,1)} async-done(((bf16[32,64,2048]{2,1,0:T(8,128)(2,1)}), bf16[32,64,2048]{2,1,0:T(8,128)(2,1)}, u32[]{:S(2)}, u32[]{:S(2)}) %all-to-all-start.1) | async-done | bytes 8388640 | tf_op jit(solution)/shard_map/all_to_all | solution.py:73
  256.9 6.2 gather_fusion.2
  263.1 3.5 convert_reduce_fusion
  285.9 59.0 %all_gather.6 = f32[512,72]{1,0:T(8,128)S(1)} all-gather(f32[16,72]{1,0:T(8,128)S(1)} %add_convert_fusion), channel_id=1, replica_groups=mesh['inline'=4,'xline'=8] {'inline','xline'}, dimensions={0}, use_global_device_ids=true | all-gather | bytes 152064 | tf_op jit(solution)/shard_map/all_gather | solution.py:90
  348.1 6.0 gather_fusion.4
  360.2 38.3 %all-gather.2.cloned.1.call-done = bf16[4096,2048]{1,0:T(8,128)(2,1)} async-done(((bf16[128,2048]{1,0:T(8,128)(2,1)}), bf16[4096,2048]{1,0:T(8,128)(2,1)}) %all-gather.2.cloned.1.call-update) | async-done | bytes 16777232 | tf_op jit(solution)/shard_map/all_gather | solution.py:132
  398.4 14.6 %gather_fusion.3 = bf16[256,8,2048]{2,1,0:T(8,128)(2,1)} fusion(bf16[512,8,2048]{2,1,0:T(8,128)(2,1)} %bitcast.119, s32[1024]{0:T(1024)S(1)} %pad_clamp_fusion.1), kind=kCustom, calls=%fused_computation.3 | custom fusion | bytes 16778240 | tf_op jit(solution)/shard_map/jit(_take)/gather | solution.py:154
  413.0 14.8 %fusion.60 = f32[2048,1024]{1,0:T(8,128)} fusion(bf16[256,8,2048]{2,1,0:T(8,128)(2,1)} %gather_fusion.3, pred[256]{0:T(512)(128)(4,1)S(1)} %compare_and_fusion.3, bf16[1,1,2048,1024]{3,2,1,0:T(8,128)(2,1)} %param.8), kind=kOutput, calls=%fused_computation.104 | convolution fusion | flops 8594128896 | bytes 20971776 | tf_op jit(solution)/shard_map/dot_general | solution.py:155
  427.8 23.1 %scatter_custom_fusion.2 = f32[2048,1024]{1,0:T(8,128)} fusion(s32[2048]{0:T(1024)S(1)} %bitcast.124, f32[2048,1024]{1,0:T(8,128)} %fusion.60, f32[]{:T(128)} %constant.48.clone.1), kind=kCustom, calls=%fused_computation.114 | custom fusion | flops 2097152 | bytes 8389120 | tf_op jit(solution)/shard_map/scatter-add | solution.py:163
  450.9 44.9 %fusion.8 = f32[32,64,1024]{2,1,0:T(8,128)S(1)} fusion(f32[32,64,1024]{2,1,0:T(8,128)} %bitcast.109, f32[]{:T(128)} %bitcast.73, f32[]{:T(128)} %bitcast.72, f32[]{:T(128)} %bitcast.71, f32[]{:T(128)} %bitcast.70, f32[]{:T(128)} %bitcast.69, f32[]{:T(128)} %bitcast.68, f32[]{:T(128)} %bitcast.67, f32[]{:T(128)} %bitcast.66, f32[]{:T(128)} %bitcast), kind=kLoop, calls=%fused_computation.48 | loop fusion | flops 35651584 | bytes 16777252 | tf_op jit(solution)/shard_map/add | solution.py:66
  504.9 10.5 %collective-permute-done.1 = f32[4,64,1024]{2,1,0:T(8,128)S(1)} collective-permute-done((f32[4,64,1024]{2,1,0:T(8,128)S(1)}, f32[4,64,1024]{2,1,0:T(8,128)S(1)}, u32[]{:S(2)}, u32[]{:S(2)}) %collective-permute-start.1) | collective-permute-done | bytes 1048608 | tf_op jit(solution)/shard_map/ppermute | solution.py:18
  516.7 35.2 %fusion.39 = f32[32,64,1024]{2,1,0:T(8,128)} fusion(f32[32,64,1024]{2,1,0:T(8,128)} %copy-done, f32[4,64,1024]{2,1,0:T(8,128)S(1)} %collective-permute-done.1, f32[4,64,1024]{2,1,0:T(8,128)} %collective-permute-done, f32[]{:T(128)} %bitcast.73, f32[]{:T(128)} %bitcast.72, f32[]{:T(128)} %bitcast.71, f32[]{:T(128)} %bitcast.70, f32[]{:T(128)} %bitcast.69, ...), kind=kLoop, calls=%fused_computation.79 | loop fusion | flops 52428800 | bytes 18874404 | tf_op jit(solution)/shard_map/add | solution.py:66
  555.6 5.1 collective-permute-start.2
  564.2 6.8 %collective-permute-done.2 = f32[32,4,1024]{2,0,1:T(8,128)} collective-permute-done((f32[32,4,1024]{2,0,1:T(8,128)S(1)}, f32[32,4,1024]{2,0,1:T(8,128)}, u32[]{:S(2)}, u32[]{:S(2)}) %collective-permute-start.2) | collective-permute-done | bytes 524320 | tf_op jit(solution)/shard_map/ppermute | solution.py:15
  572.4 43.6 %fusion.19 = f32[32,64,1024]{2,1,0:T(8,128)} fusion(f32[32,64,1024]{2,1,0:T(8,128)} %fusion.39, f32[32,4,1024]{2,1,0:T(4,128)S(1)} %copy.121, f32[32,4,1024]{2,1,0:T(4,128)S(1)} %copy.119, f32[]{:T(128)} %bitcast.73, f32[]{:T(128)} %bitcast.72, f32[]{:T(128)} %bitcast.71, f32[]{:T(128)} %bitcast.70, f32[]{:T(128)} %bitcast.69, f32[]{:T(128)} %bitcast.68, ...), kind=kLoop, calls=%fused_computation.59 | loop fusion | flops 52428800 | bytes 17825828 | tf_op jit(solution)/shard_map/add | solution.py:66
  (112 shorter events, 55.0 us)
Async XLA Ops:
  11.0 21.1 %all-to-all-start = ((s32[32,1,64]{2,1,0:T(1,128)}), s32[32,1,64]{2,1,0:T(1,128)S(1)}, u32[]{:S(2)}, u32[]{:S(2)}) async-start(s32[32,1,64]{2,1,0:T(1,128)} %bitcast.13), calls=%async_computation | async-start | bytes 32768 | tf_op jit(solution)/shard_map/all_to_all | solution.py:106
  61.8 6.2 copy-start.1
  61.8 48.7 %copy-start.2 = (bf16[128,2048]{1,0:T(8,128)(2,1)S(1)}, bf16[128,2048]{1,0:T(8,128)(2,1)}, u32[]{:S(2)}) copy-start(bf16[128,2048]{1,0:T(8,128)(2,1)} %param.9) | copy-start | bytes 1572868
  61.8 195.0 %all-to-all-start.1 = ((bf16[32,64,2048]{2,1,0:T(8,128)(2,1)}), bf16[32,64,2048]{2,1,0:T(8,128)(2,1)}, u32[]{:S(2)}, u32[]{:S(2)}) async-start(bf16[32,64,2048]{2,1,0:T(8,128)(2,1)} %broadcast_select_fusion), calls=%async_computation.1 | async-start | bytes 16777216 | tf_op jit(solution)/shard_map/all_to_all | solution.py:73
  67.7 330.7 %all-gather.2.cloned.1.call-start = ((), (), s32[]{:S(2)}) async-start(), calls=%async_computation.2 | async-start | bytes 17301504 | tf_op jit(solution)/shard_map/all_gather | solution.py:132
  277.0 8.6 %copy-start.4 = (s32[128,8]{0,1:T(8,128)S(1)}, s32[128,8]{0,1:T(8,128)}, u32[]{:S(2)}) copy-start(s32[128,8]{0,1:T(8,128)} %param.13) | copy-start | bytes 12292
  282.5 77.0 %copy-start.3 = (f32[9]{0:T(128)S(1)}, f32[9]{0:T(128)}, u32[]{:S(2)}) copy-start(f32[9]{0:T(128)} %param.11) | copy-start | bytes 112
  495.8 3.4 copy-start
  499.4 16.1 %collective-permute-start.1 = (f32[4,64,1024]{2,1,0:T(8,128)S(1)}, f32[4,64,1024]{2,1,0:T(8,128)S(1)}, u32[]{:S(2)}, u32[]{:S(2)}) collective-permute-start(f32[4,64,1024]{2,1,0:T(8,128)S(1)} %get-tuple-element.31), channel_id=1, source_target_pairs={{8,0},{16,8},{24,16},{9,1},{17,9},{25,17},{10,2},{18,10},{26,18},{... | collective-permute-start | bytes 3145736 | tf_op jit(solution)/shard_map/ppermute | solution.py:18
  501.4 15.2 %collective-permute-start = (f32[4,64,1024]{2,1,0:T(8,128)S(1)}, f32[4,64,1024]{2,1,0:T(8,128)}, u32[]{:S(2)}, u32[]{:S(2)}) collective-permute-start(f32[4,64,1024]{2,1,0:T(8,128)S(1)} %get-tuple-element.30), channel_id=1, source_target_pairs={{0,8},{8,16},{16,24},{1,9},{9,17},{17,25},{2,10},{10,18},{18,26},{... | collective-permute-start | bytes 3145736 | tf_op jit(solution)/shard_map/ppermute | solution.py:15
  554.0 9.9 %collective-permute-start.3 = (f32[32,4,1024]{2,0,1:T(8,128)S(1)}, f32[32,4,1024]{2,0,1:T(8,128)S(1)}, u32[]{:S(2)}, u32[]{:S(2)}) collective-permute-start(f32[32,4,1024]{2,0,1:T(8,128)S(1)} %copy.120), channel_id=1, source_target_pairs={{1,0},{2,1},{3,2},{4,3},{5,4},{6,5},{7,6},{9,8},{10,9},{11,10},{12... | collective-permute-start | bytes 1572872 | tf_op jit(solution)/shard_map/ppermute | solution.py:18
  555.6 15.4 %collective-permute-start.2 = (f32[32,4,1024]{2,0,1:T(8,128)S(1)}, f32[32,4,1024]{2,0,1:T(8,128)}, u32[]{:S(2)}, u32[]{:S(2)}) collective-permute-start(f32[32,4,1024]{2,0,1:T(8,128)S(1)} %copy.118), channel_id=1, source_target_pairs={{0,1},{1,2},{2,3},{3,4},{4,5},{5,6},{6,7},{8,9},{9,10},{10,11},{11... | collective-permute-start | bytes 1572872 | tf_op jit(solution)/shard_map/ppermute | solution.py:15
Sparse Core Ops, SparseCore 0:
  285.7 112.6 all-gather.1

commit v5 on v4

--- a/solution.py
+++ b/solution.py
@@ -1,10 +1,98 @@
 import jax
 import jax.numpy as jnp
 from jax import lax
+from jax.experimental import pallas as pl
+from jax.experimental.pallas import tpu as pltpu
 from jax.sharding import PartitionSpec as P
+
+HW = 4
+
+
+def _zx_kernel(taps_ref, main_ref, low_ref, high_ref, out_ref, ext_ref):
+    nx = main_ref.shape[0]
+    ext_ref[0:HW] = low_ref[...]
+    ext_ref[HW:HW + nx] = main_ref[...]
+    ext_ref[HW + nx:] = high_ref[...]
+    depth = ext_ref.shape[2]
+    x = ext_ref[...]
+    lane = lax.broadcasted_iota(jnp.int32, x.shape, 2)
+    acc = taps_ref[HW] * x
+    for j in range(2 * HW + 1):
+        if j == HW:
+            continue
+        shifted = pltpu.roll(x, (HW - j) % depth, 2)
+        source = lane + (j - HW)
+        keep = (source >= 0) & (source < depth)
+        acc = acc + taps_ref[j] * jnp.where(keep, shifted, 0.0)
+    ext_ref[...] = acc
+    out = taps_ref[0] * ext_ref[0:nx]
+    for j in range(1, 2 * HW + 1):
+        out = out + taps_ref[j] * ext_ref[j:j + nx]
+    out_ref[...] = out
+
+
+def smooth_zx(raw, low, high, taps, ty=8):
+    nx, ny, nz = raw.shape
+    grid = (ny // ty,)
+    return pl.pallas_call(
+        _zx_kernel,
+        grid=grid,
+        in_specs=[
+            pl.BlockSpec(memory_space=pltpu.SMEM),
+            pl.BlockSpec((nx, ty, nz), lambda i: (0, i, 0)),
+            pl.BlockSpec((HW, ty, nz), lambda i: (0, i, 0)),
+            pl.BlockSpec((HW, ty, nz), lambda i: (0, i, 0)),
+        ],
+        out_specs=pl.BlockSpec((nx, ty, nz), lambda i: (0, i, 0)),
+        out_shape=jax.ShapeDtypeStruct(raw.shape, jnp.float32),
+        scratch_shapes=[pltpu.VMEM((nx + 2 * HW, ty, nz), jnp.float32)],
+        cost_estimate=pl.CostEstimate(flops=40 * raw.size, transcendentals=0, bytes_accessed=int(raw.size * 8 * 1.25)),
+    )(taps, raw, low, high)
+
+
+def _y_kernel(taps_ref, main_ref, low_ref, high_ref, out_ref, ext_ref):
+    ny = main_ref.shape[1]
+    ext_ref[:, HW:2 * HW] = low_ref[...]
+    ext_ref[:, 2 * HW:2 * HW + ny] = main_ref[...]
+    ext_ref[:, 2 * HW + ny:3 * HW + ny] = high_ref[...]
+    out = taps_ref[0] * ext_ref[:, pl.ds(HW, ny)]
+    for j in range(1, 2 * HW + 1):
+        out = out + taps_ref[j] * ext_ref[:, pl.ds(HW + j, ny)]
+    out_ref[...] = out
+
+
+def smooth_y(field, low, high, taps, tx=4):
+    nx, ny, nz = field.shape
+    grid = (nx // tx,)
+    return pl.pallas_call(
+        _y_kernel,
+        grid=grid,
+        in_specs=[
+            pl.BlockSpec(memory_space=pltpu.SMEM),
+            pl.BlockSpec((tx, ny, nz), lambda i: (i, 0, 0)),
+            pl.BlockSpec((tx, HW, nz), lambda i: (i, 0, 0)),
+            pl.BlockSpec((tx, HW, nz), lambda i: (i, 0, 0)),
+        ],
+        out_specs=pl.BlockSpec((tx, ny, nz), lambda i: (i, 0, 0)),
+        out_shape=jax.ShapeDtypeStruct(field.shape, jnp.float32),
+        scratch_shapes=[pltpu.VMEM((tx, ny + 4 * HW, nz), jnp.float32)],
+        cost_estimate=pl.CostEstimate(flops=18 * field.size, transcendentals=0, bytes_accessed=int(field.size * 8 * 1.1)),
+    )(taps, field, low, high)
+
 
 CHUNK = 128
 HALO = 64
+
+
+def halos(block, axis, dim, width):
+    count = lax.axis_size(axis)
+    forward = [(i, i + 1) for i in range(count - 1)]
+    backward = [(target, source) for source, target in forward]
+    low = lax.ppermute(
+        lax.slice_in_dim(block, block.shape[dim] - width, None, axis=dim), axis, forward
+    )
+    high = lax.ppermute(lax.slice_in_dim(block, 0, width, axis=dim), axis, backward)
+    return low, high
 
 
 def extended(block, sides, width):
@@ -163,12 +251,10 @@
         .add(per_trace, mode="drop")
     )
     raw_gradient = raw_gradient.reshape(rows_x, rows_y, depth_len)
-    depth_padded = jnp.pad(raw_gradient, ((0, 0), (0, 0), (4, 4)))
-    smooth_z = filter_padded(depth_padded, taps, 2)
-    inline_wide = extended(smooth_z, (("inline", 0),), 4)
-    smooth_x = filter_padded(inline_wide, taps, 0)
-    xline_wide = extended(smooth_x, (("xline", 1),), 4)
-    gradient = filter_padded(xline_wide, taps, 1)
+    raw_low, raw_high = halos(raw_gradient, "inline", 0, HW)
+    smooth_x = smooth_zx(raw_gradient, raw_low, raw_high, taps)
+    x_low, x_high = halos(smooth_x, "xline", 1, HW)
+    gradient = smooth_y(smooth_x, x_low, x_high, taps)
     return (gradient, residual)
 
 

time: 632 us -> 552 us (0.87)
  other arithmetic: 248 us -> 122 us
  Pallas kernels: 0 us -> 51.8 us
  local copies, waits for them, and re-layouts: 80.2 us -> 69.5 us
  waiting for transfers between devices: 163 us -> 170 us
    add x3 -> x0, other arithmetic: 124 us -> none  [filter_padded(): result + taps[offset] * lax.slice_in_dim(padded, offset, offset + length,...]
    pallas_call x0 -> x2, Pallas kernels: none -> 51.8 us  [the longest x1 31.2 us: smooth_zx(): pl.pallas_call(_zx_kernel, grid=grid, in_specs=[pl.BlockSpec(memory_space...]
  transfers between devices with their start and end apart: 7 -> 7, of which waited for: 6 -> 6; matrix products, arithmetic and copies ran while one was open for 19% -> 20% of each run, Pallas kernels for 0% -> 0%
where the time goes in v5:
time: 552 us; the launch traced here: 544 us
  waiting for transfers between devices  170 us (31%)
  other arithmetic  122 us (22%)
  local copies, waits for them, and re-layouts  69.5 us (13%)
  blocking collectives  58.9 us (11%)
  Pallas kernels  51.8 us (9%)
  matrix products  32.6 us (6%)
  starting transfers between devices  23.8 us (4%)
  between operations  15 us (3%)
    all_to_all x1, waiting for transfers between devices, traverse(): lax.all_to_all(blocks, ('inline', 'xline'), split_axis=0, concat_axis=0,...  104 us
    convert_element_type x7, other arithmetic, split(): return (high.astype(jnp.bfloat16), (x - high).astype(jnp.bfloat16))  83.6 us
    all_gather x1, blocking collectives, local(): tables_all = jnp.round(lax.all_gather(tables, axes, axis=0, tiled=True))  58.9 us
    all_gather x1, waiting for transfers between devices, local(): adjoint_all = lax.all_gather(adjoint, axes, axis=0, tiled=True)  43.6 us
    pallas_call x1, Pallas kernels, smooth_zx(): pl.pallas_call(_zx_kernel, grid=grid, in_specs=[pl.BlockSpec(memory_space...  31.2 us
    scatter-add x1, other arithmetic, local(): raw_gradient = jnp.zeros((cell_count, depth_len), jnp.float32).at[cells.r...  22.9 us
    gather x1, local copies, waits for them, and re-layouts, local(): predicted = jnp.take(tile_table.astype(jnp.bfloat16), cell_recv, axis=0)  20.8 us
    pallas_call x1, Pallas kernels, smooth_y(): pl.pallas_call(_y_kernel, grid=grid, in_specs=[pl.BlockSpec(memory_space=...  20.6 us
  transfers between devices with their start and end apart: 7, of which 6 were waited for; matrix products, arithmetic and copies ran while one was open for 20% of the time, Pallas kernels for 0%

profile of v5, /device:TPU:1, one launch (start us, length us, event | category | flops | bytes accessed | tf_op | source)
XLA Modules:
  0.0 543.7 jit_solution(10002376639452530146)
XLA Ops:
  11.0 7.1 %all-to-all-start = ((s32[32,1,64]{2,1,0:T(1,128)}), s32[32,1,64]{2,1,0:T(1,128)S(1)}, u32[]{:S(2)}, u32[]{:S(2)}) async-start(s32[32,1,64]{2,1,0:T(1,128)} %bitcast.12), calls=%async_computation | async-start | bytes 32768 | tf_op jit(solution)/shard_map/all_to_all | solution.py:194
  18.1 14.0 %convolution_convert_fusion = bf16[2048,2048]{1,0:T(8,128)(2,1)} fusion(bf16[2048,1024]{1,0:T(8,128)(2,1)} %bitcast.125, bf16[1,1,2048,1024]{3,2,1,0:T(8,128)(2,1)} %param.8), kind=kOutput, calls=%fused_computation.14 | convolution fusion | flops 8594128896 | bytes 16777216 | tf_op jit(solution)/shard_map/dot_general | solution.py:205
  33.4 20.8 %gather_fusion.1 = bf16[2048,2048]{1,0:T(8,128)(2,1)} fusion(bf16[2048,2048]{1,0:T(8,128)(2,1)} %convolution_convert_fusion, s32[2048]{0:T(1024)S(1)} %broadcast_clamp_fusion), kind=kCustom, calls=%fused_computation.1 | custom fusion | bytes 16785408 | tf_op jit(solution)/shard_map/jit(_take)/gather | solution.py:208
  54.2 7.6 %broadcast_select_fusion = bf16[32,64,2048]{2,1,0:T(8,128)(2,1)} fusion(bf16[32,64,2048]{2,1,0:T(8,128)(2,1)} %bitcast.104, pred[32,64]{1,0:T(8,128)(4,1)S(1)} %compare_and_fusion), kind=kLoop, calls=%fused_computation.13 | loop fusion | flops 4194304 | bytes 16779264 | tf_op jit(solution)/shard_map/jit(_take)/select_n | solution.py:208
  61.8 5.9 %all-to-all-start.1 = ((bf16[32,64,2048]{2,1,0:T(8,128)(2,1)}), bf16[32,64,2048]{2,1,0:T(8,128)(2,1)}, u32[]{:S(2)}, u32[]{:S(2)}) async-start(bf16[32,64,2048]{2,1,0:T(8,128)(2,1)} %broadcast_select_fusion), calls=%async_computation.1 | async-start | bytes 16777216 | tf_op jit(solution)/shard_map/all_to_all | solution.py:161
  69.5 20.5 %fusion.13 = bf16[256,128]{1,0:T(8,128)(2,1)S(1)} fusion(f32[]{:T(128)} %bitcast.23, f32[]{:T(128)} %bitcast.24, f32[]{:T(128)} %bitcast.25, f32[]{:T(128)} %bitcast.26, f32[]{:T(128)} %bitcast.27, f32[]{:T(128)} %bitcast.28, f32[]{:T(128)} %bitcast.29, f32[]{:T(128)} %bitcast.30, f32[]{:T(128)} %bitcast.31, f32[]{:T(128)} %bitcast.32, f32[]{:T(128)} %bitcast.33, ...), kind=kLoop, calls=%fused_computation.41 | loop fusion | flops 2326528 | bytes 65668 | tf_op jit(solution)/shard_map/convert_element_type | solution.py:123
  90.0 20.5 %reduce-precision_convert_fusion.2 = bf16[256,128]{1,0:T(8,128)(2,1)S(1)} fusion(f32[]{:T(128)} %bitcast.23, f32[]{:T(128)} %bitcast.24, f32[]{:T(128)} %bitcast.25, f32[]{:T(128)} %bitcast.26, f32[]{:T(128)} %bitcast.27, f32[]{:T(128)} %bitcast.28, f32[]{:T(128)} %bitcast.29, f32[]{:T(128)} %bitcast.30, f32[]{:T(128)} %bitcast.31, f32[]{:T(128)} %bitcast.32, ...), kind=kLoop, calls=%fused_computation.37 | loop fusion | flops 2293760 | bytes 65668 | tf_op jit(solution)/shard_map/convert_element_type | solution.py:123
  110.6 20.5 %fusion.12 = bf16[256,128]{1,0:T(8,128)(2,1)S(1)} fusion(f32[]{:T(128)} %bitcast.55, f32[]{:T(128)} %bitcast.54, f32[]{:T(128)} %bitcast.53, f32[]{:T(128)} %bitcast.52, f32[]{:T(128)} %bitcast.51, f32[]{:T(128)} %bitcast.50, f32[]{:T(128)} %bitcast.49, f32[]{:T(128)} %bitcast.48, f32[]{:T(128)} %bitcast.47, f32[]{:T(128)} %bitcast.46, f32[]{:T(128)} %bitcast.45, ...), kind=kLoop, calls=%fused_computation.40 | loop fusion | flops 2326528 | bytes 65668 | tf_op jit(solution)/shard_map/convert_element_type | solution.py:123
  131.1 20.5 %reduce-precision_convert_fusion.3 = bf16[256,128]{1,0:T(8,128)(2,1)S(1)} fusion(f32[]{:T(128)} %bitcast.55, f32[]{:T(128)} %bitcast.54, f32[]{:T(128)} %bitcast.53, f32[]{:T(128)} %bitcast.52, f32[]{:T(128)} %bitcast.51, f32[]{:T(128)} %bitcast.50, f32[]{:T(128)} %bitcast.49, f32[]{:T(128)} %bitcast.48, f32[]{:T(128)} %bitcast.47, f32[]{:T(128)} %bitcast.46, ...), kind=kLoop, calls=%fused_computation.39 | loop fusion | flops 2293760 | bytes 65668 | tf_op jit(solution)/shard_map/convert_element_type | solution.py:123
  152.7 104.2 %all-to-all-done.1 = bf16[32,64,2048]{2,1,0:T(8,128)(2,1)} async-done(((bf16[32,64,2048]{2,1,0:T(8,128)(2,1)}), bf16[32,64,2048]{2,1,0:T(8,128)(2,1)}, u32[]{:S(2)}, u32[]{:S(2)}) %all-to-all-start.1) | async-done | bytes 8388640 | tf_op jit(solution)/shard_map/all_to_all | solution.py:161
  256.9 6.2 %gather_fusion.2 = bf16[128,8,2048]{2,1,0:T(8,128)(2,1)} fusion(bf16[256,8,2048]{2,1,0:T(8,128)(2,1)} %bitcast.18, s32[1024]{0:T(1024)S(1)} %pad_clamp_fusion), kind=kCustom, calls=%fused_computation.2 | custom fusion | bytes 8389120 | tf_op jit(solution)/shard_map/jit(_take)/gather | solution.py:211
  263.1 3.5 convert_reduce_fusion
  280.2 58.9 %all_gather.6 = f32[512,72]{1,0:T(8,128)S(1)} all-gather(f32[16,72]{1,0:T(8,128)S(1)} %add_convert_fusion), channel_id=1, replica_groups=mesh['inline'=4,'xline'=8] {'inline','xline'}, dimensions={0}, use_global_device_ids=true | all-gather | bytes 152064 | tf_op jit(solution)/shard_map/all_gather | solution.py:178
  349.1 43.6 %all-gather.2.cloned.1.call-done = bf16[4096,2048]{1,0:T(8,128)(2,1)} async-done(((bf16[128,2048]{1,0:T(8,128)(2,1)}), bf16[4096,2048]{1,0:T(8,128)(2,1)}) %all-gather.2.cloned.1.call-update) | async-done | bytes 16777232 | tf_op jit(solution)/shard_map/all_gather | solution.py:220
  392.7 14.4 %gather_fusion.3 = bf16[256,8,2048]{2,1,0:T(8,128)(2,1)} fusion(bf16[512,8,2048]{2,1,0:T(8,128)(2,1)} %bitcast.114, s32[1024]{0:T(1024)S(1)} %pad_clamp_fusion.1), kind=kCustom, calls=%fused_computation.3 | custom fusion | bytes 16778240 | tf_op jit(solution)/shard_map/jit(_take)/gather | solution.py:242
  407.1 14.8 %fusion = f32[2048,1024]{1,0:T(8,128)} fusion(bf16[256,8,2048]{2,1,0:T(8,128)(2,1)} %gather_fusion.3, pred[256]{0:T(512)(128)(4,1)S(1)} %compare_and_fusion.3, bf16[1,1,2048,1024]{3,2,1,0:T(8,128)(2,1)} %param.8), kind=kOutput, calls=%fused_computation.8 | convolution fusion | flops 8594128896 | bytes 20971776 | tf_op jit(solution)/shard_map/dot_general | solution.py:243
  421.9 22.9 %scatter_custom_fusion.2 = f32[2048,1024]{1,0:T(8,128)} fusion(s32[2048]{0:T(1024)S(1)} %bitcast.121, f32[2048,1024]{1,0:T(8,128)} %fusion, f32[]{:T(128)} %constant.48.clone.1), kind=kCustom, calls=%fused_computation.18 | custom fusion | flops 2097152 | bytes 8389120 | tf_op jit(solution)/shard_map/scatter-add | solution.py:251
  451.8 9.5 %collective-permute-done.low_ref = f32[4,64,1024]{2,1,0:T(8,128)S(1)} collective-permute-done((f32[4,64,1024]{2,1,0:T(8,128)S(1)}, f32[4,64,1024]{2,1,0:T(8,128)S(1)}, u32[]{:S(2)}, u32[]{:S(2)}) %collective-permute-start) | collective-permute-done | bytes 1048608 | tf_op jit(solution)/shard_map/ppermute | solution.py:91
  461.3 4.4 collective-permute-done.1.high_ref
  466.8 31.2 %shard_map.86.main_ref = f32[32,64,1024]{2,1,0:T(8,128)} custom-call(f32[9]{0:T(128)} %taps_ref.3, f32[32,64,1024]{2,1,0:T(8,128)} %bitcast.102, f32[4,64,1024]{2,1,0:T(8,128)} %copy-done, f32[4,64,1024]{2,1,0:T(8,128)} %copy-done.1), custom_call_target="tpu_custom_call" | custom-call | flops 83886080 | bytes 20971520 | tf_op jit(solution)/shard_map/pallas_call | solution.py:37
  501.1 4.0 collective-permute-start.2
  506.4 3.3 collective-permute-done.3.high_ref
  509.7 5.2 collective-permute-done.2.low_ref
  515.8 20.6 %shard_map.87 = f32[32,64,1024]{2,1,0:T(8,128)} custom-call(f32[9]{0:T(128)} %taps_ref.3, f32[32,64,1024]{2,1,0:T(8,128)} %shard_map.86.main_ref, f32[32,4,1024]{2,1,0:T(4,128)} %copy-done.4, f32[32,4,1024]{2,1,0:T(4,128)} %copy-done.3), custom_call_target="tpu_custom_call" | custom-call | flops 37748736 | bytes 18454936 | tf_op jit(solution)/shard_map/pallas_call | solution.py:67
  (110 shorter events, 44.3 us)
Async XLA Ops:
  11.0 21.1 %all-to-all-start = ((s32[32,1,64]{2,1,0:T(1,128)}), s32[32,1,64]{2,1,0:T(1,128)S(1)}, u32[]{:S(2)}, u32[]{:S(2)}) async-start(s32[32,1,64]{2,1,0:T(1,128)} %bitcast.12), calls=%async_computation | async-start | bytes 32768 | tf_op jit(solution)/shard_map/all_to_all | solution.py:194
  61.8 6.2 %copy-start.2 = (f32[33]{0:T(128)S(1)}, f32[33]{0:T(128)}, u32[]{:S(2)}) copy-start(f32[33]{0:T(128)} %param.10) | copy-start | bytes 400
  61.8 89.8 %copy-start.5 = (bf16[128,2048]{1,0:T(8,128)(2,1)S(1)}, bf16[128,2048]{1,0:T(8,128)(2,1)}, u32[]{:S(2)}) copy-start(bf16[128,2048]{1,0:T(8,128)(2,1)} %param.9) | copy-start | bytes 1572868
  61.8 195.0 %all-to-all-start.1 = ((bf16[32,64,2048]{2,1,0:T(8,128)(2,1)}), bf16[32,64,2048]{2,1,0:T(8,128)(2,1)}, u32[]{:S(2)}, u32[]{:S(2)}) async-start(bf16[32,64,2048]{2,1,0:T(8,128)(2,1)} %broadcast_select_fusion), calls=%async_computation.1 | async-start | bytes 16777216 | tf_op jit(solution)/shard_map/all_to_all | solution.py:161
  67.7 324.9 %all-gather.2.cloned.1.call-start = ((), (), s32[]{:S(2)}) async-start(), calls=%async_computation.2 | async-start | bytes 17301504 | tf_op jit(solution)/shard_map/all_gather | solution.py:220
  275.1 4.9 copy-start.6
  446.5 14.9 %collective-permute-start = (f32[4,64,1024]{2,1,0:T(8,128)S(1)}, f32[4,64,1024]{2,1,0:T(8,128)S(1)}, u32[]{:S(2)}, u32[]{:S(2)}) collective-permute-start(f32[4,64,1024]{2,1,0:T(8,128)S(1)} %bitcast.117), channel_id=1, source_target_pairs={{0,8},{8,16},{16,24},{1,9},{9,17},{17,25},{2,10},{10,18},{18,26},{... | collective-permute-start | bytes 3145736 | tf_op jit(solution)/shard_map/ppermute | solution.py:91
  449.6 16.1 %collective-permute-start.1 = (f32[4,64,1024]{2,1,0:T(8,128)S(1)}, f32[4,64,1024]{2,1,0:T(8,128)S(1)}, u32[]{:S(2)}, u32[]{:S(2)}) collective-permute-start(f32[4,64,1024]{2,1,0:T(8,128)S(1)} %bitcast.116), channel_id=1, source_target_pairs={{8,0},{16,8},{24,16},{9,1},{17,9},{25,17},{10,2},{18,10},{26,18},{... | collective-permute-start | bytes 3145736 | tf_op jit(solution)/shard_map/ppermute | solution.py:94
  461.3 4.4 copy-start
  465.7 1.1 copy-start.1
  499.8 9.9 %collective-permute-start.3 = (f32[32,4,1024]{2,1,0:T(4,128)S(1)}, f32[32,4,1024]{2,1,0:T(4,128)S(1)}, u32[]{:S(2)}, u32[]{:S(2)}) collective-permute-start(f32[32,4,1024]{2,1,0:T(4,128)S(1)} %get-tuple-element.26), channel_id=1, source_target_pairs={{1,0},{2,1},{3,2},{4,3},{5,4},{6,5},{7,6},{9,8},{10,9},{11,10},{12... | collective-permute-start | bytes 1572872 | tf_op jit(solution)/shard_map/ppermute | solution.py:94
  501.1 13.9 %collective-permute-start.2 = (f32[32,4,1024]{2,1,0:T(4,128)S(1)}, f32[32,4,1024]{2,1,0:T(4,128)S(1)}, u32[]{:S(2)}, u32[]{:S(2)}) collective-permute-start(f32[32,4,1024]{2,1,0:T(4,128)S(1)} %get-tuple-element.27), channel_id=1, source_target_pairs={{0,1},{1,2},{2,3},{3,4},{4,5},{5,6},{6,7},{8,9},{9,10},{10,11},{11... | collective-permute-start | bytes 1572872 | tf_op jit(solution)/shard_map/ppermute | solution.py:91
  509.7 5.2 copy-start.3
  515.0 0.8 copy-start.4
Sparse Core Ops, SparseCore 0:
  280.1 112.5 all-gather.1

commit v6 on v5

--- a/solution.py
+++ b/solution.py
@@ -31,29 +31,34 @@
     out_ref[...] = out
 
 
-def smooth_zx(raw, low, high, taps, ty=8):
+def smooth_zx(raw, low, high, taps, blocks, ty=8):
     nx, ny, nz = raw.shape
-    grid = (ny // ty,)
     return pl.pallas_call(
         _zx_kernel,
-        grid=grid,
+        grid=(len(blocks),),
         in_specs=[
             pl.BlockSpec(memory_space=pltpu.SMEM),
-            pl.BlockSpec((nx, ty, nz), lambda i: (0, i, 0)),
-            pl.BlockSpec((HW, ty, nz), lambda i: (0, i, 0)),
-            pl.BlockSpec((HW, ty, nz), lambda i: (0, i, 0)),
+            pl.BlockSpec((nx, ty, nz), lambda i: (0, blocks[0] + i * (blocks[-1] - blocks[0]) // max(1, len(blocks) - 1), 0)),
+            pl.BlockSpec((HW, ty, nz), lambda i: (0, blocks[0] + i * (blocks[-1] - blocks[0]) // max(1, len(blocks) - 1), 0)),
+            pl.BlockSpec((HW, ty, nz), lambda i: (0, blocks[0] + i * (blocks[-1] - blocks[0]) // max(1, len(blocks) - 1), 0)),
         ],
         out_specs=pl.BlockSpec((nx, ty, nz), lambda i: (0, i, 0)),
-        out_shape=jax.ShapeDtypeStruct(raw.shape, jnp.float32),
+        out_shape=jax.ShapeDtypeStruct((nx, ty * len(blocks), nz), jnp.float32),
         scratch_shapes=[pltpu.VMEM((nx + 2 * HW, ty, nz), jnp.float32)],
-        cost_estimate=pl.CostEstimate(flops=40 * raw.size, transcendentals=0, bytes_accessed=int(raw.size * 8 * 1.25)),
+        cost_estimate=pl.CostEstimate(
+            flops=40 * nx * ty * nz * len(blocks), transcendentals=0,
+            bytes_accessed=int(nx * ty * nz * len(blocks) * 10),
+        ),
     )(taps, raw, low, high)
 
 
-def _y_kernel(taps_ref, main_ref, low_ref, high_ref, out_ref, ext_ref):
-    ny = main_ref.shape[1]
+def _y_kernel(taps_ref, first_ref, middle_ref, last_ref, low_ref, high_ref, out_ref, ext_ref):
+    edge = first_ref.shape[1]
+    ny = middle_ref.shape[1] + 2 * edge
     ext_ref[:, HW:2 * HW] = low_ref[...]
-    ext_ref[:, 2 * HW:2 * HW + ny] = main_ref[...]
+    ext_ref[:, 2 * HW:2 * HW + edge] = first_ref[...]
+    ext_ref[:, 2 * HW + edge:2 * HW + ny - edge] = middle_ref[...]
+    ext_ref[:, 2 * HW + ny - edge:2 * HW + ny] = last_ref[...]
     ext_ref[:, 2 * HW + ny:3 * HW + ny] = high_ref[...]
     out = taps_ref[0] * ext_ref[:, pl.ds(HW, ny)]
     for j in range(1, 2 * HW + 1):
@@ -61,23 +66,28 @@
     out_ref[...] = out
 
 
-def smooth_y(field, low, high, taps, tx=4):
-    nx, ny, nz = field.shape
-    grid = (nx // tx,)
+def smooth_y(edges, middle, low, high, taps, tx=4):
+    nx, two_edge, nz = edges.shape
+    edge = two_edge // 2
+    ny = middle.shape[1] + two_edge
     return pl.pallas_call(
         _y_kernel,
-        grid=grid,
+        grid=(nx // tx,),
         in_specs=[
             pl.BlockSpec(memory_space=pltpu.SMEM),
-            pl.BlockSpec((tx, ny, nz), lambda i: (i, 0, 0)),
+            pl.BlockSpec((tx, edge, nz), lambda i: (i, 0, 0)),
+            pl.BlockSpec((tx, ny - 2 * edge, nz), lambda i: (i, 0, 0)),
+            pl.BlockSpec((tx, edge, nz), lambda i: (i, 1, 0)),
             pl.BlockSpec((tx, HW, nz), lambda i: (i, 0, 0)),
             pl.BlockSpec((tx, HW, nz), lambda i: (i, 0, 0)),
         ],
         out_specs=pl.BlockSpec((tx, ny, nz), lambda i: (i, 0, 0)),
-        out_shape=jax.ShapeDtypeStruct(field.shape, jnp.float32),
+        out_shape=jax.ShapeDtypeStruct((nx, ny, nz), jnp.float32),
         scratch_shapes=[pltpu.VMEM((tx, ny + 4 * HW, nz), jnp.float32)],
-        cost_estimate=pl.CostEstimate(flops=18 * field.size, transcendentals=0, bytes_accessed=int(field.size * 8 * 1.1)),
-    )(taps, field, low, high)
+        cost_estimate=pl.CostEstimate(
+            flops=18 * nx * ny * nz, transcendentals=0, bytes_accessed=int(nx * ny * nz * 8.8)
+        ),
+    )(taps, edges, middle, edges, low, high)
 
 
 CHUNK = 128
@@ -252,9 +262,11 @@
     )
     raw_gradient = raw_gradient.reshape(rows_x, rows_y, depth_len)
     raw_low, raw_high = halos(raw_gradient, "inline", 0, HW)
-    smooth_x = smooth_zx(raw_gradient, raw_low, raw_high, taps)
-    x_low, x_high = halos(smooth_x, "xline", 1, HW)
-    gradient = smooth_y(smooth_x, x_low, x_high, taps)
+    y_blocks = rows_y // 8
+    edges = smooth_zx(raw_gradient, raw_low, raw_high, taps, (0, y_blocks - 1))
+    x_low, x_high = halos(edges, "xline", 1, HW)
+    middle = smooth_zx(raw_gradient, raw_low, raw_high, taps, tuple(range(1, y_blocks - 1)))
+    gradient = smooth_y(edges, middle, x_low, x_high, taps)
     return (gradient, residual)
 
 

time: 552 us -> 546 us (0.989)
  waiting for transfers between devices: 170 us -> 162 us
    pallas_call x2 -> x3, Pallas kernels: 51.8 us -> 54 us  [the longest x2 33.6 us: smooth_zx(): pl.pallas_call(_zx_kernel, grid=(len(blocks),), in_specs=[pl.BlockSpec(me...]
  transfers between devices with their start and end apart: 7 -> 7, of which waited for: 6 -> 4; matrix products, arithmetic and copies ran while one was open for 20% -> 20% of each run, Pallas kernels for 0% -> 4%
where the time goes in v6:
time: 546 us; the launch traced here: 538 us
  waiting for transfers between devices  162 us (30%)
  other arithmetic  122 us (22%)
  local copies, waits for them, and re-layouts  70.4 us (13%)
  blocking collectives  58.9 us (11%)
  Pallas kernels  54 us (10%)
  matrix products  32.6 us (6%)
  starting transfers between devices  23.6 us (4%)
  between operations  15 us (3%)
    all_to_all x1, waiting for transfers between devices, traverse(): lax.all_to_all(blocks, ('inline', 'xline'), split_axis=0, concat_axis=0,...  104 us
    convert_element_type x7, other arithmetic, split(): return (high.astype(jnp.bfloat16), (x - high).astype(jnp.bfloat16))  83.6 us
    all_gather x1, blocking collectives, local(): tables_all = jnp.round(lax.all_gather(tables, axes, axis=0, tiled=True))  58.9 us
    all_gather x1, waiting for transfers between devices, local(): adjoint_all = lax.all_gather(adjoint, axes, axis=0, tiled=True)  43.6 us
    pallas_call x2, Pallas kernels, smooth_zx(): pl.pallas_call(_zx_kernel, grid=(len(blocks),), in_specs=[pl.BlockSpec(me...  33.6 us
    scatter-add x1, other arithmetic, local(): raw_gradient = jnp.zeros((cell_count, depth_len), jnp.float32).at[cells.r...  22.9 us
    gather x1, local copies, waits for them, and re-layouts, local(): predicted = jnp.take(tile_table.astype(jnp.bfloat16), cell_recv, axis=0)  20.8 us
    pallas_call x1, Pallas kernels, smooth_y(): pl.pallas_call(_y_kernel, grid=(nx // tx,), in_specs=[pl.BlockSpec(memory...  20.4 us
  transfers between devices with their start and end apart: 7, of which 4 were waited for; matrix products, arithmetic and copies ran while one was open for 20% of the time, Pallas kernels for 4%

profile of v6, /device:TPU:1, one launch (start us, length us, event | category | flops | bytes accessed | tf_op | source)
XLA Modules:
  0.0 538.0 jit_solution(18389969484147745932)
XLA Ops:
  11.0 7.1 %all-to-all-start = ((s32[32,1,64]{2,1,0:T(1,128)}), s32[32,1,64]{2,1,0:T(1,128)S(1)}, u32[]{:S(2)}, u32[]{:S(2)}) async-start(s32[32,1,64]{2,1,0:T(1,128)} %bitcast.12), calls=%async_computation | async-start | bytes 32768 | tf_op jit(solution)/shard_map/all_to_all | solution.py:204
  18.1 14.0 %convolution_convert_fusion = bf16[2048,2048]{1,0:T(8,128)(2,1)} fusion(bf16[2048,1024]{1,0:T(8,128)(2,1)} %bitcast.126, bf16[1,1,2048,1024]{3,2,1,0:T(8,128)(2,1)} %param.8), kind=kOutput, calls=%fused_computation.14 | convolution fusion | flops 8594128896 | bytes 16777216 | tf_op jit(solution)/shard_map/dot_general | solution.py:215
  33.4 20.8 %gather_fusion.1 = bf16[2048,2048]{1,0:T(8,128)(2,1)} fusion(bf16[2048,2048]{1,0:T(8,128)(2,1)} %convolution_convert_fusion, s32[2048]{0:T(1024)S(1)} %broadcast_clamp_fusion), kind=kCustom, calls=%fused_computation.1 | custom fusion | bytes 16785408 | tf_op jit(solution)/shard_map/jit(_take)/gather | solution.py:218
  54.2 7.6 %broadcast_select_fusion = bf16[32,64,2048]{2,1,0:T(8,128)(2,1)} fusion(bf16[32,64,2048]{2,1,0:T(8,128)(2,1)} %bitcast.105, pred[32,64]{1,0:T(8,128)(4,1)S(1)} %compare_and_fusion), kind=kLoop, calls=%fused_computation.13 | loop fusion | flops 4194304 | bytes 16779264 | tf_op jit(solution)/shard_map/jit(_take)/select_n | solution.py:218
  61.8 5.9 %all-to-all-start.1 = ((bf16[32,64,2048]{2,1,0:T(8,128)(2,1)}), bf16[32,64,2048]{2,1,0:T(8,128)(2,1)}, u32[]{:S(2)}, u32[]{:S(2)}) async-start(bf16[32,64,2048]{2,1,0:T(8,128)(2,1)} %broadcast_select_fusion), calls=%async_computation.1 | async-start | bytes 16777216 | tf_op jit(solution)/shard_map/all_to_all | solution.py:171
  69.5 20.5 %fusion.13 = bf16[256,128]{1,0:T(8,128)(2,1)S(1)} fusion(f32[]{:T(128)} %bitcast.23, f32[]{:T(128)} %bitcast.24, f32[]{:T(128)} %bitcast.25, f32[]{:T(128)} %bitcast.26, f32[]{:T(128)} %bitcast.27, f32[]{:T(128)} %bitcast.28, f32[]{:T(128)} %bitcast.29, f32[]{:T(128)} %bitcast.30, f32[]{:T(128)} %bitcast.31, f32[]{:T(128)} %bitcast.32, f32[]{:T(128)} %bitcast.33, ...), kind=kLoop, calls=%fused_computation.41 | loop fusion | flops 2326528 | bytes 65668 | tf_op jit(solution)/shard_map/convert_element_type | solution.py:133
  90.0 20.5 %reduce-precision_convert_fusion.2 = bf16[256,128]{1,0:T(8,128)(2,1)S(1)} fusion(f32[]{:T(128)} %bitcast.23, f32[]{:T(128)} %bitcast.24, f32[]{:T(128)} %bitcast.25, f32[]{:T(128)} %bitcast.26, f32[]{:T(128)} %bitcast.27, f32[]{:T(128)} %bitcast.28, f32[]{:T(128)} %bitcast.29, f32[]{:T(128)} %bitcast.30, f32[]{:T(128)} %bitcast.31, f32[]{:T(128)} %bitcast.32, ...), kind=kLoop, calls=%fused_computation.37 | loop fusion | flops 2293760 | bytes 65668 | tf_op jit(solution)/shard_map/convert_element_type | solution.py:133
  110.6 20.5 %fusion.12 = bf16[256,128]{1,0:T(8,128)(2,1)S(1)} fusion(f32[]{:T(128)} %bitcast.55, f32[]{:T(128)} %bitcast.54, f32[]{:T(128)} %bitcast.53, f32[]{:T(128)} %bitcast.52, f32[]{:T(128)} %bitcast.51, f32[]{:T(128)} %bitcast.50, f32[]{:T(128)} %bitcast.49, f32[]{:T(128)} %bitcast.48, f32[]{:T(128)} %bitcast.47, f32[]{:T(128)} %bitcast.46, f32[]{:T(128)} %bitcast.45, ...), kind=kLoop, calls=%fused_computation.40 | loop fusion | flops 2326528 | bytes 65668 | tf_op jit(solution)/shard_map/convert_element_type | solution.py:133
  131.1 20.5 %reduce-precision_convert_fusion.3 = bf16[256,128]{1,0:T(8,128)(2,1)S(1)} fusion(f32[]{:T(128)} %bitcast.55, f32[]{:T(128)} %bitcast.54, f32[]{:T(128)} %bitcast.53, f32[]{:T(128)} %bitcast.52, f32[]{:T(128)} %bitcast.51, f32[]{:T(128)} %bitcast.50, f32[]{:T(128)} %bitcast.49, f32[]{:T(128)} %bitcast.48, f32[]{:T(128)} %bitcast.47, f32[]{:T(128)} %bitcast.46, ...), kind=kLoop, calls=%fused_computation.39 | loop fusion | flops 2293760 | bytes 65668 | tf_op jit(solution)/shard_map/convert_element_type | solution.py:133
  152.7 104.2 %all-to-all-done.1 = bf16[32,64,2048]{2,1,0:T(8,128)(2,1)} async-done(((bf16[32,64,2048]{2,1,0:T(8,128)(2,1)}), bf16[32,64,2048]{2,1,0:T(8,128)(2,1)}, u32[]{:S(2)}, u32[]{:S(2)}) %all-to-all-start.1) | async-done | bytes 8388640 | tf_op jit(solution)/shard_map/all_to_all | solution.py:171
  256.9 6.2 %gather_fusion.2 = bf16[128,8,2048]{2,1,0:T(8,128)(2,1)} fusion(bf16[256,8,2048]{2,1,0:T(8,128)(2,1)} %bitcast.18, s32[1024]{0:T(1024)S(1)} %pad_clamp_fusion), kind=kCustom, calls=%fused_computation.2 | custom fusion | bytes 8389120 | tf_op jit(solution)/shard_map/jit(_take)/gather | solution.py:221
  263.1 3.5 convert_reduce_fusion
  280.2 58.9 %all_gather.6 = f32[512,72]{1,0:T(8,128)S(1)} all-gather(f32[16,72]{1,0:T(8,128)S(1)} %add_convert_fusion), channel_id=1, replica_groups=mesh['inline'=4,'xline'=8] {'inline','xline'}, dimensions={0}, use_global_device_ids=true | all-gather | bytes 152064 | tf_op jit(solution)/shard_map/all_gather | solution.py:188
  349.1 43.6 %all-gather.2.cloned.1.call-done = bf16[4096,2048]{1,0:T(8,128)(2,1)} async-done(((bf16[128,2048]{1,0:T(8,128)(2,1)}), bf16[4096,2048]{1,0:T(8,128)(2,1)}) %all-gather.2.cloned.1.call-update) | async-done | bytes 16777232 | tf_op jit(solution)/shard_map/all_gather | solution.py:230
  392.7 14.5 %gather_fusion.3 = bf16[256,8,2048]{2,1,0:T(8,128)(2,1)} fusion(bf16[512,8,2048]{2,1,0:T(8,128)(2,1)} %bitcast.115, s32[1024]{0:T(1024)S(1)} %pad_clamp_fusion.1), kind=kCustom, calls=%fused_computation.3 | custom fusion | bytes 16778240 | tf_op jit(solution)/shard_map/jit(_take)/gather | solution.py:252
  407.2 14.8 %fusion = f32[2048,1024]{1,0:T(8,128)} fusion(bf16[256,8,2048]{2,1,0:T(8,128)(2,1)} %gather_fusion.3, pred[256]{0:T(512)(128)(4,1)S(1)} %compare_and_fusion.3, bf16[1,1,2048,1024]{3,2,1,0:T(8,128)(2,1)} %param.8), kind=kOutput, calls=%fused_computation.8 | convolution fusion | flops 8594128896 | bytes 20971776 | tf_op jit(solution)/shard_map/dot_general | solution.py:253
  422.0 22.9 %scatter_custom_fusion.2 = f32[2048,1024]{1,0:T(8,128)} fusion(s32[2048]{0:T(1024)S(1)} %bitcast.122, f32[2048,1024]{1,0:T(8,128)} %fusion, f32[]{:T(128)} %constant.48.clone.1), kind=kCustom, calls=%fused_computation.18 | custom fusion | flops 2097152 | bytes 8389120 | tf_op jit(solution)/shard_map/scatter-add | solution.py:261
  446.6 2.9 collective-permute-start
  451.6 9.5 %collective-permute-done.low_ref = f32[4,64,1024]{2,1,0:T(8,128)S(1)} collective-permute-done((f32[4,64,1024]{2,1,0:T(8,128)S(1)}, f32[4,64,1024]{2,1,0:T(8,128)S(1)}, u32[]{:S(2)}, u32[]{:S(2)}) %collective-permute-start) | collective-permute-done | bytes 1048608 | tf_op jit(solution)/shard_map/ppermute | solution.py:101
  461.2 4.4 collective-permute-done.1.high_ref
  466.5 9.5 %shard_map.86.first_ref.last_ref = f32[32,16,1024]{2,1,0:T(8,128)} custom-call(f32[9]{0:T(128)} %taps_ref.5, f32[32,64,1024]{2,1,0:T(8,128)} %bitcast.102, f32[4,64,1024]{2,1,0:T(8,128)} %copy-done, f32[4,64,1024]{2,1,0:T(8,128)} %copy-done.1), custom_call_target="tpu_custom_call" | custom-call | flops 20971520 | bytes 5242880 | tf_op jit(solution)/shard_map/pallas_call | solution.py:36
  479.1 4.0 collective-permute-start.2
  484.5 24.1 %shard_map.87.middle_ref = f32[32,48,1024]{2,1,0:T(8,128)} custom-call(f32[9]{0:T(128)} %taps_ref.5, f32[32,64,1024]{2,1,0:T(8,128)} %bitcast.103, f32[4,64,1024]{2,1,0:T(8,128)} %copy-done, f32[4,64,1024]{2,1,0:T(8,128)} %copy-done.1), custom_call_target="tpu_custom_call" | custom-call | flops 62914560 | bytes 15728640 | tf_op jit(solution)/shard_map/pallas_call | solution.py:36
  510.3 20.4 %shard_map.88 = f32[32,64,1024]{2,1,0:T(8,128)} custom-call(f32[9]{0:T(128)} %taps_ref.5, f32[32,16,1024]{2,1,0:T(8,128)} %shard_map.86.first_ref.last_ref, f32[32,48,1024]{2,1,0:T(8,128)} %shard_map.87.middle_ref, f32[32,16,1024]{2,1,0:T(8,128)} %shard_map.86.first_ref.last_ref, f32[32,4,1024]{2,1,0:T(4,128)} %copy-done.4, f32[32,4,1024]{2,1,0:T(4,128)} %copy-done.3), custom_call_target="tpu_custom_call" | custom-call | flops 37748736 | bytes 18454936 | tf_op jit(solution)/shard_map/pallas_call | solution.py:73
  (111 shorter events, 42.0 us)
Async XLA Ops:
  11.0 21.1 %all-to-all-start = ((s32[32,1,64]{2,1,0:T(1,128)}), s32[32,1,64]{2,1,0:T(1,128)S(1)}, u32[]{:S(2)}, u32[]{:S(2)}) async-start(s32[32,1,64]{2,1,0:T(1,128)} %bitcast.12), calls=%async_computation | async-start | bytes 32768 | tf_op jit(solution)/shard_map/all_to_all | solution.py:204
  61.8 6.2 %copy-start.2 = (f32[33]{0:T(128)S(1)}, f32[33]{0:T(128)}, u32[]{:S(2)}) copy-start(f32[33]{0:T(128)} %param.10) | copy-start | bytes 400
  61.8 89.8 %copy-start.5 = (bf16[128,2048]{1,0:T(8,128)(2,1)S(1)}, bf16[128,2048]{1,0:T(8,128)(2,1)}, u32[]{:S(2)}) copy-start(bf16[128,2048]{1,0:T(8,128)(2,1)} %param.9) | copy-start | bytes 1572868
  61.8 195.0 %all-to-all-start.1 = ((bf16[32,64,2048]{2,1,0:T(8,128)(2,1)}), bf16[32,64,2048]{2,1,0:T(8,128)(2,1)}, u32[]{:S(2)}, u32[]{:S(2)}) async-start(bf16[32,64,2048]{2,1,0:T(8,128)(2,1)} %broadcast_select_fusion), calls=%async_computation.1 | async-start | bytes 16777216 | tf_op jit(solution)/shard_map/all_to_all | solution.py:171
  67.7 324.9 %all-gather.2.cloned.1.call-start = ((), (), s32[]{:S(2)}) async-start(), calls=%async_computation.2 | async-start | bytes 17301504 | tf_op jit(solution)/shard_map/all_gather | solution.py:230
  275.1 4.9 copy-start.6
  446.6 14.6 %collective-permute-start = (f32[4,64,1024]{2,1,0:T(8,128)S(1)}, f32[4,64,1024]{2,1,0:T(8,128)S(1)}, u32[]{:S(2)}, u32[]{:S(2)}) collective-permute-start(f32[4,64,1024]{2,1,0:T(8,128)S(1)} %bitcast.118), channel_id=1, source_target_pairs={{0,8},{8,16},{16,24},{1,9},{9,17},{17,25},{2,10},{10,18},{18,26},{... | collective-permute-start | bytes 3145736 | tf_op jit(solution)/shard_map/ppermute | solution.py:101
  449.4 16.1 %collective-permute-start.1 = (f32[4,64,1024]{2,1,0:T(8,128)S(1)}, f32[4,64,1024]{2,1,0:T(8,128)S(1)}, u32[]{:S(2)}, u32[]{:S(2)}) collective-permute-start(f32[4,64,1024]{2,1,0:T(8,128)S(1)} %bitcast.117), channel_id=1, source_target_pairs={{8,0},{16,8},{24,16},{9,1},{17,9},{25,17},{10,2},{18,10},{26,18},{... | collective-permute-start | bytes 3145736 | tf_op jit(solution)/shard_map/ppermute | solution.py:104
  461.2 4.4 copy-start
  465.6 1.0 copy-start.1
  477.8 30.7 %collective-permute-start.3 = (f32[32,4,1024]{2,1,0:T(4,128)S(1)}, f32[32,4,1024]{2,1,0:T(4,128)S(1)}, u32[]{:S(2)}, u32[]{:S(2)}) collective-permute-start(f32[32,4,1024]{2,1,0:T(4,128)S(1)} %get-tuple-element.28), channel_id=1, source_target_pairs={{1,0},{2,1},{3,2},{4,3},{5,4},{6,5},{7,6},{9,8},{10,9},{11,10},{12... | collective-permute-start | bytes 1572872 | tf_op jit(solution)/shard_map/ppermute | solution.py:104
  479.1 29.4 %collective-permute-start.2 = (f32[32,4,1024]{2,1,0:T(4,128)S(1)}, f32[32,4,1024]{2,1,0:T(4,128)S(1)}, u32[]{:S(2)}, u32[]{:S(2)}) collective-permute-start(f32[32,4,1024]{2,1,0:T(4,128)S(1)} %get-tuple-element.29), channel_id=1, source_target_pairs={{0,1},{1,2},{2,3},{3,4},{4,5},{5,6},{6,7},{8,9},{9,10},{10,11},{11... | collective-permute-start | bytes 1572872 | tf_op jit(solution)/shard_map/ppermute | solution.py:101
  508.6 0.9 copy-start.3
  509.4 0.8 copy-start.4
Sparse Core Ops, SparseCore 0:
  280.1 112.5 all-gather.1

commit v7 on v6

--- a/solution.py
+++ b/solution.py
@@ -182,10 +182,6 @@
     cell_count = rows_x * rows_y
     capacity = 2 * max(1, block_count * aperture_len // device_count)
     item_count = block_count * aperture_len
-    tables = jnp.concatenate(
-        [aperture, landing.reshape(block_count, per_block * aperture_len)], axis=1
-    ).astype(jnp.float32)
-    tables_all = jnp.round(lax.all_gather(tables, axes, axis=0, tiled=True))
     target_tile = aperture.reshape(item_count)
     onehot = (target_tile[:, None] == jnp.arange(device_count, dtype=jnp.int32)[None, :]).astype(
         jnp.int32
@@ -227,10 +223,27 @@
     residual = modeled - observed.astype(jnp.float32)
     adjoint = banded(residual, band_block(wavelet, half)).astype(jnp.bfloat16)
 
-    adjoint_all = lax.all_gather(adjoint, axes, axis=0, tiled=True)
+    extra = 128
+    coded = jnp.concatenate(
+        [
+            jnp.repeat(aperture, per_block, axis=0),
+            landing // 64,
+            landing % 64,
+            jnp.zeros((trace_count, extra - 3 * aperture_len), jnp.int32),
+        ],
+        axis=1,
+    ).astype(jnp.bfloat16)
+    half_s = samples // 2
+    first_all = lax.all_gather(
+        jnp.concatenate([adjoint[:, :half_s], coded], axis=1), axes, axis=0, tiled=True
+    )
+    second_all = lax.all_gather(adjoint[:, half_s:], axes, axis=0, tiled=True)
     all_blocks = block_count * device_count
-    aperture_all = tables_all[:, :aperture_len].astype(jnp.int32)
-    landing_all = tables_all[:, aperture_len:].astype(jnp.int32).reshape(all_blocks * per_block, aperture_len)
+    codes = first_all[:, half_s:half_s + 3 * aperture_len].astype(jnp.int32)
+    aperture_all = codes.reshape(all_blocks, per_block, 3 * aperture_len)[:, 0, :aperture_len]
+    landing_all = (
+        codes[:, aperture_len:2 * aperture_len] * 64 + codes[:, 2 * aperture_len:3 * aperture_len]
+    )
     relevant = capacity * device_count
     hit = aperture_all == me
     has = jnp.any(hit, axis=1)
@@ -249,10 +262,18 @@
     cells = jnp.where(
         (jnp.arange(relevant) < found)[:, None], jnp.take(cells_all, chosen, axis=0), cell_count
     )
-    picked = jnp.take(adjoint_all.reshape(all_blocks, per_block, samples), chosen, axis=0)
+    picked_first = jnp.take(
+        first_all[:, :half_s].reshape(all_blocks, per_block, half_s), chosen, axis=0
+    )
     per_trace = jnp.dot(
-        picked.reshape(relevant * per_block, samples),
-        weight_matrix,
+        picked_first.reshape(relevant * per_block, half_s),
+        weight_matrix[:half_s],
+        preferred_element_type=jnp.float32,
+    )
+    picked_second = jnp.take(second_all.reshape(all_blocks, per_block, half_s), chosen, axis=0)
+    per_trace = per_trace + jnp.dot(
+        picked_second.reshape(relevant * per_block, half_s),
+        weight_matrix[half_s:],
         preferred_element_type=jnp.float32,
     )
     raw_gradient = (

time: 546 us -> 599 us (1.097)
  waiting for transfers between devices: 162 us -> 226 us
  blocking collectives: 58.9 us -> 0 us
  local copies, waits for them, and re-layouts: 70.4 us -> 97.8 us
  other arithmetic: 122 us -> 135 us
    all_gather x1 -> x2, waiting for transfers between devices: 43.6 us -> 108 us  [the longest x1 95.3 us: local(): lax.all_gather(jnp.concatenate([adjoint[:, :half_s], coded], axis=1), axe...]
    all_gather x1 -> x0, blocking collectives: 58.9 us -> none  [local(): tables_all = jnp.round(lax.all_gather(tables, axes, axis=0, tiled=True))]
    slice x1 -> x4, local copies, waits for them, and re-layouts: 0.07 us -> 20.5 us  [the longest x2 19.7 us: local(): first_all[:, :half_s].reshape(all_blocks, per_block, half_s)]
    reduce_or x1, other arithmetic: 0.02 us -> 10.9 us  [local(): has = jnp.any(hit, axis=1)]
    dot_general x1 -> x2, matrix products: 14.8 us -> 21.8 us  [the longest x1 11 us: local(): jnp.dot(picked_first.reshape(relevant * per_block, half_s), weight_matrix...]
    gather x1 -> x2, local copies, waits for them, and re-layouts: 14.5 us -> 13.5 us  [the longest x1 7.3 us: local(): jnp.take(first_all[:, :half_s].reshape(all_blocks, per_block, half_s), ch...]
  transfers between devices with their start and end apart: 7 -> 8, of which waited for: 4 -> 5; matrix products, arithmetic and copies ran while one was open for 20% -> 28% of each run, Pallas kernels for 4% -> 4%
where the time goes in v7:
time: 599 us; the launch traced here: 589 us
  waiting for transfers between devices  226 us (38%)
  other arithmetic  135 us (23%)
  local copies, waits for them, and re-layouts  97.8 us (16%)
  Pallas kernels  54.3 us (9%)
  matrix products  38.3 us (6%)
  starting transfers between devices  22.4 us (4%)
  between operations  15.1 us (3%)
    all_to_all x1, waiting for transfers between devices, traverse(): lax.all_to_all(blocks, ('inline', 'xline'), split_axis=0, concat_axis=0,...  104 us
    all_gather x1, waiting for transfers between devices, local(): lax.all_gather(jnp.concatenate([adjoint[:, :half_s], coded], axis=1), axe...  95.3 us
    convert_element_type x7, other arithmetic, split(): return (high.astype(jnp.bfloat16), (x - high).astype(jnp.bfloat16))  84.4 us
    pallas_call x2, Pallas kernels, smooth_zx(): pl.pallas_call(_zx_kernel, grid=(len(blocks),), in_specs=[pl.BlockSpec(me...  33.9 us
    scatter-add x1, other arithmetic, local(): raw_gradient = jnp.zeros((cell_count, depth_len), jnp.float32).at[cells.r...  23.3 us
    gather x1, local copies, waits for them, and re-layouts, local(): predicted = jnp.take(tile_table.astype(jnp.bfloat16), cell_recv, axis=0)  20.8 us
    pallas_call x1, Pallas kernels, smooth_y(): pl.pallas_call(_y_kernel, grid=(nx // tx,), in_specs=[pl.BlockSpec(memory...  20.4 us
    slice x2, local copies, waits for them, and re-layouts, local(): first_all[:, :half_s].reshape(all_blocks, per_block, half_s)  19.7 us
  transfers between devices with their start and end apart: 8, of which 5 were waited for; matrix products, arithmetic and copies ran while one was open for 28% of the time, Pallas kernels for 4%

profile of v7, /device:TPU:1, one launch (start us, length us, event | category | flops | bytes accessed | tf_op | source)
XLA Modules:
  0.0 588.8 jit_solution(1079453419114040838)
XLA Ops:
  11.0 7.1 %all-to-all-start = ((s32[32,1,64]{2,1,0:T(1,128)}), s32[32,1,64]{2,1,0:T(1,128)S(1)}, u32[]{:S(2)}, u32[]{:S(2)}) async-start(s32[32,1,64]{2,1,0:T(1,128)} %bitcast.4), calls=%async_computation | async-start | bytes 32768 | tf_op jit(solution)/shard_map/all_to_all | solution.py:200
  18.1 14.0 %convolution_convert_fusion = bf16[2048,2048]{1,0:T(8,128)(2,1)} fusion(bf16[2048,1024]{1,0:T(8,128)(2,1)} %bitcast.139, bf16[1,1,2048,1024]{3,2,1,0:T(8,128)(2,1)} %param.10), kind=kOutput, calls=%fused_computation.13 | convolution fusion | flops 8594128896 | bytes 16777216 | tf_op jit(solution)/shard_map/dot_general | solution.py:211
  33.4 20.8 %gather_fusion = bf16[2048,2048]{1,0:T(8,128)(2,1)} fusion(bf16[2048,2048]{1,0:T(8,128)(2,1)} %convolution_convert_fusion, s32[2048]{0:T(1024)S(1)} %broadcast_clamp_fusion), kind=kCustom, calls=%fused_computation.2 | custom fusion | bytes 16785408 | tf_op jit(solution)/shard_map/jit(_take)/gather | solution.py:214
  54.2 7.6 %broadcast_select_fusion = bf16[32,64,2048]{2,1,0:T(8,128)(2,1)} fusion(bf16[32,64,2048]{2,1,0:T(8,128)(2,1)} %bitcast.116, pred[32,64]{1,0:T(8,128)(4,1)S(1)} %compare_and_fusion), kind=kLoop, calls=%fused_computation.12 | loop fusion | flops 4194304 | bytes 16779264 | tf_op jit(solution)/shard_map/jit(_take)/select_n | solution.py:214
  69.9 20.5 %reduce-precision_convert_fusion.3 = bf16[256,128]{1,0:T(8,128)(2,1)S(1)} fusion(f32[]{:T(128)} %bitcast.47, f32[]{:T(128)} %bitcast.46, f32[]{:T(128)} %bitcast.45, f32[]{:T(128)} %bitcast.44, f32[]{:T(128)} %bitcast.43, f32[]{:T(128)} %bitcast.42, f32[]{:T(128)} %bitcast.41, f32[]{:T(128)} %bitcast.40, f32[]{:T(128)} %bitcast.39, f32[]{:T(128)} %bitcast.38, ...), kind=kLoop, calls=%fused_computation.51 | loop fusion | flops 2293760 | bytes 65668 | tf_op jit(solution)/shard_map/convert_element_type | solution.py:133
  90.4 20.5 %fusion.21 = bf16[256,128]{1,0:T(8,128)(2,1)S(1)} fusion(f32[]{:T(128)} %bitcast.47, f32[]{:T(128)} %bitcast.46, f32[]{:T(128)} %bitcast.45, f32[]{:T(128)} %bitcast.44, f32[]{:T(128)} %bitcast.43, f32[]{:T(128)} %bitcast.42, f32[]{:T(128)} %bitcast.41, f32[]{:T(128)} %bitcast.40, f32[]{:T(128)} %bitcast.39, f32[]{:T(128)} %bitcast.38, f32[]{:T(128)} %bitcast.37, ...), kind=kLoop, calls=%fused_computation.52 | loop fusion | flops 2326528 | bytes 65668 | tf_op jit(solution)/shard_map/convert_element_type | solution.py:133
  112.0 20.5 %reduce-precision_convert_fusion.2 = bf16[256,128]{1,0:T(8,128)(2,1)S(1)} fusion(f32[]{:T(128)} %bitcast.15, f32[]{:T(128)} %bitcast.16, f32[]{:T(128)} %bitcast.17, f32[]{:T(128)} %bitcast.18, f32[]{:T(128)} %bitcast.19, f32[]{:T(128)} %bitcast.20, f32[]{:T(128)} %bitcast.21, f32[]{:T(128)} %bitcast.22, f32[]{:T(128)} %bitcast.23, f32[]{:T(128)} %bitcast.24, ...), kind=kLoop, calls=%fused_computation.49 | loop fusion | flops 2293760 | bytes 65668 | tf_op jit(solution)/shard_map/convert_element_type | solution.py:133
  132.5 20.5 %fusion.22 = bf16[256,128]{1,0:T(8,128)(2,1)S(1)} fusion(f32[]{:T(128)} %bitcast.15, f32[]{:T(128)} %bitcast.16, f32[]{:T(128)} %bitcast.17, f32[]{:T(128)} %bitcast.18, f32[]{:T(128)} %bitcast.19, f32[]{:T(128)} %bitcast.20, f32[]{:T(128)} %bitcast.21, f32[]{:T(128)} %bitcast.22, f32[]{:T(128)} %bitcast.23, f32[]{:T(128)} %bitcast.24, f32[]{:T(128)} %bitcast.25, ...), kind=kLoop, calls=%fused_computation.53 | loop fusion | flops 2326528 | bytes 65668 | tf_op jit(solution)/shard_map/convert_element_type | solution.py:133
  153.3 103.6 %all-to-all-done.1 = bf16[32,64,2048]{2,1,0:T(8,128)(2,1)} async-done(((bf16[32,64,2048]{2,1,0:T(8,128)(2,1)}), bf16[32,64,2048]{2,1,0:T(8,128)(2,1)}, u32[]{:S(2)}, u32[]{:S(2)}) %all-to-all-start.1) | async-done | bytes 8388640 | tf_op jit(solution)/shard_map/all_to_all | solution.py:171
  256.9 6.2 %gather_fusion.1 = bf16[128,8,2048]{2,1,0:T(8,128)(2,1)} fusion(bf16[256,8,2048]{2,1,0:T(8,128)(2,1)} %bitcast.10, s32[1024]{0:T(1024)S(1)} %pad_clamp_fusion.1), kind=kCustom, calls=%fused_computation.3 | custom fusion | bytes 8389120 | tf_op jit(solution)/shard_map/jit(_take)/gather | solution.py:217
  282.6 95.3 %all-gather.3.cloned.1.call-done = bf16[4096,1152]{0,1:T(8,128)(2,1)} async-done(((bf16[128,1152]{0,1:T(8,128)(2,1)}), bf16[4096,1152]{0,1:T(8,128)(2,1)}) %all-gather.3.cloned.1.call-update) | async-done | bytes 9437200 | tf_op jit(solution)/shard_map/all_gather | solution.py:237
  386.1 10.9 %fusion.71 = (pred[512]{0:T(512)(128)(4,1)S(1)}, pred[512,1,8]{2,1,0:T(4,128)(4,1)S(1)}) fusion(s32[]{:T(128)S(6)} %add.311, s32[512,8,24]{2,1,0:T(8,128)} %bitcast.128), kind=kLoop, calls=%fused_computation.150 | loop fusion | flops 7680 | bytes 20996 | tf_op jit(solution)/shard_map/reduce_or | solution.py:249
  406.1 7.9 %slice.334 = bf16[4096,1024]{0,1:T(8,128)(2,1)} slice(bf16[4096,1152]{0,1:T(8,128)(2,1)} %all-gather.3.cloned.1.call-done), slice={[0:4096], [0:1024]} | slice | bytes 16777216 | tf_op jit(solution)/shard_map/slice | solution.py:266
  414.0 11.8 %copy.100 = bf16[4096,1024]{1,0:T(8,128)(2,1)} copy(bf16[4096,1024]{0,1:T(8,128)(2,1)} %slice.334) | data formatting | bytes 16777216 | tf_op jit(solution)/shard_map/slice | solution.py:266
  425.9 7.3 %gather_fusion.4 = bf16[256,8,1024]{2,1,0:T(8,128)(2,1)} fusion(bf16[512,8,1024]{2,1,0:T(8,128)(2,1)} %bitcast.117, s32[1024]{0:T(1024)S(1)} %pad_clamp_fusion), kind=kCustom, calls=%fused_computation.clone | custom fusion | bytes 8389632 | tf_op jit(solution)/shard_map/jit(_take)/gather | solution.py:265
  433.2 11.0 %fusion.4 = f32[2048,1024]{1,0:T(8,128)} fusion(bf16[256,8,1024]{2,1,0:T(8,128)(2,1)} %gather_fusion.4, pred[256]{0:T(512)(128)(4,1)S(1)} %compare_and_fusion.3, bf16[1,1,2048,1024]{3,2,1,0:T(8,128)(2,1)} %param.10), kind=kOutput, calls=%fused_computation.16 | convolution fusion | flops 4297064448 | bytes 14680320 | tf_op jit(solution)/shard_map/dot_general | solution.py:268
  444.1 12.4 %all-gather.5.cloned.1.call-done = bf16[4096,1024]{1,0:T(8,128)(2,1)} async-done(((bf16[128,1024]{1,0:T(8,128)(2,1)}), bf16[4096,1024]{1,0:T(8,128)(2,1)}) %all-gather.5.cloned.1.call-update) | async-done | bytes 8388624 | tf_op jit(solution)/shard_map/all_gather | solution.py:240
  456.5 6.2 %gather_fusion.5 = bf16[256,8,1024]{2,1,0:T(8,128)(2,1)} fusion(bf16[512,8,1024]{2,1,0:T(8,128)(2,1)} %bitcast.129, s32[1024]{0:T(1024)S(1)} %pad_clamp_fusion), kind=kCustom, calls=%fused_computation.1.clone | custom fusion | bytes 8389632 | tf_op jit(solution)/shard_map/jit(_take)/gather | solution.py:273
  462.7 10.8 %fusion.2 = f32[2048,1024]{1,0:T(8,128)} fusion(bf16[256,8,1024]{2,1,0:T(8,128)(2,1)} %gather_fusion.5, pred[256]{0:T(512)(128)(4,1)S(1)} %compare_and_fusion.3, bf16[1,1,2048,1024]{3,2,1,0:T(8,128)(2,1)} %param.10), kind=kOutput, calls=%fused_computation.14 | convolution fusion | flops 4297064448 | bytes 14680320 | tf_op jit(solution)/shard_map/dot_general | solution.py:274
  473.5 23.3 %scatter_custom_fusion.2 = f32[2048,1024]{1,0:T(8,128)} fusion(s32[2048]{0:T(1024)S(1)} %bitcast.135, f32[2048,1024]{1,0:T(8,128)} %fusion.4, f32[2048,1024]{1,0:T(8,128)} %fusion.2, f32[]{:T(128)} %constant.58.clone.1), kind=kCustom, calls=%fused_computation.9 | custom fusion | flops 4194304 | bytes 25165828 | tf_op jit(solution)/shard_map/scatter-add | solution.py:282
  503.6 9.8 %collective-permute-done.low_ref = f32[4,64,1024]{2,1,0:T(8,128)S(1)} collective-permute-done((f32[4,64,1024]{2,1,0:T(8,128)S(1)}, f32[4,64,1024]{2,1,0:T(8,128)S(1)}, u32[]{:S(2)}, u32[]{:S(2)}) %collective-permute-start) | collective-permute-done | bytes 1048608 | tf_op jit(solution)/shard_map/ppermute | solution.py:101
  518.8 9.5 %shard_map.86.first_ref.last_ref = f32[32,16,1024]{2,1,0:T(8,128)} custom-call(f32[9]{0:T(128)} %taps_ref.5, f32[32,64,1024]{2,1,0:T(8,128)} %bitcast.113, f32[4,64,1024]{2,1,0:T(8,128)} %copy-done, f32[4,64,1024]{2,1,0:T(8,128)} %copy-done.1), custom_call_target="tpu_custom_call" | custom-call | flops 20971520 | bytes 5242880 | tf_op jit(solution)/shard_map/pallas_call | solution.py:36
  535.0 24.4 %shard_map.87.middle_ref = f32[32,48,1024]{2,1,0:T(8,128)} custom-call(f32[9]{0:T(128)} %taps_ref.5, f32[32,64,1024]{2,1,0:T(8,128)} %bitcast.114, f32[4,64,1024]{2,1,0:T(8,128)} %copy-done, f32[4,64,1024]{2,1,0:T(8,128)} %copy-done.1), custom_call_target="tpu_custom_call" | custom-call | flops 62914560 | bytes 15728640 | tf_op jit(solution)/shard_map/pallas_call | solution.py:36
  561.1 20.4 %shard_map.88 = f32[32,64,1024]{2,1,0:T(8,128)} custom-call(f32[9]{0:T(128)} %taps_ref.5, f32[32,16,1024]{2,1,0:T(8,128)} %shard_map.86.first_ref.last_ref, f32[32,48,1024]{2,1,0:T(8,128)} %shard_map.87.middle_ref, f32[32,16,1024]{2,1,0:T(8,128)} %shard_map.86.first_ref.last_ref, f32[32,4,1024]{2,1,0:T(4,128)} %copy-done.5, f32[32,4,1024]{2,1,0:T(4,128)} %copy-done.6), custom_call_target="tpu_custom_call" | custom-call | flops 37748736 | bytes 18454936 | tf_op jit(solution)/shard_map/pallas_call | solution.py:73
  (132 shorter events, 71.3 us)
Async XLA Ops:
  11.0 21.1 %all-to-all-start = ((s32[32,1,64]{2,1,0:T(1,128)}), s32[32,1,64]{2,1,0:T(1,128)S(1)}, u32[]{:S(2)}, u32[]{:S(2)}) async-start(s32[32,1,64]{2,1,0:T(1,128)} %bitcast.4), calls=%async_computation | async-start | bytes 32768 | tf_op jit(solution)/shard_map/all_to_all | solution.py:200
  61.8 6.6 %copy-start.9 = (s32[16,8]{0,1:T(8,128)S(1)}, s32[16,8]{0,1:T(8,128)}, u32[]{:S(2)}) copy-start(s32[16,8]{0,1:T(8,128)} %param.14) | copy-start | bytes 1540
  61.8 6.6 %copy-start.4 = (f32[33]{0:T(128)S(1)}, f32[33]{0:T(128)}, u32[]{:S(2)}) copy-start(f32[33]{0:T(128)} %param.12) | copy-start | bytes 400
  61.8 49.1 %copy-start.7 = (bf16[128,2048]{1,0:T(8,128)(2,1)S(1)}, bf16[128,2048]{1,0:T(8,128)(2,1)}, u32[]{:S(2)}) copy-start(bf16[128,2048]{1,0:T(8,128)(2,1)} %param.11) | copy-start | bytes 1572868
  61.8 195.0 %all-to-all-start.1 = ((bf16[32,64,2048]{2,1,0:T(8,128)(2,1)}), bf16[32,64,2048]{2,1,0:T(8,128)(2,1)}, u32[]{:S(2)}, u32[]{:S(2)}) async-start(bf16[32,64,2048]{2,1,0:T(8,128)(2,1)} %broadcast_select_fusion), calls=%async_computation.1 | async-start | bytes 16777216 | tf_op jit(solution)/shard_map/all_to_all | solution.py:171
  67.7 310.1 %all-gather.3.cloned.1.call-start = ((), (), s32[]{:S(2)}) async-start(), calls=%async_computation.2 | async-start | bytes 9732096 | tf_op jit(solution)/shard_map/all_gather | solution.py:237
  278.2 1.2 copy-start.2
  278.6 2.4 copy-start.8
  281.1 0.7 copy-start.3
  281.8 174.7 %all-gather.5.cloned.1.call-start = ((), (), s32[]{:S(2)}) async-start(), calls=%async_computation.3 | async-start | bytes 8650752 | tf_op jit(solution)/shard_map/all_gather | solution.py:240
  498.5 14.9 %collective-permute-start = (f32[4,64,1024]{2,1,0:T(8,128)S(1)}, f32[4,64,1024]{2,1,0:T(8,128)S(1)}, u32[]{:S(2)}, u32[]{:S(2)}) collective-permute-start(f32[4,64,1024]{2,1,0:T(8,128)S(1)} %bitcast.131), channel_id=1, source_target_pairs={{0,8},{8,16},{16,24},{1,9},{9,17},{17,25},{2,10},{10,18},{18,26},{... | collective-permute-start | bytes 3145736 | tf_op jit(solution)/shard_map/ppermute | solution.py:101
  501.7 16.1 %collective-permute-start.1 = (f32[4,64,1024]{2,1,0:T(8,128)S(1)}, f32[4,64,1024]{2,1,0:T(8,128)S(1)}, u32[]{:S(2)}, u32[]{:S(2)}) collective-permute-start(f32[4,64,1024]{2,1,0:T(8,128)S(1)} %bitcast.130), channel_id=1, source_target_pairs={{8,0},{16,8},{24,16},{9,1},{17,9},{25,17},{10,2},{18,10},{26,18},{... | collective-permute-start | bytes 3145736 | tf_op jit(solution)/shard_map/ppermute | solution.py:104
  513.4 4.4 copy-start
  517.8 1.0 copy-start.1
  530.1 29.2 %collective-permute-start.2 = (f32[32,4,1024]{2,1,0:T(4,128)S(1)}, f32[32,4,1024]{2,1,0:T(4,128)S(1)}, u32[]{:S(2)}, u32[]{:S(2)}) collective-permute-start(f32[32,4,1024]{2,1,0:T(4,128)S(1)} %get-tuple-element.30), channel_id=1, source_target_pairs={{0,1},{1,2},{2,3},{3,4},{4,5},{5,6},{6,7},{8,9},{9,10},{10,11},{11... | collective-permute-start | bytes 1572872 | tf_op jit(solution)/shard_map/ppermute | solution.py:101
  532.4 27.0 %collective-permute-start.3 = (f32[32,4,1024]{2,1,0:T(4,128)S(1)}, f32[32,4,1024]{2,1,0:T(4,128)S(1)}, u32[]{:S(2)}, u32[]{:S(2)}) collective-permute-start(f32[32,4,1024]{2,1,0:T(4,128)S(1)} %get-tuple-element.29), channel_id=1, source_target_pairs={{1,0},{2,1},{3,2},{4,3},{5,4},{6,5},{7,6},{9,8},{10,9},{11,10},{12... | collective-permute-start | bytes 1572872 | tf_op jit(solution)/shard_map/ppermute | solution.py:104
  559.4 0.8 copy-start.5
  560.2 0.9 copy-start.6
Sparse Core Ops, SparseCore 0:
  281.9 95.8 all-gather.2
  380.9 75.5 all-gather.4

commit v8 on v6

--- a/solution.py
+++ b/solution.py
@@ -212,15 +212,27 @@
     tile_rows = image.reshape(cell_count, depth_len)
     weight_matrix = weights.reshape(samples, depth_len)
     contract = (((1,), (1,)), ((), ()))
-    tile_table = lax.dot_general(
-        tile_rows, weight_matrix, contract, preferred_element_type=jnp.float32
-    )
-    predicted = jnp.take(tile_table.astype(jnp.bfloat16), cell_recv, axis=0)
-    outgoing = predicted.reshape(device_count, capacity * per_block, samples)
-    returned = traverse(outgoing).reshape(device_count * capacity, per_block, samples)
-    own_preds = jnp.take(returned, target_slot, axis=0).reshape(
-        block_count, aperture_len, per_block, samples
-    )
+    half_cap = capacity // 2
+    requests = cell_recv.reshape(device_count, capacity, per_block)
+    returned = []
+    for part in range(2):
+        wanted = requests[:, part * half_cap:(part + 1) * half_cap].reshape(-1)
+        predicted = lax.dot_general(
+            jnp.take(tile_rows, wanted, axis=0), weight_matrix, contract,
+            preferred_element_type=jnp.float32,
+        ).astype(jnp.bfloat16)
+        returned.append(
+            traverse(predicted.reshape(device_count, half_cap * per_block, samples)).reshape(
+                device_count * half_cap, per_block, samples
+            )
+        )
+    tile_of = target_tile
+    within = slot_index % half_cap
+    from_first = jnp.take(returned[0], tile_of * half_cap + within, axis=0)
+    from_second = jnp.take(returned[1], tile_of * half_cap + within, axis=0)
+    own_preds = jnp.where(
+        (slot_index < half_cap)[:, None, None], from_first, from_second
+    ).reshape(block_count, aperture_len, per_block, samples)
     synthetic = jnp.sum(own_preds.astype(jnp.float32), axis=1).reshape(trace_count, samples)
     half = wavelet.shape[0] // 2
     modeled = banded(synthetic, band_block(wavelet[::-1], half))

time: 546 us -> 530 us (0.971)
  waiting for transfers between devices: 162 us -> 143 us
  blocking collectives: 58.9 us -> 73.2 us
  other arithmetic: 122 us -> 115 us
    all_to_all x1 -> x2, waiting for transfers between devices: 104 us -> 85.3 us  [traverse(): lax.all_to_all(blocks, ('inline', 'xline'), split_axis=0, concat_axis=0,...]
    all_to_all x0 -> x1, blocking collectives: none -> 13.6 us  [local(): lax.all_to_all(cell_send.reshape(device_count, capacity * per_block), axe...]
    select_n x3 -> x1, other arithmetic: 7.63 us -> 0.01 us  [local(): jnp.zeros((device_count * capacity, per_block), jnp.int32).at[target_slot]]
    all_to_all x1 -> x0, starting transfers between devices: 7.1 us -> none  [local(): lax.all_to_all(cell_send.reshape(device_count, capacity * per_block), axe...]
    dot_general x1 -> x2, matrix products: 14 us -> 17.1 us  [local(): lax.dot_general(jnp.take(tile_rows, wanted, axis=0), weight_matrix, contr...]
    gather x2 -> x4, local copies, waits for them, and re-layouts: 27 us -> 25.4 us  [the longest x2 15.4 us: local(): jnp.take(tile_rows, wanted, axis=0)]
  transfers between devices with their start and end apart: 7 -> 7, of which waited for: 4 -> 5; matrix products, arithmetic and copies ran while one was open for 20% -> 23% of each run, Pallas kernels for 4% -> 5%
where the time goes in v8:
time: 530 us; the launch traced here: 521 us
  waiting for transfers between devices  143 us (27%)
  other arithmetic  115 us (22%)
  blocking collectives  73.2 us (14%)
  local copies, waits for them, and re-layouts  68.3 us (13%)
  Pallas kernels  54 us (10%)
  matrix products  34.5 us (7%)
  starting transfers between devices  18.2 us (3%)
  between operations  15.1 us (3%)
    all_to_all x2, waiting for transfers between devices, traverse(): lax.all_to_all(blocks, ('inline', 'xline'), split_axis=0, concat_axis=0,...  85.3 us
    convert_element_type x7, other arithmetic, split(): return (high.astype(jnp.bfloat16), (x - high).astype(jnp.bfloat16))  83.6 us
    all_gather x1, blocking collectives, local(): tables_all = jnp.round(lax.all_gather(tables, axes, axis=0, tiled=True))  59.6 us
    all_gather x1, waiting for transfers between devices, local(): adjoint_all = lax.all_gather(adjoint, axes, axis=0, tiled=True)  43.8 us
    pallas_call x2, Pallas kernels, smooth_zx(): pl.pallas_call(_zx_kernel, grid=(len(blocks),), in_specs=[pl.BlockSpec(me...  33.6 us
    scatter-add x1, other arithmetic, local(): raw_gradient = jnp.zeros((cell_count, depth_len), jnp.float32).at[cells.r...  22.9 us
    pallas_call x1, Pallas kernels, smooth_y(): pl.pallas_call(_y_kernel, grid=(nx // tx,), in_specs=[pl.BlockSpec(memory...  20.4 us
    dot_general x2, matrix products, local(): lax.dot_general(jnp.take(tile_rows, wanted, axis=0), weight_matrix, contr...  17.1 us
  transfers between devices with their start and end apart: 7, of which 5 were waited for; matrix products, arithmetic and copies ran while one was open for 23% of the time, Pallas kernels for 5%

profile of v8, /device:TPU:1, one launch (start us, length us, event | category | flops | bytes accessed | tf_op | source)
XLA Modules:
  0.0 521.5 jit_solution(7127723294468427959)
XLA Ops:
  11.1 13.6 %all_to_all.19 = s32[32,1,64]{2,1,0:T(1,128)S(1)} all-to-all(s32[32,1,64]{2,1,0:T(1,128)S(1)} %bitcast.131), channel_id=1, replica_groups=mesh['inline'=4,'xline'=8] {'inline','xline'}, dimensions={0} | all-to-all | bytes 16384 | tf_op jit(solution)/shard_map/all_to_all | solution.py:204
  25.1 7.7 %gather_fusion.3 = bf16[1024,1024]{1,0:T(8,128)(2,1)S(1)} fusion(bf16[2048,1024]{1,0:T(8,128)(2,1)} %bitcast.109, s32[1024]{0:T(1024)S(1)} %fusion.67), kind=kCustom, calls=%fused_computation.clone | custom fusion | bytes 4198400 | tf_op jit(solution)/shard_map/jit(_take)/gather | solution.py:221
  32.8 8.6 %fusion.12 = bf16[1024,2048]{1,0:T(8,128)(2,1)} fusion(bf16[1,1,2048,1024]{3,2,1,0:T(8,128)(2,1)} %param.12, bf16[1024,1024]{1,0:T(8,128)(2,1)S(1)} %gather_fusion.3, pred[1024]{0:T(1024)(128)(4,1)S(1)} %compare_and_fusion.1), kind=kOutput, calls=%fused_computation.24 | convolution fusion | flops 4298113024 | bytes 10486784 | tf_op jit(solution)/shard_map/dot_general | solution.py:220
  45.3 7.7 %gather_fusion.5 = bf16[1024,1024]{1,0:T(8,128)(2,1)S(1)} fusion(bf16[2048,1024]{1,0:T(8,128)(2,1)} %bitcast.110, s32[1024]{0:T(1024)S(1)} %fusion.68), kind=kCustom, calls=%fused_computation.2.clone | custom fusion | bytes 4198400 | tf_op jit(solution)/shard_map/jit(_take)/gather | solution.py:221
  53.1 8.5 %fusion.15 = bf16[1024,2048]{1,0:T(8,128)(2,1)} fusion(bf16[1,1,2048,1024]{3,2,1,0:T(8,128)(2,1)} %param.12, bf16[1024,1024]{1,0:T(8,128)(2,1)S(1)} %gather_fusion.5, pred[1024]{0:T(1024)(128)(4,1)S(1)} %compare_and_fusion), kind=kOutput, calls=%fused_computation.25 | convolution fusion | flops 4298113024 | bytes 10486784 | tf_op jit(solution)/shard_map/dot_general | solution.py:220
  61.6 79.3 %all-to-all-done.1 = bf16[32,32,2048]{2,1,0:T(8,128)(2,1)} async-done(((bf16[32,32,2048]{2,1,0:T(8,128)(2,1)}), bf16[32,32,2048]{2,1,0:T(8,128)(2,1)}, u32[]{:S(2)}, u32[]{:S(2)}) %all-to-all-start.1) | async-done | bytes 4194336 | tf_op jit(solution)/shard_map/all_to_all | solution.py:171
  146.5 20.5 %fusion.28 = bf16[256,128]{1,0:T(8,128)(2,1)S(1)} fusion(f32[]{:T(128)} %bitcast.24, f32[]{:T(128)} %bitcast.25, f32[]{:T(128)} %bitcast.26, f32[]{:T(128)} %bitcast.27, f32[]{:T(128)} %bitcast.28, f32[]{:T(128)} %bitcast.29, f32[]{:T(128)} %bitcast.30, f32[]{:T(128)} %bitcast.31, f32[]{:T(128)} %bitcast.32, f32[]{:T(128)} %bitcast.33, f32[]{:T(128)} %bitcast.34, ...), kind=kLoop, calls=%fused_computation.53 | loop fusion | flops 2326528 | bytes 65668 | tf_op jit(solution)/shard_map/convert_element_type | solution.py:133
  167.0 20.5 %reduce-precision_convert_fusion.2 = bf16[256,128]{1,0:T(8,128)(2,1)S(1)} fusion(f32[]{:T(128)} %bitcast.24, f32[]{:T(128)} %bitcast.25, f32[]{:T(128)} %bitcast.26, f32[]{:T(128)} %bitcast.27, f32[]{:T(128)} %bitcast.28, f32[]{:T(128)} %bitcast.29, f32[]{:T(128)} %bitcast.30, f32[]{:T(128)} %bitcast.31, f32[]{:T(128)} %bitcast.32, f32[]{:T(128)} %bitcast.33, ...), kind=kLoop, calls=%fused_computation.49 | loop fusion | flops 2293760 | bytes 65668 | tf_op jit(solution)/shard_map/convert_element_type | solution.py:133
  187.6 20.5 %fusion.27 = bf16[256,128]{1,0:T(8,128)(2,1)S(1)} fusion(f32[]{:T(128)} %bitcast.56, f32[]{:T(128)} %bitcast.55, f32[]{:T(128)} %bitcast.54, f32[]{:T(128)} %bitcast.53, f32[]{:T(128)} %bitcast.52, f32[]{:T(128)} %bitcast.51, f32[]{:T(128)} %bitcast.50, f32[]{:T(128)} %bitcast.49, f32[]{:T(128)} %bitcast.48, f32[]{:T(128)} %bitcast.47, f32[]{:T(128)} %bitcast.46, ...), kind=kLoop, calls=%fused_computation.52 | loop fusion | flops 2326528 | bytes 65668 | tf_op jit(solution)/shard_map/convert_element_type | solution.py:133
  208.1 20.5 %reduce-precision_convert_fusion.3 = bf16[256,128]{1,0:T(8,128)(2,1)S(1)} fusion(f32[]{:T(128)} %bitcast.56, f32[]{:T(128)} %bitcast.55, f32[]{:T(128)} %bitcast.54, f32[]{:T(128)} %bitcast.53, f32[]{:T(128)} %bitcast.52, f32[]{:T(128)} %bitcast.51, f32[]{:T(128)} %bitcast.50, f32[]{:T(128)} %bitcast.49, f32[]{:T(128)} %bitcast.48, f32[]{:T(128)} %bitcast.47, ...), kind=kLoop, calls=%fused_computation.51 | loop fusion | flops 2293760 | bytes 65668 | tf_op jit(solution)/shard_map/convert_element_type | solution.py:133
  229.7 5.0 gather_fusion.4
  234.7 5.9 %all-to-all-done.2 = bf16[32,32,2048]{2,1,0:T(8,128)(2,1)} async-done(((bf16[32,32,2048]{2,1,0:T(8,128)(2,1)}), bf16[32,32,2048]{2,1,0:T(8,128)(2,1)}, u32[]{:S(2)}, u32[]{:S(2)}) %all-to-all-start.2) | async-done | bytes 4194336 | tf_op jit(solution)/shard_map/all_to_all | solution.py:171
  240.6 5.0 gather_fusion.6
  245.6 4.5 convert_reduce_fusion
  262.9 59.6 %all_gather.6 = f32[512,72]{1,0:T(8,128)S(1)} all-gather(f32[16,72]{1,0:T(8,128)S(1)} %add_convert_fusion), channel_id=1, replica_groups=mesh['inline'=4,'xline'=8] {'inline','xline'}, dimensions={0}, use_global_device_ids=true | all-gather | bytes 152064 | tf_op jit(solution)/shard_map/all_gather | solution.py:188
  332.5 43.8 %all-gather.2.cloned.1.call-done = bf16[4096,2048]{1,0:T(8,128)(2,1)} async-done(((bf16[128,2048]{1,0:T(8,128)(2,1)}), bf16[4096,2048]{1,0:T(8,128)(2,1)}) %all-gather.2.cloned.1.call-update) | async-done | bytes 16777232 | tf_op jit(solution)/shard_map/all_gather | solution.py:242
  376.2 14.5 %gather_fusion.1 = bf16[256,8,2048]{2,1,0:T(8,128)(2,1)} fusion(bf16[512,8,2048]{2,1,0:T(8,128)(2,1)} %bitcast.123, s32[1024]{0:T(1024)S(1)} %pad_clamp_fusion.1), kind=kCustom, calls=%fused_computation.5 | custom fusion | bytes 16778240 | tf_op jit(solution)/shard_map/jit(_take)/gather | solution.py:264
  390.7 14.8 %fusion = f32[2048,1024]{1,0:T(8,128)} fusion(bf16[256,8,2048]{2,1,0:T(8,128)(2,1)} %gather_fusion.1, pred[256]{0:T(512)(128)(4,1)S(1)} %compare_and_fusion.4, bf16[1,1,2048,1024]{3,2,1,0:T(8,128)(2,1)} %param.12), kind=kOutput, calls=%fused_computation.11 | convolution fusion | flops 8594128896 | bytes 20971776 | tf_op jit(solution)/shard_map/dot_general | solution.py:265
  405.5 22.9 %scatter_custom_fusion.2 = f32[2048,1024]{1,0:T(8,128)} fusion(s32[2048]{0:T(1024)S(1)} %bitcast.132, f32[2048,1024]{1,0:T(8,128)} %fusion, f32[]{:T(128)} %constant.62.clone.1), kind=kCustom, calls=%fused_computation.22 | custom fusion | flops 2097152 | bytes 8389120 | tf_op jit(solution)/shard_map/scatter-add | solution.py:273
  435.2 9.5 %collective-permute-done.low_ref = f32[4,64,1024]{2,1,0:T(8,128)S(1)} collective-permute-done((f32[4,64,1024]{2,1,0:T(8,128)S(1)}, f32[4,64,1024]{2,1,0:T(8,128)S(1)}, u32[]{:S(2)}, u32[]{:S(2)}) %collective-permute-start) | collective-permute-done | bytes 1048608 | tf_op jit(solution)/shard_map/ppermute | solution.py:101
  444.7 4.4 collective-permute-done.1.high_ref
  450.1 9.5 %shard_map.86.first_ref.last_ref = f32[32,16,1024]{2,1,0:T(8,128)} custom-call(f32[9]{0:T(128)} %taps_ref.5, f32[32,64,1024]{2,1,0:T(8,128)} %bitcast.111, f32[4,64,1024]{2,1,0:T(8,128)} %copy-done, f32[4,64,1024]{2,1,0:T(8,128)} %copy-done.1), custom_call_target="tpu_custom_call" | custom-call | flops 20971520 | bytes 5242880 | tf_op jit(solution)/shard_map/pallas_call | solution.py:36
  468.0 24.1 %shard_map.87.middle_ref = f32[32,48,1024]{2,1,0:T(8,128)} custom-call(f32[9]{0:T(128)} %taps_ref.5, f32[32,64,1024]{2,1,0:T(8,128)} %bitcast.112, f32[4,64,1024]{2,1,0:T(8,128)} %copy-done, f32[4,64,1024]{2,1,0:T(8,128)} %copy-done.1), custom_call_target="tpu_custom_call" | custom-call | flops 62914560 | bytes 15728640 | tf_op jit(solution)/shard_map/pallas_call | solution.py:36
  493.8 20.4 %shard_map.88 = f32[32,64,1024]{2,1,0:T(8,128)} custom-call(f32[9]{0:T(128)} %taps_ref.5, f32[32,16,1024]{2,1,0:T(8,128)} %shard_map.86.first_ref.last_ref, f32[32,48,1024]{2,1,0:T(8,128)} %shard_map.87.middle_ref, f32[32,16,1024]{2,1,0:T(8,128)} %shard_map.86.first_ref.last_ref, f32[32,4,1024]{2,1,0:T(4,128)} %copy-done.5, f32[32,4,1024]{2,1,0:T(4,128)} %copy-done.4), custom_call_target="tpu_custom_call" | custom-call | flops 37748736 | bytes 18454936 | tf_op jit(solution)/shard_map/pallas_call | solution.py:73
  (120 shorter events, 54.9 us)
Async XLA Ops:
  41.4 99.6 %all-to-all-start.1 = ((bf16[32,32,2048]{2,1,0:T(8,128)(2,1)}), bf16[32,32,2048]{2,1,0:T(8,128)(2,1)}, u32[]{:S(2)}, u32[]{:S(2)}) async-start(bf16[32,32,2048]{2,1,0:T(8,128)(2,1)} %bitcast.125), calls=%async_computation.1 | async-start | bytes 8388608 | tf_op jit(solution)/shard_map/all_to_all | solution.py:171
  140.9 4.1 copy-start.3
  140.9 87.7 %copy-start.6 = (bf16[128,2048]{1,0:T(8,128)(2,1)S(1)}, bf16[128,2048]{1,0:T(8,128)(2,1)}, u32[]{:S(2)}) copy-start(bf16[128,2048]{1,0:T(8,128)(2,1)} %param.13) | copy-start | bytes 1572868
  140.9 99.7 %all-to-all-start.2 = ((bf16[32,32,2048]{2,1,0:T(8,128)(2,1)}), bf16[32,32,2048]{2,1,0:T(8,128)(2,1)}, u32[]{:S(2)}, u32[]{:S(2)}) async-start(bf16[32,32,2048]{2,1,0:T(8,128)(2,1)} %bitcast.124), calls=%async_computation.2 | async-start | bytes 8388608 | tf_op jit(solution)/shard_map/all_to_all | solution.py:171
  144.8 231.4 %all-gather.2.cloned.1.call-start = ((), (), s32[]{:S(2)}) async-start(), calls=%async_computation.3 | async-start | bytes 17301504 | tf_op jit(solution)/shard_map/all_gather | solution.py:242
  259.9 1.2 copy-start.2
  260.4 2.3 copy-start.7
  430.0 14.7 %collective-permute-start = (f32[4,64,1024]{2,1,0:T(8,128)S(1)}, f32[4,64,1024]{2,1,0:T(8,128)S(1)}, u32[]{:S(2)}, u32[]{:S(2)}) collective-permute-start(f32[4,64,1024]{2,1,0:T(8,128)S(1)} %bitcast.128), channel_id=1, source_target_pairs={{0,8},{8,16},{16,24},{1,9},{9,17},{17,25},{2,10},{10,18},{18,26},{... | collective-permute-start | bytes 3145736 | tf_op jit(solution)/shard_map/ppermute | solution.py:101
  433.0 16.1 %collective-permute-start.1 = (f32[4,64,1024]{2,1,0:T(8,128)S(1)}, f32[4,64,1024]{2,1,0:T(8,128)S(1)}, u32[]{:S(2)}, u32[]{:S(2)}) collective-permute-start(f32[4,64,1024]{2,1,0:T(8,128)S(1)} %bitcast.127), channel_id=1, source_target_pairs={{8,0},{16,8},{24,16},{9,1},{17,9},{25,17},{10,2},{18,10},{26,18},{... | collective-permute-start | bytes 3145736 | tf_op jit(solution)/shard_map/ppermute | solution.py:104
  444.7 4.4 copy-start
  449.1 1.0 copy-start.1
  461.4 30.7 %collective-permute-start.3 = (f32[32,4,1024]{2,1,0:T(4,128)S(1)}, f32[32,4,1024]{2,1,0:T(4,128)S(1)}, u32[]{:S(2)}, u32[]{:S(2)}) collective-permute-start(f32[32,4,1024]{2,1,0:T(4,128)S(1)} %get-tuple-element.32), channel_id=1, source_target_pairs={{1,0},{2,1},{3,2},{4,3},{5,4},{6,5},{7,6},{9,8},{10,9},{11,10},{12... | collective-permute-start | bytes 1572872 | tf_op jit(solution)/shard_map/ppermute | solution.py:104
  462.7 29.4 %collective-permute-start.2 = (f32[32,4,1024]{2,1,0:T(4,128)S(1)}, f32[32,4,1024]{2,1,0:T(4,128)S(1)}, u32[]{:S(2)}, u32[]{:S(2)}) collective-permute-start(f32[32,4,1024]{2,1,0:T(4,128)S(1)} %get-tuple-element.33), channel_id=1, source_target_pairs={{0,1},{1,2},{2,3},{3,4},{4,5},{5,6},{6,7},{8,9},{9,10},{10,11},{11... | collective-permute-start | bytes 1572872 | tf_op jit(solution)/shard_map/ppermute | solution.py:101
  492.1 0.9 copy-start.4
  493.0 0.8 copy-start.5
Sparse Core Ops, SparseCore 0:
  262.8 113.4 all-gather.1

commit v9 on v8

--- a/solution.py
+++ b/solution.py
@@ -10,24 +10,22 @@
 
 def _zx_kernel(taps_ref, main_ref, low_ref, high_ref, out_ref, ext_ref):
     nx = main_ref.shape[0]
-    ext_ref[0:HW] = low_ref[...]
-    ext_ref[HW:HW + nx] = main_ref[...]
-    ext_ref[HW + nx:] = high_ref[...]
-    depth = ext_ref.shape[2]
+    depth = main_ref.shape[2]
+    ext_ref[:, :, depth:] = jnp.zeros(ext_ref.shape[:2] + (ext_ref.shape[2] - depth,), jnp.float32)
+    ext_ref[0:HW, :, :depth] = low_ref[...]
+    ext_ref[HW:HW + nx, :, :depth] = main_ref[...]
+    ext_ref[HW + nx:, :, :depth] = high_ref[...]
     x = ext_ref[...]
-    lane = lax.broadcasted_iota(jnp.int32, x.shape, 2)
+    wide = x.shape[2]
     acc = taps_ref[HW] * x
     for j in range(2 * HW + 1):
         if j == HW:
             continue
-        shifted = pltpu.roll(x, (HW - j) % depth, 2)
-        source = lane + (j - HW)
-        keep = (source >= 0) & (source < depth)
-        acc = acc + taps_ref[j] * jnp.where(keep, shifted, 0.0)
+        acc = acc + taps_ref[j] * pltpu.roll(x, (HW - j) % wide, 2)
     ext_ref[...] = acc
-    out = taps_ref[0] * ext_ref[0:nx]
+    out = taps_ref[0] * ext_ref[0:nx, :, :depth]
     for j in range(1, 2 * HW + 1):
-        out = out + taps_ref[j] * ext_ref[j:j + nx]
+        out = out + taps_ref[j] * ext_ref[j:j + nx, :, :depth]
     out_ref[...] = out
 
 
@@ -44,7 +42,7 @@
         ],
         out_specs=pl.BlockSpec((nx, ty, nz), lambda i: (0, i, 0)),
         out_shape=jax.ShapeDtypeStruct((nx, ty * len(blocks), nz), jnp.float32),
-        scratch_shapes=[pltpu.VMEM((nx + 2 * HW, ty, nz), jnp.float32)],
+        scratch_shapes=[pltpu.VMEM((nx + 2 * HW, ty, nz + 128), jnp.float32)],
         cost_estimate=pl.CostEstimate(
             flops=40 * nx * ty * nz * len(blocks), transcendentals=0,
             bytes_accessed=int(nx * ty * nz * len(blocks) * 10),

time: 530 us -> 530 us (level)
  transfers between devices with their start and end apart: 7 -> 7, of which waited for: 5 -> 5; matrix products, arithmetic and copies ran while one was open for 23% -> 22% of each run, Pallas kernels for 5% -> 5%
where the time goes in v9:
time: 530 us; the launch traced here: 522 us
  waiting for transfers between devices  143 us (27%)
  other arithmetic  115 us (22%)
  blocking collectives  73.2 us (14%)
  local copies, waits for them, and re-layouts  68.4 us (13%)
  Pallas kernels  54.6 us (10%)
  matrix products  34.5 us (7%)
  starting transfers between devices  18.2 us (3%)
  between operations  15.1 us (3%)
    all_to_all x2, waiting for transfers between devices, traverse(): lax.all_to_all(blocks, ('inline', 'xline'), split_axis=0, concat_axis=0,...  85.3 us
    convert_element_type x7, other arithmetic, split(): return (high.astype(jnp.bfloat16), (x - high).astype(jnp.bfloat16))  83.6 us
    all_gather x1, blocking collectives, local(): tables_all = jnp.round(lax.all_gather(tables, axes, axis=0, tiled=True))  59.6 us
    all_gather x1, waiting for transfers between devices, local(): adjoint_all = lax.all_gather(adjoint, axes, axis=0, tiled=True)  43.8 us
    pallas_call x2, Pallas kernels, smooth_zx(): pl.pallas_call(_zx_kernel, grid=(len(blocks),), in_specs=[pl.BlockSpec(me...  34.2 us
    scatter-add x1, other arithmetic, local(): raw_gradient = jnp.zeros((cell_count, depth_len), jnp.float32).at[cells.r...  22.9 us
    pallas_call x1, Pallas kernels, smooth_y(): pl.pallas_call(_y_kernel, grid=(nx // tx,), in_specs=[pl.BlockSpec(memory...  20.4 us
    dot_general x2, matrix products, local(): lax.dot_general(jnp.take(tile_rows, wanted, axis=0), weight_matrix, contr...  17.1 us
  transfers between devices with their start and end apart: 7, of which 5 were waited for; matrix products, arithmetic and copies ran while one was open for 22% of the time, Pallas kernels for 5%

profile of v9, /device:TPU:1, one launch (start us, length us, event | category | flops | bytes accessed | tf_op | source)
XLA Modules:
  0.0 522.2 jit_solution(1462630661327578300)
XLA Ops:
  11.1 13.6 %all_to_all.19 = s32[32,1,64]{2,1,0:T(1,128)S(1)} all-to-all(s32[32,1,64]{2,1,0:T(1,128)S(1)} %bitcast.131), channel_id=1, replica_groups=mesh['inline'=4,'xline'=8] {'inline','xline'}, dimensions={0} | all-to-all | bytes 16384 | tf_op jit(solution)/shard_map/all_to_all | solution.py:202
  25.1 7.7 %gather_fusion.3 = bf16[1024,1024]{1,0:T(8,128)(2,1)S(1)} fusion(bf16[2048,1024]{1,0:T(8,128)(2,1)} %bitcast.109, s32[1024]{0:T(1024)S(1)} %fusion.67), kind=kCustom, calls=%fused_computation.clone | custom fusion | bytes 4198400 | tf_op jit(solution)/shard_map/jit(_take)/gather | solution.py:219
  32.8 8.6 %fusion.12 = bf16[1024,2048]{1,0:T(8,128)(2,1)} fusion(bf16[1,1,2048,1024]{3,2,1,0:T(8,128)(2,1)} %param.12, bf16[1024,1024]{1,0:T(8,128)(2,1)S(1)} %gather_fusion.3, pred[1024]{0:T(1024)(128)(4,1)S(1)} %compare_and_fusion.1), kind=kOutput, calls=%fused_computation.24 | convolution fusion | flops 4298113024 | bytes 10486784 | tf_op jit(solution)/shard_map/dot_general | solution.py:218
  45.3 7.7 %gather_fusion.5 = bf16[1024,1024]{1,0:T(8,128)(2,1)S(1)} fusion(bf16[2048,1024]{1,0:T(8,128)(2,1)} %bitcast.110, s32[1024]{0:T(1024)S(1)} %fusion.68), kind=kCustom, calls=%fused_computation.2.clone | custom fusion | bytes 4198400 | tf_op jit(solution)/shard_map/jit(_take)/gather | solution.py:219
  53.1 8.5 %fusion.15 = bf16[1024,2048]{1,0:T(8,128)(2,1)} fusion(bf16[1,1,2048,1024]{3,2,1,0:T(8,128)(2,1)} %param.12, bf16[1024,1024]{1,0:T(8,128)(2,1)S(1)} %gather_fusion.5, pred[1024]{0:T(1024)(128)(4,1)S(1)} %compare_and_fusion), kind=kOutput, calls=%fused_computation.25 | convolution fusion | flops 4298113024 | bytes 10486784 | tf_op jit(solution)/shard_map/dot_general | solution.py:218
  61.6 79.3 %all-to-all-done.1 = bf16[32,32,2048]{2,1,0:T(8,128)(2,1)} async-done(((bf16[32,32,2048]{2,1,0:T(8,128)(2,1)}), bf16[32,32,2048]{2,1,0:T(8,128)(2,1)}, u32[]{:S(2)}, u32[]{:S(2)}) %all-to-all-start.1) | async-done | bytes 4194336 | tf_op jit(solution)/shard_map/all_to_all | solution.py:169
  146.5 20.5 %fusion.28 = bf16[256,128]{1,0:T(8,128)(2,1)S(1)} fusion(f32[]{:T(128)} %bitcast.24, f32[]{:T(128)} %bitcast.25, f32[]{:T(128)} %bitcast.26, f32[]{:T(128)} %bitcast.27, f32[]{:T(128)} %bitcast.28, f32[]{:T(128)} %bitcast.29, f32[]{:T(128)} %bitcast.30, f32[]{:T(128)} %bitcast.31, f32[]{:T(128)} %bitcast.32, f32[]{:T(128)} %bitcast.33, f32[]{:T(128)} %bitcast.34, ...), kind=kLoop, calls=%fused_computation.53 | loop fusion | flops 2326528 | bytes 65668 | tf_op jit(solution)/shard_map/convert_element_type | solution.py:131
  167.0 20.5 %reduce-precision_convert_fusion.2 = bf16[256,128]{1,0:T(8,128)(2,1)S(1)} fusion(f32[]{:T(128)} %bitcast.24, f32[]{:T(128)} %bitcast.25, f32[]{:T(128)} %bitcast.26, f32[]{:T(128)} %bitcast.27, f32[]{:T(128)} %bitcast.28, f32[]{:T(128)} %bitcast.29, f32[]{:T(128)} %bitcast.30, f32[]{:T(128)} %bitcast.31, f32[]{:T(128)} %bitcast.32, f32[]{:T(128)} %bitcast.33, ...), kind=kLoop, calls=%fused_computation.49 | loop fusion | flops 2293760 | bytes 65668 | tf_op jit(solution)/shard_map/convert_element_type | solution.py:131
  187.6 20.5 %fusion.27 = bf16[256,128]{1,0:T(8,128)(2,1)S(1)} fusion(f32[]{:T(128)} %bitcast.56, f32[]{:T(128)} %bitcast.55, f32[]{:T(128)} %bitcast.54, f32[]{:T(128)} %bitcast.53, f32[]{:T(128)} %bitcast.52, f32[]{:T(128)} %bitcast.51, f32[]{:T(128)} %bitcast.50, f32[]{:T(128)} %bitcast.49, f32[]{:T(128)} %bitcast.48, f32[]{:T(128)} %bitcast.47, f32[]{:T(128)} %bitcast.46, ...), kind=kLoop, calls=%fused_computation.52 | loop fusion | flops 2326528 | bytes 65668 | tf_op jit(solution)/shard_map/convert_element_type | solution.py:131
  208.1 20.5 %reduce-precision_convert_fusion.3 = bf16[256,128]{1,0:T(8,128)(2,1)S(1)} fusion(f32[]{:T(128)} %bitcast.56, f32[]{:T(128)} %bitcast.55, f32[]{:T(128)} %bitcast.54, f32[]{:T(128)} %bitcast.53, f32[]{:T(128)} %bitcast.52, f32[]{:T(128)} %bitcast.51, f32[]{:T(128)} %bitcast.50, f32[]{:T(128)} %bitcast.49, f32[]{:T(128)} %bitcast.48, f32[]{:T(128)} %bitcast.47, ...), kind=kLoop, calls=%fused_computation.51 | loop fusion | flops 2293760 | bytes 65668 | tf_op jit(solution)/shard_map/convert_element_type | solution.py:131
  229.7 5.0 gather_fusion.4
  234.7 5.9 %all-to-all-done.2 = bf16[32,32,2048]{2,1,0:T(8,128)(2,1)} async-done(((bf16[32,32,2048]{2,1,0:T(8,128)(2,1)}), bf16[32,32,2048]{2,1,0:T(8,128)(2,1)}, u32[]{:S(2)}, u32[]{:S(2)}) %all-to-all-start.2) | async-done | bytes 4194336 | tf_op jit(solution)/shard_map/all_to_all | solution.py:169
  240.6 5.0 gather_fusion.6
  245.6 4.5 convert_reduce_fusion
  262.9 59.6 %all_gather.6 = f32[512,72]{1,0:T(8,128)S(1)} all-gather(f32[16,72]{1,0:T(8,128)S(1)} %add_convert_fusion), channel_id=1, replica_groups=mesh['inline'=4,'xline'=8] {'inline','xline'}, dimensions={0}, use_global_device_ids=true | all-gather | bytes 152064 | tf_op jit(solution)/shard_map/all_gather | solution.py:186
  332.5 43.8 %all-gather.2.cloned.1.call-done = bf16[4096,2048]{1,0:T(8,128)(2,1)} async-done(((bf16[128,2048]{1,0:T(8,128)(2,1)}), bf16[4096,2048]{1,0:T(8,128)(2,1)}) %all-gather.2.cloned.1.call-update) | async-done | bytes 16777232 | tf_op jit(solution)/shard_map/all_gather | solution.py:240
  376.2 14.6 %gather_fusion.1 = bf16[256,8,2048]{2,1,0:T(8,128)(2,1)} fusion(bf16[512,8,2048]{2,1,0:T(8,128)(2,1)} %bitcast.123, s32[1024]{0:T(1024)S(1)} %pad_clamp_fusion.1), kind=kCustom, calls=%fused_computation.5 | custom fusion | bytes 16778240 | tf_op jit(solution)/shard_map/jit(_take)/gather | solution.py:262
  390.8 14.8 %fusion = f32[2048,1024]{1,0:T(8,128)} fusion(bf16[256,8,2048]{2,1,0:T(8,128)(2,1)} %gather_fusion.1, pred[256]{0:T(512)(128)(4,1)S(1)} %compare_and_fusion.4, bf16[1,1,2048,1024]{3,2,1,0:T(8,128)(2,1)} %param.12), kind=kOutput, calls=%fused_computation.11 | convolution fusion | flops 8594128896 | bytes 20971776 | tf_op jit(solution)/shard_map/dot_general | solution.py:263
  405.6 22.9 %scatter_custom_fusion.2 = f32[2048,1024]{1,0:T(8,128)} fusion(s32[2048]{0:T(1024)S(1)} %bitcast.132, f32[2048,1024]{1,0:T(8,128)} %fusion, f32[]{:T(128)} %constant.62.clone.1), kind=kCustom, calls=%fused_computation.22 | custom fusion | flops 2097152 | bytes 8389120 | tf_op jit(solution)/shard_map/scatter-add | solution.py:271
  435.2 9.5 %collective-permute-done.low_ref = f32[4,64,1024]{2,1,0:T(8,128)S(1)} collective-permute-done((f32[4,64,1024]{2,1,0:T(8,128)S(1)}, f32[4,64,1024]{2,1,0:T(8,128)S(1)}, u32[]{:S(2)}, u32[]{:S(2)}) %collective-permute-start) | collective-permute-done | bytes 1048608 | tf_op jit(solution)/shard_map/ppermute | solution.py:99
  444.8 4.4 collective-permute-done.1.high_ref
  450.1 9.7 %shard_map.86.first_ref.last_ref = f32[32,16,1024]{2,1,0:T(8,128)} custom-call(f32[9]{0:T(128)} %taps_ref.5, f32[32,64,1024]{2,1,0:T(8,128)} %bitcast.111, f32[4,64,1024]{2,1,0:T(8,128)} %copy-done, f32[4,64,1024]{2,1,0:T(8,128)} %copy-done.1), custom_call_target="tpu_custom_call" | custom-call | flops 20971520 | bytes 5242880 | tf_op jit(solution)/shard_map/pallas_call | solution.py:34
  468.2 24.5 %shard_map.87.middle_ref = f32[32,48,1024]{2,1,0:T(8,128)} custom-call(f32[9]{0:T(128)} %taps_ref.5, f32[32,64,1024]{2,1,0:T(8,128)} %bitcast.112, f32[4,64,1024]{2,1,0:T(8,128)} %copy-done, f32[4,64,1024]{2,1,0:T(8,128)} %copy-done.1), custom_call_target="tpu_custom_call" | custom-call | flops 62914560 | bytes 15728640 | tf_op jit(solution)/shard_map/pallas_call | solution.py:34
  494.5 20.4 %shard_map.88 = f32[32,64,1024]{2,1,0:T(8,128)} custom-call(f32[9]{0:T(128)} %taps_ref.5, f32[32,16,1024]{2,1,0:T(8,128)} %shard_map.86.first_ref.last_ref, f32[32,48,1024]{2,1,0:T(8,128)} %shard_map.87.middle_ref, f32[32,16,1024]{2,1,0:T(8,128)} %shard_map.86.first_ref.last_ref, f32[32,4,1024]{2,1,0:T(4,128)} %copy-done.5, f32[32,4,1024]{2,1,0:T(4,128)} %copy-done.4), custom_call_target="tpu_custom_call" | custom-call | flops 37748736 | bytes 18454936 | tf_op jit(solution)/shard_map/pallas_call | solution.py:71
  (120 shorter events, 54.9 us)
Async XLA Ops:
  41.4 99.6 %all-to-all-start.1 = ((bf16[32,32,2048]{2,1,0:T(8,128)(2,1)}), bf16[32,32,2048]{2,1,0:T(8,128)(2,1)}, u32[]{:S(2)}, u32[]{:S(2)}) async-start(bf16[32,32,2048]{2,1,0:T(8,128)(2,1)} %bitcast.125), calls=%async_computation.1 | async-start | bytes 8388608 | tf_op jit(solution)/shard_map/all_to_all | solution.py:169
  140.9 4.1 copy-start.3
  140.9 87.7 %copy-start.6 = (bf16[128,2048]{1,0:T(8,128)(2,1)S(1)}, bf16[128,2048]{1,0:T(8,128)(2,1)}, u32[]{:S(2)}) copy-start(bf16[128,2048]{1,0:T(8,128)(2,1)} %param.13) | copy-start | bytes 1572868
  140.9 99.7 %all-to-all-start.2 = ((bf16[32,32,2048]{2,1,0:T(8,128)(2,1)}), bf16[32,32,2048]{2,1,0:T(8,128)(2,1)}, u32[]{:S(2)}, u32[]{:S(2)}) async-start(bf16[32,32,2048]{2,1,0:T(8,128)(2,1)} %bitcast.124), calls=%async_computation.2 | async-start | bytes 8388608 | tf_op jit(solution)/shard_map/all_to_all | solution.py:169
  144.8 231.4 %all-gather.2.cloned.1.call-start = ((), (), s32[]{:S(2)}) async-start(), calls=%async_computation.3 | async-start | bytes 17301504 | tf_op jit(solution)/shard_map/all_gather | solution.py:240
  259.9 1.2 copy-start.2
  260.4 2.3 copy-start.7
  430.1 14.6 %collective-permute-start = (f32[4,64,1024]{2,1,0:T(8,128)S(1)}, f32[4,64,1024]{2,1,0:T(8,128)S(1)}, u32[]{:S(2)}, u32[]{:S(2)}) collective-permute-start(f32[4,64,1024]{2,1,0:T(8,128)S(1)} %bitcast.128), channel_id=1, source_target_pairs={{0,8},{8,16},{16,24},{1,9},{9,17},{17,25},{2,10},{10,18},{18,26},{... | collective-permute-start | bytes 3145736 | tf_op jit(solution)/shard_map/ppermute | solution.py:99
  433.0 16.1 %collective-permute-start.1 = (f32[4,64,1024]{2,1,0:T(8,128)S(1)}, f32[4,64,1024]{2,1,0:T(8,128)S(1)}, u32[]{:S(2)}, u32[]{:S(2)}) collective-permute-start(f32[4,64,1024]{2,1,0:T(8,128)S(1)} %bitcast.127), channel_id=1, source_target_pairs={{8,0},{16,8},{24,16},{9,1},{17,9},{25,17},{10,2},{18,10},{26,18},{... | collective-permute-start | bytes 3145736 | tf_op jit(solution)/shard_map/ppermute | solution.py:102
  444.8 4.4 copy-start
  449.1 1.0 copy-start.1
  461.6 31.2 %collective-permute-start.3 = (f32[32,4,1024]{2,1,0:T(4,128)S(1)}, f32[32,4,1024]{2,1,0:T(4,128)S(1)}, u32[]{:S(2)}, u32[]{:S(2)}) collective-permute-start(f32[32,4,1024]{2,1,0:T(4,128)S(1)} %get-tuple-element.32), channel_id=1, source_target_pairs={{1,0},{2,1},{3,2},{4,3},{5,4},{6,5},{7,6},{9,8},{10,9},{11,10},{12... | collective-permute-start | bytes 1572872 | tf_op jit(solution)/shard_map/ppermute | solution.py:102
  462.9 29.9 %collective-permute-start.2 = (f32[32,4,1024]{2,1,0:T(4,128)S(1)}, f32[32,4,1024]{2,1,0:T(4,128)S(1)}, u32[]{:S(2)}, u32[]{:S(2)}) collective-permute-start(f32[32,4,1024]{2,1,0:T(4,128)S(1)} %get-tuple-element.33), channel_id=1, source_target_pairs={{0,1},{1,2},{2,3},{3,4},{4,5},{5,6},{6,7},{8,9},{9,10},{10,11},{11... | collective-permute-start | bytes 1572872 | tf_op jit(solution)/shard_map/ppermute | solution.py:99
  492.8 0.9 copy-start.4
  493.6 0.8 copy-start.5
Sparse Core Ops, SparseCore 0:
  262.8 113.4 all-gather.1

commit v10 on v8

--- a/solution.py
+++ b/solution.py
@@ -13,18 +13,6 @@
     ext_ref[0:HW] = low_ref[...]
     ext_ref[HW:HW + nx] = main_ref[...]
     ext_ref[HW + nx:] = high_ref[...]
-    depth = ext_ref.shape[2]
-    x = ext_ref[...]
-    lane = lax.broadcasted_iota(jnp.int32, x.shape, 2)
-    acc = taps_ref[HW] * x
-    for j in range(2 * HW + 1):
-        if j == HW:
-            continue
-        shifted = pltpu.roll(x, (HW - j) % depth, 2)
-        source = lane + (j - HW)
-        keep = (source >= 0) & (source < depth)
-        acc = acc + taps_ref[j] * jnp.where(keep, shifted, 0.0)
-    ext_ref[...] = acc
     out = taps_ref[0] * ext_ref[0:nx]
     for j in range(1, 2 * HW + 1):
         out = out + taps_ref[j] * ext_ref[j:j + nx]
@@ -262,10 +250,12 @@
         (jnp.arange(relevant) < found)[:, None], jnp.take(cells_all, chosen, axis=0), cell_count
     )
     picked = jnp.take(adjoint_all.reshape(all_blocks, per_block, samples), chosen, axis=0)
-    per_trace = jnp.dot(
-        picked.reshape(relevant * per_block, samples),
-        weight_matrix,
-        preferred_element_type=jnp.float32,
+    weight_wide = jnp.pad(weight_matrix.astype(jnp.float32), ((0, 0), (HW, HW)))
+    smoothed_weights = filter_padded(weight_wide, taps, 1)
+    w_high, w_low = split(smoothed_weights)
+    flat = picked.reshape(relevant * per_block, samples)
+    per_trace = jnp.dot(flat, w_high, preferred_element_type=jnp.float32) + jnp.dot(
+        flat, w_low, preferred_element_type=jnp.float32
     )
     raw_gradient = (
         jnp.zeros((cell_count, depth_len), jnp.float32)

time: 530 us -> 524 us (0.989)
  waiting for transfers between devices: 143 us -> 110 us
  other arithmetic: 115 us -> 144 us
  Pallas kernels: 54 us -> 32.9 us
  matrix products: 34.5 us -> 48.4 us
  local copies, waits for them, and re-layouts: 68.3 us -> 73.9 us
    all_gather x1, waiting for transfers between devices: 43.8 us -> 10.5 us  [local(): adjoint_all = lax.all_gather(adjoint, axes, axis=0, tiled=True)]
    add x0 -> x1, other arithmetic: none -> 24.6 us  [filter_padded(): result + taps[offset] * lax.slice_in_dim(padded, offset, offset + length,...]
    pallas_call x2, Pallas kernels: 33.6 us -> 12.5 us  [smooth_zx(): pl.pallas_call(_zx_kernel, grid=(len(blocks),), in_specs=[pl.BlockSpec(me...]
    dot_general x1 -> x2, matrix products: 14.8 us -> 27.5 us  [the longest x1 16.4 us: local(): jnp.dot(flat, w_low, preferred_element_type=jnp.float32)]
  transfers between devices with their start and end apart: 7 -> 7, of which waited for: 5 -> 5; matrix products, arithmetic and copies ran while one was open for 23% -> 29% of each run, Pallas kernels for 5% -> 2%
where the time goes in v10:
time: 524 us; the launch traced here: 516 us
  other arithmetic  144 us (27%)
  waiting for transfers between devices  110 us (21%)
  local copies, waits for them, and re-layouts  73.9 us (14%)
  blocking collectives  73.2 us (14%)
  matrix products  48.4 us (9%)
  Pallas kernels  32.9 us (6%)
  starting transfers between devices  18.1 us (3%)
  between operations  14.8 us (3%)
    all_to_all x2, waiting for transfers between devices, traverse(): lax.all_to_all(blocks, ('inline', 'xline'), split_axis=0, concat_axis=0,...  85.3 us
    convert_element_type x7, other arithmetic, split(): return (high.astype(jnp.bfloat16), (x - high).astype(jnp.bfloat16))  83.6 us
    all_gather x1, blocking collectives, local(): tables_all = jnp.round(lax.all_gather(tables, axes, axis=0, tiled=True))  59.6 us
    add x1, other arithmetic, filter_padded(): result + taps[offset] * lax.slice_in_dim(padded, offset, offset + length,...  24.6 us
    scatter-add x1, other arithmetic, local(): raw_gradient = jnp.zeros((cell_count, depth_len), jnp.float32).at[cells.r...  23.1 us
    pallas_call x1, Pallas kernels, smooth_y(): pl.pallas_call(_y_kernel, grid=(nx // tx,), in_specs=[pl.BlockSpec(memory...  20.4 us
    dot_general x2, matrix products, local(): lax.dot_general(jnp.take(tile_rows, wanted, axis=0), weight_matrix, contr...  17.1 us
    dot_general x1, matrix products, local(): jnp.dot(flat, w_low, preferred_element_type=jnp.float32)  16.4 us
  transfers between devices with their start and end apart: 7, of which 5 were waited for; matrix products, arithmetic and copies ran while one was open for 29% of the time, Pallas kernels for 2%

profile of v10, /device:TPU:1, one launch (start us, length us, event | category | flops | bytes accessed | tf_op | source)
XLA Modules:
  0.0 515.7 jit_solution(9831842168062261156)
XLA Ops:
  11.1 13.6 %all_to_all.19 = s32[32,1,64]{2,1,0:T(1,128)S(1)} all-to-all(s32[32,1,64]{2,1,0:T(1,128)S(1)} %bitcast.140), channel_id=1, replica_groups=mesh['inline'=4,'xline'=8] {'inline','xline'}, dimensions={0} | all-to-all | bytes 16384 | tf_op jit(solution)/shard_map/all_to_all | solution.py:192
  25.1 7.7 %gather_fusion.3 = bf16[1024,1024]{1,0:T(8,128)(2,1)S(1)} fusion(bf16[2048,1024]{1,0:T(8,128)(2,1)} %bitcast.118, s32[1024]{0:T(1024)S(1)} %fusion.82), kind=kCustom, calls=%fused_computation.clone | custom fusion | bytes 4198400 | tf_op jit(solution)/shard_map/jit(_take)/gather | solution.py:209
  32.8 8.6 %fusion.27 = bf16[1024,2048]{1,0:T(8,128)(2,1)} fusion(bf16[1,1,2048,1024]{3,2,1,0:T(8,128)(2,1)} %param.12, bf16[1024,1024]{1,0:T(8,128)(2,1)S(1)} %gather_fusion.3, pred[1024]{0:T(1024)(128)(4,1)S(1)} %compare_and_fusion.1), kind=kOutput, calls=%fused_computation.50 | convolution fusion | flops 4298113024 | bytes 10486784 | tf_op jit(solution)/shard_map/dot_general | solution.py:208
  45.3 7.7 %gather_fusion.5 = bf16[1024,1024]{1,0:T(8,128)(2,1)S(1)} fusion(bf16[2048,1024]{1,0:T(8,128)(2,1)} %bitcast.119, s32[1024]{0:T(1024)S(1)} %fusion.83), kind=kCustom, calls=%fused_computation.2.clone | custom fusion | bytes 4198400 | tf_op jit(solution)/shard_map/jit(_take)/gather | solution.py:209
  53.1 8.5 %fusion.30 = bf16[1024,2048]{1,0:T(8,128)(2,1)} fusion(bf16[1,1,2048,1024]{3,2,1,0:T(8,128)(2,1)} %param.12, bf16[1024,1024]{1,0:T(8,128)(2,1)S(1)} %gather_fusion.5, pred[1024]{0:T(1024)(128)(4,1)S(1)} %compare_and_fusion), kind=kOutput, calls=%fused_computation.51 | convolution fusion | flops 4298113024 | bytes 10486784 | tf_op jit(solution)/shard_map/dot_general | solution.py:208
  61.6 79.3 %all-to-all-done.1 = bf16[32,32,2048]{2,1,0:T(8,128)(2,1)} async-done(((bf16[32,32,2048]{2,1,0:T(8,128)(2,1)}), bf16[32,32,2048]{2,1,0:T(8,128)(2,1)}, u32[]{:S(2)}, u32[]{:S(2)}) %all-to-all-start.1) | async-done | bytes 4194336 | tf_op jit(solution)/shard_map/all_to_all | solution.py:159
  146.3 20.5 %fusion.43 = bf16[256,128]{1,0:T(8,128)(2,1)S(1)} fusion(f32[]{:T(128)} %bitcast.24, f32[]{:T(128)} %bitcast.25, f32[]{:T(128)} %bitcast.26, f32[]{:T(128)} %bitcast.27, f32[]{:T(128)} %bitcast.28, f32[]{:T(128)} %bitcast.29, f32[]{:T(128)} %bitcast.30, f32[]{:T(128)} %bitcast.31, f32[]{:T(128)} %bitcast.32, f32[]{:T(128)} %bitcast.33, f32[]{:T(128)} %bitcast.34, ...), kind=kLoop, calls=%fused_computation.79 | loop fusion | flops 2326528 | bytes 65668 | tf_op jit(solution)/shard_map/convert_element_type | solution.py:121
  166.9 20.5 %reduce-precision_convert_fusion.4 = bf16[256,128]{1,0:T(8,128)(2,1)S(1)} fusion(f32[]{:T(128)} %bitcast.24, f32[]{:T(128)} %bitcast.25, f32[]{:T(128)} %bitcast.26, f32[]{:T(128)} %bitcast.27, f32[]{:T(128)} %bitcast.28, f32[]{:T(128)} %bitcast.29, f32[]{:T(128)} %bitcast.30, f32[]{:T(128)} %bitcast.31, f32[]{:T(128)} %bitcast.32, f32[]{:T(128)} %bitcast.33, ...), kind=kLoop, calls=%fused_computation.75 | loop fusion | flops 2293760 | bytes 65668 | tf_op jit(solution)/shard_map/convert_element_type | solution.py:121
  187.4 20.5 %fusion.42 = bf16[256,128]{1,0:T(8,128)(2,1)S(1)} fusion(f32[]{:T(128)} %bitcast.56, f32[]{:T(128)} %bitcast.55, f32[]{:T(128)} %bitcast.54, f32[]{:T(128)} %bitcast.53, f32[]{:T(128)} %bitcast.52, f32[]{:T(128)} %bitcast.51, f32[]{:T(128)} %bitcast.50, f32[]{:T(128)} %bitcast.49, f32[]{:T(128)} %bitcast.48, f32[]{:T(128)} %bitcast.47, f32[]{:T(128)} %bitcast.46, ...), kind=kLoop, calls=%fused_computation.78 | loop fusion | flops 2326528 | bytes 65668 | tf_op jit(solution)/shard_map/convert_element_type | solution.py:121
  208.0 20.5 %reduce-precision_convert_fusion.5 = bf16[256,128]{1,0:T(8,128)(2,1)S(1)} fusion(f32[]{:T(128)} %bitcast.56, f32[]{:T(128)} %bitcast.55, f32[]{:T(128)} %bitcast.54, f32[]{:T(128)} %bitcast.53, f32[]{:T(128)} %bitcast.52, f32[]{:T(128)} %bitcast.51, f32[]{:T(128)} %bitcast.50, f32[]{:T(128)} %bitcast.49, f32[]{:T(128)} %bitcast.48, f32[]{:T(128)} %bitcast.47, ...), kind=kLoop, calls=%fused_computation.77 | loop fusion | flops 2293760 | bytes 65668 | tf_op jit(solution)/shard_map/convert_element_type | solution.py:121
  229.6 5.0 gather_fusion.4
  234.6 5.9 %all-to-all-done.2 = bf16[32,32,2048]{2,1,0:T(8,128)(2,1)} async-done(((bf16[32,32,2048]{2,1,0:T(8,128)(2,1)}), bf16[32,32,2048]{2,1,0:T(8,128)(2,1)}, u32[]{:S(2)}, u32[]{:S(2)}) %all-to-all-start.2) | async-done | bytes 4194336 | tf_op jit(solution)/shard_map/all_to_all | solution.py:159
  240.5 5.0 gather_fusion.6
  265.5 59.6 %all_gather.6 = f32[512,72]{1,0:T(8,128)S(1)} all-gather(f32[16,72]{1,0:T(8,128)S(1)} %add_convert_fusion), channel_id=1, replica_groups=mesh['inline'=4,'xline'=8] {'inline','xline'}, dimensions={0}, use_global_device_ids=true | all-gather | bytes 152064 | tf_op jit(solution)/shard_map/all_gather | solution.py:176
  331.3 6.1 %gather_fusion.2 = s32[512,8]{1,0:T(8,128)S(1)} fusion(s32[512,8,8]{1,2,0:T(8,128)} %copy.89, s32[512]{0:T(512)S(1)} %bitcast.122), kind=kCustom, calls=%fused_computation.6 | custom fusion | bytes 36864 | tf_op jit(solution)/shard_map/jit(take_along_axis)/gather | solution.py:246
  343.8 24.6 %fusion.8 = f32[2048,1024]{1,0:T(8,128)} fusion(f32[2048,1024]{1,0:T(8,128)S(1)} %bitcast_convert_fusion, f32[]{:T(128)} %bitcast.73, f32[]{:T(128)} %bitcast.72, f32[]{:T(128)} %bitcast.71, f32[]{:T(128)} %bitcast.70, f32[]{:T(128)} %bitcast.69, f32[]{:T(128)} %bitcast.68, f32[]{:T(128)} %bitcast.67, f32[]{:T(128)} %bitcast.66, f32[]{:T(128)} %bitcast.65), kind=kLoop, calls=%fused_computation.28 | loop fusion | flops 35651584 | bytes 16777252 | tf_op jit(solution)/shard_map/add | solution.py:152
  368.3 10.5 %all-gather.2.cloned.1.call-done = bf16[4096,2048]{1,0:T(8,128)(2,1)} async-done(((bf16[128,2048]{1,0:T(8,128)(2,1)}), bf16[4096,2048]{1,0:T(8,128)(2,1)}) %all-gather.2.cloned.1.call-update) | async-done | bytes 16777232 | tf_op jit(solution)/shard_map/all_gather | solution.py:230
  378.8 14.2 %gather_fusion.1 = bf16[256,8,2048]{2,1,0:T(8,128)(2,1)} fusion(bf16[512,8,2048]{2,1,0:T(8,128)(2,1)} %bitcast.132, s32[1024]{0:T(1024)S(1)} %pad_clamp_fusion.1), kind=kCustom, calls=%fused_computation.5 | custom fusion | bytes 16778240 | tf_op jit(solution)/shard_map/jit(_take)/gather | solution.py:252
  393.0 16.4 %fusion.19 = f32[2048,1024]{1,0:T(8,128)} fusion(f32[2048,1024]{1,0:T(8,128)} %fusion.8, bf16[256,8,2048]{2,1,0:T(8,128)(2,1)} %gather_fusion.1, pred[2048]{0:T(1024)(128)(4,1)S(1)} %broadcast_in_dim.240), kind=kOutput, calls=%fused_computation.41 | convolution fusion | flops 8600420352 | bytes 25167872 | tf_op jit(solution)/shard_map/dot_general | solution.py:257
  409.4 11.1 %fusion.21 = f32[2048,1024]{1,0:T(8,128)} fusion(f32[2048,1024]{1,0:T(8,128)S(1)} %copy-done, bf16[256,8,2048]{2,1,0:T(8,128)(2,1)S(1)} %copy-done.1, pred[2048]{0:T(1024)(128)(4,1)S(1)} %broadcast_in_dim.240), kind=kOutput, calls=%fused_computation.42 | convolution fusion | flops 8598323200 | bytes 25167872 | tf_op jit(solution)/shard_map/dot_general | solution.py:257
  420.6 23.1 %scatter_custom_fusion.2 = f32[2048,1024]{1,0:T(8,128)} fusion(s32[2048]{0:T(1024)S(1)} %bitcast.141, f32[2048,1024]{1,0:T(8,128)} %fusion.21, f32[2048,1024]{1,0:T(8,128)} %fusion.19, f32[]{:T(128)} %constant.62.clone.1), kind=kCustom, calls=%fused_computation.39 | custom fusion | flops 4194304 | bytes 25165828 | tf_op jit(solution)/shard_map/scatter-add | solution.py:263
  450.5 9.8 %collective-permute-done.low_ref = f32[4,64,1024]{2,1,0:T(8,128)S(1)} collective-permute-done((f32[4,64,1024]{2,1,0:T(8,128)S(1)}, f32[4,64,1024]{2,1,0:T(8,128)S(1)}, u32[]{:S(2)}, u32[]{:S(2)}) %collective-permute-start) | collective-permute-done | bytes 1048608 | tf_op jit(solution)/shard_map/ppermute | solution.py:89
  477.8 8.8 %shard_map.87.middle_ref = f32[32,48,1024]{2,1,0:T(8,128)} custom-call(f32[9]{0:T(128)} %taps_ref.5, f32[32,64,1024]{2,1,0:T(8,128)} %bitcast.121, f32[4,64,1024]{2,1,0:T(8,128)} %copy-done.2, f32[4,64,1024]{2,1,0:T(8,128)} %collective-permute-done.1.high_ref), custom_call_target="tpu_custom_call" | custom-call | flops 62914560 | bytes 15728640 | tf_op jit(solution)/shard_map/pallas_call | solution.py:24
  488.3 20.4 %shard_map.88 = f32[32,64,1024]{2,1,0:T(8,128)} custom-call(f32[9]{0:T(128)} %taps_ref.5, f32[32,16,1024]{2,1,0:T(8,128)} %shard_map.86.first_ref.last_ref, f32[32,48,1024]{2,1,0:T(8,128)} %shard_map.87.middle_ref, f32[32,16,1024]{2,1,0:T(8,128)} %shard_map.86.first_ref.last_ref, f32[32,4,1024]{2,1,0:T(4,128)} %copy-done.5, f32[32,4,1024]{2,1,0:T(4,128)} %copy-done.4), custom_call_target="tpu_custom_call" | custom-call | flops 37748736 | bytes 18454936 | tf_op jit(solution)/shard_map/pallas_call | solution.py:61
  (128 shorter events, 72.8 us)
Async XLA Ops:
  41.4 99.6 %all-to-all-start.1 = ((bf16[32,32,2048]{2,1,0:T(8,128)(2,1)}), bf16[32,32,2048]{2,1,0:T(8,128)(2,1)}, u32[]{:S(2)}, u32[]{:S(2)}) async-start(bf16[32,32,2048]{2,1,0:T(8,128)(2,1)} %bitcast.134), calls=%async_computation.1 | async-start | bytes 8388608 | tf_op jit(solution)/shard_map/all_to_all | solution.py:159
  61.6 83.3 %copy-start.3 = (f32[33]{0:T(128)S(1)}, f32[33]{0:T(128)}, u32[]{:S(2)}) copy-start(f32[33]{0:T(128)} %param.14) | copy-start | bytes 400
  61.6 166.9 %copy-start.6 = (bf16[128,2048]{1,0:T(8,128)(2,1)S(1)}, bf16[128,2048]{1,0:T(8,128)(2,1)}, u32[]{:S(2)}) copy-start(bf16[128,2048]{1,0:T(8,128)(2,1)} %param.13) | copy-start | bytes 1572868
  140.9 99.5 %all-to-all-start.2 = ((bf16[32,32,2048]{2,1,0:T(8,128)(2,1)}), bf16[32,32,2048]{2,1,0:T(8,128)(2,1)}, u32[]{:S(2)}, u32[]{:S(2)}) async-start(bf16[32,32,2048]{2,1,0:T(8,128)(2,1)} %bitcast.133), calls=%async_computation.2 | async-start | bytes 8388608 | tf_op jit(solution)/shard_map/all_to_all | solution.py:159
  144.7 234.1 %all-gather.2.cloned.1.call-start = ((), (), s32[]{:S(2)}) async-start(), calls=%async_computation.3 | async-start | bytes 17301504 | tf_op jit(solution)/shard_map/all_gather | solution.py:230
  258.4 6.8 %copy-start.8 = (s32[128,8]{0,1:T(8,128)S(1)}, s32[128,8]{0,1:T(8,128)}, u32[]{:S(2)}) copy-start(s32[128,8]{0,1:T(8,128)} %param.17) | copy-start | bytes 12292
  262.1 77.8 %copy-start.7 = (f32[9]{0:T(128)S(1)}, f32[9]{0:T(128)}, u32[]{:S(2)}) copy-start(f32[9]{0:T(128)} %taps_ref.5) | copy-start | bytes 112
  393.0 16.4 %copy-start = (f32[2048,1024]{1,0:T(8,128)S(1)}, f32[2048,1024]{1,0:T(8,128)}, u32[]{:S(2)}) copy-start(f32[2048,1024]{1,0:T(8,128)} %fusion.8) | copy-start | bytes 25165828
  393.0 16.4 %copy-start.1 = (bf16[256,8,2048]{2,1,0:T(8,128)(2,1)S(1)}, bf16[256,8,2048]{2,1,0:T(8,128)(2,1)}, u32[]{:S(2)}) copy-start(bf16[256,8,2048]{2,1,0:T(8,128)(2,1)} %gather_fusion.1) | copy-start | bytes 25165828
  445.3 14.9 %collective-permute-start = (f32[4,64,1024]{2,1,0:T(8,128)S(1)}, f32[4,64,1024]{2,1,0:T(8,128)S(1)}, u32[]{:S(2)}, u32[]{:S(2)}) collective-permute-start(f32[4,64,1024]{2,1,0:T(8,128)S(1)} %bitcast.137), channel_id=1, source_target_pairs={{0,8},{8,16},{16,24},{1,9},{9,17},{17,25},{2,10},{10,18},{18,26},{... | collective-permute-start | bytes 3145736 | tf_op jit(solution)/shard_map/ppermute | solution.py:89
  448.5 16.4 %collective-permute-start.1 = (f32[4,64,1024]{2,1,0:T(8,128)S(1)}, f32[4,64,1024]{2,1,0:T(8,128)}, u32[]{:S(2)}, u32[]{:S(2)}) collective-permute-start(f32[4,64,1024]{2,1,0:T(8,128)S(1)} %bitcast.136), channel_id=1, source_target_pairs={{8,0},{16,8},{24,16},{9,1},{17,9},{25,17},{10,2},{18,10},{26,18},{... | collective-permute-start | bytes 3145736 | tf_op jit(solution)/shard_map/ppermute | solution.py:92
  460.3 4.7 copy-start.2
  471.2 15.4 %collective-permute-start.3 = (f32[32,4,1024]{2,1,0:T(4,128)}, f32[32,4,1024]{2,1,0:T(4,128)S(1)}, u32[]{:S(2)}, u32[]{:S(2)}) collective-permute-start(f32[32,4,1024]{2,1,0:T(4,128)} %get-tuple-element.32), channel_id=1, source_target_pairs={{1,0},{2,1},{3,2},{4,3},{5,4},{6,5},{7,6},{9,8},{10,9},{11,10},{12... | collective-permute-start | bytes 1572872 | tf_op jit(solution)/shard_map/ppermute | solution.py:92
  472.5 14.2 %collective-permute-start.2 = (f32[32,4,1024]{2,1,0:T(4,128)S(1)}, f32[32,4,1024]{2,1,0:T(4,128)S(1)}, u32[]{:S(2)}, u32[]{:S(2)}) collective-permute-start(f32[32,4,1024]{2,1,0:T(4,128)S(1)} %get-tuple-element.33), channel_id=1, source_target_pairs={{0,1},{1,2},{2,3},{3,4},{4,5},{5,6},{6,7},{8,9},{9,10},{10,11},{11... | collective-permute-start | bytes 1572872 | tf_op jit(solution)/shard_map/ppermute | solution.py:89
  486.7 0.8 copy-start.4
  487.5 0.8 copy-start.5
Sparse Core Ops, SparseCore 0:
  265.3 113.4 all-gather.1

commit v11 on v10

--- a/solution.py
+++ b/solution.py
@@ -252,10 +252,9 @@
     picked = jnp.take(adjoint_all.reshape(all_blocks, per_block, samples), chosen, axis=0)
     weight_wide = jnp.pad(weight_matrix.astype(jnp.float32), ((0, 0), (HW, HW)))
     smoothed_weights = filter_padded(weight_wide, taps, 1)
-    w_high, w_low = split(smoothed_weights)
     flat = picked.reshape(relevant * per_block, samples)
-    per_trace = jnp.dot(flat, w_high, preferred_element_type=jnp.float32) + jnp.dot(
-        flat, w_low, preferred_element_type=jnp.float32
+    per_trace = jnp.dot(
+        flat, smoothed_weights.astype(jnp.bfloat16), preferred_element_type=jnp.float32
     )
     raw_gradient = (
         jnp.zeros((cell_count, depth_len), jnp.float32)

time: 524 us -> 550 us (1.050)
  waiting for transfers between devices: 110 us -> 136 us
  matrix products: 48.4 us -> 74.1 us
  other arithmetic: 144 us -> 123 us
    dot_general x2 -> x1, matrix products: 27.5 us -> 54.5 us  [local(): jnp.dot(flat, smoothed_weights.astype(jnp.bfloat16), preferred_element_ty...]
    all_gather x1, waiting for transfers between devices: 10.5 us -> 36.4 us  [local(): adjoint_all = lax.all_gather(adjoint, axes, axis=0, tiled=True)]
    add x1 -> x0, other arithmetic: 24.6 us -> none  [filter_padded(): result + taps[offset] * lax.slice_in_dim(padded, offset, offset + length,...]
  transfers between devices with their start and end apart: 7 -> 7, of which waited for: 5 -> 6; matrix products, arithmetic and copies ran while one was open for 29% -> 23% of each run, Pallas kernels for 2% -> 2%
where the time goes in v11:
time: 550 us; the launch traced here: 541 us
  waiting for transfers between devices  136 us (25%)
  other arithmetic  123 us (22%)
  matrix products  74.1 us (13%)
  blocking collectives  73.3 us (13%)
  local copies, waits for them, and re-layouts  70.3 us (13%)
  Pallas kernels  32.7 us (6%)
  starting transfers between devices  16.7 us (3%)
  between operations  15.1 us (3%)
    convert_element_type x7, other arithmetic, split(): return (high.astype(jnp.bfloat16), (x - high).astype(jnp.bfloat16))  85 us
    all_to_all x2, waiting for transfers between devices, traverse(): lax.all_to_all(blocks, ('inline', 'xline'), split_axis=0, concat_axis=0,...  84.7 us
    all_gather x1, blocking collectives, local(): tables_all = jnp.round(lax.all_gather(tables, axes, axis=0, tiled=True))  59.7 us
    dot_general x1, matrix products, local(): jnp.dot(flat, smoothed_weights.astype(jnp.bfloat16), preferred_element_ty...  54.5 us
    all_gather x1, waiting for transfers between devices, local(): adjoint_all = lax.all_gather(adjoint, axes, axis=0, tiled=True)  36.4 us
    scatter-add x1, other arithmetic, local(): raw_gradient = jnp.zeros((cell_count, depth_len), jnp.float32).at[cells.r...  23.1 us
    pallas_call x1, Pallas kernels, smooth_y(): pl.pallas_call(_y_kernel, grid=(nx // tx,), in_specs=[pl.BlockSpec(memory...  20.4 us
    dot_general x2, matrix products, local(): lax.dot_general(jnp.take(tile_rows, wanted, axis=0), weight_matrix, contr...  17.1 us
  transfers between devices with their start and end apart: 7, of which 6 were waited for; matrix products, arithmetic and copies ran while one was open for 23% of the time, Pallas kernels for 2%

profile of v11, /device:TPU:1, one launch (start us, length us, event | category | flops | bytes accessed | tf_op | source)
XLA Modules:
  0.0 541.2 jit_solution(1125609757394771906)
XLA Ops:
  11.1 13.6 %all_to_all.19 = s32[32,1,64]{2,1,0:T(1,128)S(1)} all-to-all(s32[32,1,64]{2,1,0:T(1,128)S(1)} %bitcast.137), channel_id=1, replica_groups=mesh['inline'=4,'xline'=8] {'inline','xline'}, dimensions={0} | all-to-all | bytes 16384 | tf_op jit(solution)/shard_map/all_to_all | solution.py:192
  25.1 7.7 %gather_fusion.5 = bf16[1024,1024]{1,0:T(8,128)(2,1)S(1)} fusion(bf16[2048,1024]{1,0:T(8,128)(2,1)} %bitcast.115, s32[1024]{0:T(1024)S(1)} %fusion.83), kind=kCustom, calls=%fused_computation.2.clone | custom fusion | bytes 4198400 | tf_op jit(solution)/shard_map/jit(_take)/gather | solution.py:209
  32.8 8.5 %fusion.30 = bf16[1024,2048]{1,0:T(8,128)(2,1)} fusion(bf16[1,1,2048,1024]{3,2,1,0:T(8,128)(2,1)} %param.12, bf16[1024,1024]{1,0:T(8,128)(2,1)S(1)} %gather_fusion.5, pred[1024]{0:T(1024)(128)(4,1)S(1)} %compare_and_fusion), kind=kOutput, calls=%fused_computation.49 | convolution fusion | flops 4298113024 | bytes 10486784 | tf_op jit(solution)/shard_map/dot_general | solution.py:208
  45.3 7.7 %gather_fusion.3 = bf16[1024,1024]{1,0:T(8,128)(2,1)S(1)} fusion(bf16[2048,1024]{1,0:T(8,128)(2,1)} %bitcast.116, s32[1024]{0:T(1024)S(1)} %fusion.82), kind=kCustom, calls=%fused_computation.clone | custom fusion | bytes 4198400 | tf_op jit(solution)/shard_map/jit(_take)/gather | solution.py:209
  53.1 8.5 %fusion.27 = bf16[1024,2048]{1,0:T(8,128)(2,1)} fusion(bf16[1,1,2048,1024]{3,2,1,0:T(8,128)(2,1)} %param.12, bf16[1024,1024]{1,0:T(8,128)(2,1)S(1)} %gather_fusion.3, pred[1024]{0:T(1024)(128)(4,1)S(1)} %compare_and_fusion.1), kind=kOutput, calls=%fused_computation.48 | convolution fusion | flops 4298113024 | bytes 10486784 | tf_op jit(solution)/shard_map/dot_general | solution.py:208
  61.6 79.4 %all-to-all-done.2 = bf16[32,32,2048]{2,1,0:T(8,128)(2,1)} async-done(((bf16[32,32,2048]{2,1,0:T(8,128)(2,1)}), bf16[32,32,2048]{2,1,0:T(8,128)(2,1)}, u32[]{:S(2)}, u32[]{:S(2)}) %all-to-all-start.2) | async-done | bytes 4194336 | tf_op jit(solution)/shard_map/all_to_all | solution.py:159
  146.5 20.7 %reduce-precision_convert_fusion.3 = bf16[256,128]{1,0:T(8,128)(2,1)S(1)} fusion(f32[]{:T(128)} %bitcast.56, f32[]{:T(128)} %bitcast.55, f32[]{:T(128)} %bitcast.54, f32[]{:T(128)} %bitcast.53, f32[]{:T(128)} %bitcast.52, f32[]{:T(128)} %bitcast.51, f32[]{:T(128)} %bitcast.50, f32[]{:T(128)} %bitcast.49, f32[]{:T(128)} %bitcast.48, f32[]{:T(128)} %bitcast.47, ...), kind=kLoop, calls=%fused_computation.75 | loop fusion | flops 2293760 | bytes 65668 | tf_op jit(solution)/shard_map/convert_element_type | solution.py:121
  167.1 20.7 %fusion.42 = bf16[256,128]{1,0:T(8,128)(2,1)S(1)} fusion(f32[]{:T(128)} %bitcast.56, f32[]{:T(128)} %bitcast.55, f32[]{:T(128)} %bitcast.54, f32[]{:T(128)} %bitcast.53, f32[]{:T(128)} %bitcast.52, f32[]{:T(128)} %bitcast.51, f32[]{:T(128)} %bitcast.50, f32[]{:T(128)} %bitcast.49, f32[]{:T(128)} %bitcast.48, f32[]{:T(128)} %bitcast.47, f32[]{:T(128)} %bitcast.46, ...), kind=kLoop, calls=%fused_computation.76 | loop fusion | flops 2326528 | bytes 65668 | tf_op jit(solution)/shard_map/convert_element_type | solution.py:121
  188.8 20.7 %reduce-precision_convert_fusion.2 = bf16[256,128]{1,0:T(8,128)(2,1)S(1)} fusion(f32[]{:T(128)} %bitcast.24, f32[]{:T(128)} %bitcast.25, f32[]{:T(128)} %bitcast.26, f32[]{:T(128)} %bitcast.27, f32[]{:T(128)} %bitcast.28, f32[]{:T(128)} %bitcast.29, f32[]{:T(128)} %bitcast.30, f32[]{:T(128)} %bitcast.31, f32[]{:T(128)} %bitcast.32, f32[]{:T(128)} %bitcast.33, ...), kind=kLoop, calls=%fused_computation.73 | loop fusion | flops 2293760 | bytes 65668 | tf_op jit(solution)/shard_map/convert_element_type | solution.py:121
  209.5 20.7 %fusion.43 = bf16[256,128]{1,0:T(8,128)(2,1)S(1)} fusion(f32[]{:T(128)} %bitcast.24, f32[]{:T(128)} %bitcast.25, f32[]{:T(128)} %bitcast.26, f32[]{:T(128)} %bitcast.27, f32[]{:T(128)} %bitcast.28, f32[]{:T(128)} %bitcast.29, f32[]{:T(128)} %bitcast.30, f32[]{:T(128)} %bitcast.31, f32[]{:T(128)} %bitcast.32, f32[]{:T(128)} %bitcast.33, f32[]{:T(128)} %bitcast.34, ...), kind=kLoop, calls=%fused_computation.77 | loop fusion | flops 2326528 | bytes 65668 | tf_op jit(solution)/shard_map/convert_element_type | solution.py:121
  230.3 5.0 gather_fusion.6
  235.3 5.3 all-to-all-done.1
  240.6 5.0 gather_fusion.4
  245.6 4.5 convert_reduce_fusion
  264.7 59.7 %all_gather.6 = f32[512,72]{1,0:T(8,128)S(1)} all-gather(f32[16,72]{1,0:T(8,128)S(1)} %add_convert_fusion), channel_id=1, replica_groups=mesh['inline'=4,'xline'=8] {'inline','xline'}, dimensions={0}, use_global_device_ids=true | all-gather | bytes 152064 | tf_op jit(solution)/shard_map/all_gather | solution.py:176
  335.0 6.5 %bitcast_convert_fusion = f32[2048,1024]{1,0:T(8,128)} fusion(bf16[1,1,2048,1024]{3,2,1,0:T(8,128)(2,1)} %param.12), kind=kLoop, calls=%fused_computation.39 | loop fusion | flops 2097152 | bytes 12582912 | tf_op jit(solution)/shard_map/convert_element_type | solution.py:253
  341.5 36.4 %all-gather.2.cloned.1.call-done = bf16[4096,2048]{1,0:T(8,128)(2,1)} async-done(((bf16[128,2048]{1,0:T(8,128)(2,1)}), bf16[4096,2048]{1,0:T(8,128)(2,1)}) %all-gather.2.cloned.1.call-update) | async-done | bytes 16777232 | tf_op jit(solution)/shard_map/all_gather | solution.py:230
  378.0 14.7 %gather_fusion.1 = bf16[256,8,2048]{2,1,0:T(8,128)(2,1)} fusion(bf16[512,8,2048]{2,1,0:T(8,128)(2,1)} %bitcast.129, s32[1024]{0:T(1024)S(1)} %pad_clamp_fusion.1), kind=kCustom, calls=%fused_computation.5 | custom fusion | bytes 16778240 | tf_op jit(solution)/shard_map/jit(_take)/gather | solution.py:252
  392.7 54.5 %fusion.17 = f32[2048,1024]{1,0:T(8,128)} fusion(bf16[256,8,2048]{2,1,0:T(8,128)(2,1)} %gather_fusion.1, pred[2048]{0:T(1024)(128)(4,1)S(1)} %broadcast_in_dim.240, f32[2048,1024]{1,0:T(8,128)} %bitcast_convert_fusion, f32[]{:T(128)} %bitcast.73, f32[]{:T(128)} %bitcast.72, f32[]{:T(128)} %bitcast.71, f32[]{:T(128)} %bitcast.70, f32[]{:T(128)} %bitcast.69, ...), kind=kOutput, calls=%fused_computation.37 | convolution fusion | flops 8631877632 | bytes 25167908 | tf_op jit(solution)/shard_map/dot_general | solution.py:256
  447.2 23.1 %scatter_custom_fusion.2 = f32[2048,1024]{1,0:T(8,128)} fusion(s32[2048]{0:T(1024)S(1)} %bitcast.138, f32[2048,1024]{1,0:T(8,128)} %fusion.17, f32[]{:T(128)} %constant.62.clone.1), kind=kCustom, calls=%fused_computation.46 | custom fusion | flops 2097152 | bytes 8389120 | tf_op jit(solution)/shard_map/scatter-add | solution.py:262
  477.0 9.8 %collective-permute-done.low_ref = f32[4,64,1024]{2,1,0:T(8,128)S(1)} collective-permute-done((f32[4,64,1024]{2,1,0:T(8,128)S(1)}, f32[4,64,1024]{2,1,0:T(8,128)S(1)}, u32[]{:S(2)}, u32[]{:S(2)}) %collective-permute-start) | collective-permute-done | bytes 1048608 | tf_op jit(solution)/shard_map/ppermute | solution.py:89
  486.8 4.4 collective-permute-done.1.high_ref
  502.6 8.8 %shard_map.87.middle_ref = f32[32,48,1024]{2,1,0:T(8,128)} custom-call(f32[9]{0:T(128)} %taps_ref.5, f32[32,64,1024]{2,1,0:T(8,128)} %bitcast.118, f32[4,64,1024]{2,1,0:T(8,128)} %copy-done, f32[4,64,1024]{2,1,0:T(8,128)} %copy-done.1), custom_call_target="tpu_custom_call" | custom-call | flops 62914560 | bytes 15728640 | tf_op jit(solution)/shard_map/pallas_call | solution.py:24
  513.5 20.4 %shard_map.88 = f32[32,64,1024]{2,1,0:T(8,128)} custom-call(f32[9]{0:T(128)} %taps_ref.5, f32[32,16,1024]{2,1,0:T(8,128)} %shard_map.86.first_ref.last_ref, f32[32,48,1024]{2,1,0:T(8,128)} %shard_map.87.middle_ref, f32[32,16,1024]{2,1,0:T(8,128)} %shard_map.86.first_ref.last_ref, f32[32,4,1024]{2,1,0:T(4,128)} %copy-done.4, f32[32,4,1024]{2,1,0:T(4,128)} %copy-done.5), custom_call_target="tpu_custom_call" | custom-call | flops 37748736 | bytes 18454936 | tf_op jit(solution)/shard_map/pallas_call | solution.py:61
  (126 shorter events, 59.8 us)
Async XLA Ops:
  41.3 99.6 %all-to-all-start.2 = ((bf16[32,32,2048]{2,1,0:T(8,128)(2,1)}), bf16[32,32,2048]{2,1,0:T(8,128)(2,1)}, u32[]{:S(2)}, u32[]{:S(2)}) async-start(bf16[32,32,2048]{2,1,0:T(8,128)(2,1)} %bitcast.131), calls=%async_computation.2 | async-start | bytes 8388608 | tf_op jit(solution)/shard_map/all_to_all | solution.py:159
  140.9 4.1 copy-start.3
  140.9 46.9 %copy-start.6 = (bf16[128,2048]{1,0:T(8,128)(2,1)S(1)}, bf16[128,2048]{1,0:T(8,128)(2,1)}, u32[]{:S(2)}) copy-start(bf16[128,2048]{1,0:T(8,128)(2,1)} %param.13) | copy-start | bytes 1572868
  140.9 99.7 %all-to-all-start.1 = ((bf16[32,32,2048]{2,1,0:T(8,128)(2,1)}), bf16[32,32,2048]{2,1,0:T(8,128)(2,1)}, u32[]{:S(2)}, u32[]{:S(2)}) async-start(bf16[32,32,2048]{2,1,0:T(8,128)(2,1)} %bitcast.130), calls=%async_computation.1 | async-start | bytes 8388608 | tf_op jit(solution)/shard_map/all_to_all | solution.py:159
  144.8 233.2 %all-gather.2.cloned.1.call-start = ((), (), s32[]{:S(2)}) async-start(), calls=%async_computation.3 | async-start | bytes 17301504 | tf_op jit(solution)/shard_map/all_gather | solution.py:230
  261.7 1.2 copy-start.2
  262.1 2.3 copy-start.8
  264.7 69.6 %copy-start.7 = (f32[9]{0:T(128)S(1)}, f32[9]{0:T(128)}, u32[]{:S(2)}) copy-start(f32[9]{0:T(128)} %taps_ref.5) | copy-start | bytes 112
  471.9 14.8 %collective-permute-start = (f32[4,64,1024]{2,1,0:T(8,128)S(1)}, f32[4,64,1024]{2,1,0:T(8,128)S(1)}, u32[]{:S(2)}, u32[]{:S(2)}) collective-permute-start(f32[4,64,1024]{2,1,0:T(8,128)S(1)} %bitcast.134), channel_id=1, source_target_pairs={{0,8},{8,16},{16,24},{1,9},{9,17},{17,25},{2,10},{10,18},{18,26},{... | collective-permute-start | bytes 3145736 | tf_op jit(solution)/shard_map/ppermute | solution.py:89
  475.0 16.1 %collective-permute-start.1 = (f32[4,64,1024]{2,1,0:T(8,128)S(1)}, f32[4,64,1024]{2,1,0:T(8,128)S(1)}, u32[]{:S(2)}, u32[]{:S(2)}) collective-permute-start(f32[4,64,1024]{2,1,0:T(8,128)S(1)} %bitcast.133), channel_id=1, source_target_pairs={{8,0},{16,8},{24,16},{9,1},{17,9},{25,17},{10,2},{18,10},{26,18},{... | collective-permute-start | bytes 3145736 | tf_op jit(solution)/shard_map/ppermute | solution.py:92
  486.8 4.4 copy-start
  491.2 1.0 copy-start.1
  497.4 14.3 %collective-permute-start.2 = (f32[32,4,1024]{2,1,0:T(4,128)S(1)}, f32[32,4,1024]{2,1,0:T(4,128)S(1)}, u32[]{:S(2)}, u32[]{:S(2)}) collective-permute-start(f32[32,4,1024]{2,1,0:T(4,128)S(1)} %get-tuple-element.33), channel_id=1, source_target_pairs={{0,1},{1,2},{2,3},{3,4},{4,5},{5,6},{6,7},{8,9},{9,10},{10,11},{11... | collective-permute-start | bytes 1572872 | tf_op jit(solution)/shard_map/ppermute | solution.py:89
  500.0 11.8 %collective-permute-start.3 = (f32[32,4,1024]{2,1,0:T(4,128)S(1)}, f32[32,4,1024]{2,1,0:T(4,128)S(1)}, u32[]{:S(2)}, u32[]{:S(2)}) collective-permute-start(f32[32,4,1024]{2,1,0:T(4,128)S(1)} %get-tuple-element.32), channel_id=1, source_target_pairs={{1,0},{2,1},{3,2},{4,3},{5,4},{6,5},{7,6},{9,8},{10,9},{11,10},{12... | collective-permute-start | bytes 1572872 | tf_op jit(solution)/shard_map/ppermute | solution.py:92
  511.8 0.8 copy-start.4
  512.6 0.9 copy-start.5
Sparse Core Ops, SparseCore 0:
  264.5 113.4 all-gather.1

commit v12 on v10

--- a/solution.py
+++ b/solution.py
@@ -13,10 +13,17 @@
     ext_ref[0:HW] = low_ref[...]
     ext_ref[HW:HW + nx] = main_ref[...]
     ext_ref[HW + nx:] = high_ref[...]
-    out = taps_ref[0] * ext_ref[0:nx]
-    for j in range(1, 2 * HW + 1):
-        out = out + taps_ref[j] * ext_ref[j:j + nx]
-    out_ref[...] = out
+    lanes = 128
+
+    def lane_chunk(c, carry):
+        cols = pl.ds(pl.multiple_of(c * lanes, lanes), lanes)
+        out = taps_ref[0] * ext_ref[0:nx, :, cols]
+        for j in range(1, 2 * HW + 1):
+            out = out + taps_ref[j] * ext_ref[j:j + nx, :, cols]
+        out_ref[:, :, cols] = out
+        return carry
+
+    lax.fori_loop(0, main_ref.shape[2] // lanes, lane_chunk, 0)
 
 
 def smooth_zx(raw, low, high, taps, blocks, ty=8):
@@ -48,10 +55,17 @@
     ext_ref[:, 2 * HW + edge:2 * HW + ny - edge] = middle_ref[...]
     ext_ref[:, 2 * HW + ny - edge:2 * HW + ny] = last_ref[...]
     ext_ref[:, 2 * HW + ny:3 * HW + ny] = high_ref[...]
-    out = taps_ref[0] * ext_ref[:, pl.ds(HW, ny)]
-    for j in range(1, 2 * HW + 1):
-        out = out + taps_ref[j] * ext_ref[:, pl.ds(HW + j, ny)]
-    out_ref[...] = out
+    lanes = 128
+
+    def lane_chunk(c, carry):
+        cols = pl.ds(pl.multiple_of(c * lanes, lanes), lanes)
+        out = taps_ref[0] * ext_ref[:, pl.ds(HW, ny), cols]
+        for j in range(1, 2 * HW + 1):
+            out = out + taps_ref[j] * ext_ref[:, pl.ds(HW + j, ny), cols]
+        out_ref[:, :, cols] = out
+        return carry
+
+    lax.fori_loop(0, out_ref.shape[2] // lanes, lane_chunk, 0)
 
 
 def smooth_y(edges, middle, low, high, taps, tx=4):

time: 524 us -> 518 us (0.989)
  Pallas kernels: 32.9 us -> 26.7 us
    pallas_call x1, Pallas kernels: 20.4 us -> 14 us  [smooth_y(): pl.pallas_call(_y_kernel, grid=(nx // tx,), in_specs=[pl.BlockSpec(memory...]
  transfers between devices with their start and end apart: 7 -> 7, of which waited for: 5 -> 5; matrix products, arithmetic and copies ran while one was open for 29% -> 30% of each run, Pallas kernels for 2% -> 2%
where the time goes in v12:
time: 518 us; the launch traced here: 510 us
  other arithmetic  144 us (28%)
  waiting for transfers between devices  110 us (21%)
  local copies, waits for them, and re-layouts  73.9 us (14%)
  blocking collectives  73.2 us (14%)
  matrix products  48.3 us (9%)
  Pallas kernels  26.7 us (5%)
  starting transfers between devices  18.1 us (3%)
  between operations  15.1 us (3%)
    all_to_all x2, waiting for transfers between devices, traverse(): lax.all_to_all(blocks, ('inline', 'xline'), split_axis=0, concat_axis=0,...  85.3 us
    convert_element_type x7, other arithmetic, split(): return (high.astype(jnp.bfloat16), (x - high).astype(jnp.bfloat16))  83.6 us
    all_gather x1, blocking collectives, local(): tables_all = jnp.round(lax.all_gather(tables, axes, axis=0, tiled=True))  59.6 us
    add x1, other arithmetic, filter_padded(): result + taps[offset] * lax.slice_in_dim(padded, offset, offset + length,...  24.6 us
    scatter-add x1, other arithmetic, local(): raw_gradient = jnp.zeros((cell_count, depth_len), jnp.float32).at[cells.r...  23.1 us
    dot_general x2, matrix products, local(): lax.dot_general(jnp.take(tile_rows, wanted, axis=0), weight_matrix, contr...  17.1 us
    dot_general x1, matrix products, local(): jnp.dot(flat, w_low, preferred_element_type=jnp.float32)  16.2 us
    gather x2, local copies, waits for them, and re-layouts, local(): jnp.take(tile_rows, wanted, axis=0)  15.4 us
  transfers between devices with their start and end apart: 7, of which 5 were waited for; matrix products, arithmetic and copies ran while one was open for 30% of the time, Pallas kernels for 2%

profile of v12, /device:TPU:1, one launch (start us, length us, event | category | flops | bytes accessed | tf_op | source)
XLA Modules:
  0.0 509.7 jit_solution(10049233764076599531)
XLA Ops:
  11.1 13.6 %all_to_all.19 = s32[32,1,64]{2,1,0:T(1,128)S(1)} all-to-all(s32[32,1,64]{2,1,0:T(1,128)S(1)} %bitcast.140), channel_id=1, replica_groups=mesh['inline'=4,'xline'=8] {'inline','xline'}, dimensions={0} | all-to-all | bytes 16384 | tf_op jit(solution)/shard_map/all_to_all | solution.py:206
  25.1 7.7 %gather_fusion.3 = bf16[1024,1024]{1,0:T(8,128)(2,1)S(1)} fusion(bf16[2048,1024]{1,0:T(8,128)(2,1)} %bitcast.118, s32[1024]{0:T(1024)S(1)} %fusion.82), kind=kCustom, calls=%fused_computation.clone | custom fusion | bytes 4198400 | tf_op jit(solution)/shard_map/jit(_take)/gather | solution.py:223
  32.8 8.6 %fusion.27 = bf16[1024,2048]{1,0:T(8,128)(2,1)} fusion(bf16[1,1,2048,1024]{3,2,1,0:T(8,128)(2,1)} %param.12, bf16[1024,1024]{1,0:T(8,128)(2,1)S(1)} %gather_fusion.3, pred[1024]{0:T(1024)(128)(4,1)S(1)} %compare_and_fusion.1), kind=kOutput, calls=%fused_computation.50 | convolution fusion | flops 4298113024 | bytes 10486784 | tf_op jit(solution)/shard_map/dot_general | solution.py:222
  45.3 7.7 %gather_fusion.5 = bf16[1024,1024]{1,0:T(8,128)(2,1)S(1)} fusion(bf16[2048,1024]{1,0:T(8,128)(2,1)} %bitcast.119, s32[1024]{0:T(1024)S(1)} %fusion.83), kind=kCustom, calls=%fused_computation.2.clone | custom fusion | bytes 4198400 | tf_op jit(solution)/shard_map/jit(_take)/gather | solution.py:223
  53.1 8.5 %fusion.30 = bf16[1024,2048]{1,0:T(8,128)(2,1)} fusion(bf16[1,1,2048,1024]{3,2,1,0:T(8,128)(2,1)} %param.12, bf16[1024,1024]{1,0:T(8,128)(2,1)S(1)} %gather_fusion.5, pred[1024]{0:T(1024)(128)(4,1)S(1)} %compare_and_fusion), kind=kOutput, calls=%fused_computation.51 | convolution fusion | flops 4298113024 | bytes 10486784 | tf_op jit(solution)/shard_map/dot_general | solution.py:222
  61.6 79.3 %all-to-all-done.1 = bf16[32,32,2048]{2,1,0:T(8,128)(2,1)} async-done(((bf16[32,32,2048]{2,1,0:T(8,128)(2,1)}), bf16[32,32,2048]{2,1,0:T(8,128)(2,1)}, u32[]{:S(2)}, u32[]{:S(2)}) %all-to-all-start.1) | async-done | bytes 4194336 | tf_op jit(solution)/shard_map/all_to_all | solution.py:173
  146.3 20.5 %fusion.43 = bf16[256,128]{1,0:T(8,128)(2,1)S(1)} fusion(f32[]{:T(128)} %bitcast.24, f32[]{:T(128)} %bitcast.25, f32[]{:T(128)} %bitcast.26, f32[]{:T(128)} %bitcast.27, f32[]{:T(128)} %bitcast.28, f32[]{:T(128)} %bitcast.29, f32[]{:T(128)} %bitcast.30, f32[]{:T(128)} %bitcast.31, f32[]{:T(128)} %bitcast.32, f32[]{:T(128)} %bitcast.33, f32[]{:T(128)} %bitcast.34, ...), kind=kLoop, calls=%fused_computation.79 | loop fusion | flops 2326528 | bytes 65668 | tf_op jit(solution)/shard_map/convert_element_type | solution.py:135
  166.9 20.5 %reduce-precision_convert_fusion.4 = bf16[256,128]{1,0:T(8,128)(2,1)S(1)} fusion(f32[]{:T(128)} %bitcast.24, f32[]{:T(128)} %bitcast.25, f32[]{:T(128)} %bitcast.26, f32[]{:T(128)} %bitcast.27, f32[]{:T(128)} %bitcast.28, f32[]{:T(128)} %bitcast.29, f32[]{:T(128)} %bitcast.30, f32[]{:T(128)} %bitcast.31, f32[]{:T(128)} %bitcast.32, f32[]{:T(128)} %bitcast.33, ...), kind=kLoop, calls=%fused_computation.75 | loop fusion | flops 2293760 | bytes 65668 | tf_op jit(solution)/shard_map/convert_element_type | solution.py:135
  187.4 20.5 %fusion.42 = bf16[256,128]{1,0:T(8,128)(2,1)S(1)} fusion(f32[]{:T(128)} %bitcast.56, f32[]{:T(128)} %bitcast.55, f32[]{:T(128)} %bitcast.54, f32[]{:T(128)} %bitcast.53, f32[]{:T(128)} %bitcast.52, f32[]{:T(128)} %bitcast.51, f32[]{:T(128)} %bitcast.50, f32[]{:T(128)} %bitcast.49, f32[]{:T(128)} %bitcast.48, f32[]{:T(128)} %bitcast.47, f32[]{:T(128)} %bitcast.46, ...), kind=kLoop, calls=%fused_computation.78 | loop fusion | flops 2326528 | bytes 65668 | tf_op jit(solution)/shard_map/convert_element_type | solution.py:135
  208.0 20.5 %reduce-precision_convert_fusion.5 = bf16[256,128]{1,0:T(8,128)(2,1)S(1)} fusion(f32[]{:T(128)} %bitcast.56, f32[]{:T(128)} %bitcast.55, f32[]{:T(128)} %bitcast.54, f32[]{:T(128)} %bitcast.53, f32[]{:T(128)} %bitcast.52, f32[]{:T(128)} %bitcast.51, f32[]{:T(128)} %bitcast.50, f32[]{:T(128)} %bitcast.49, f32[]{:T(128)} %bitcast.48, f32[]{:T(128)} %bitcast.47, ...), kind=kLoop, calls=%fused_computation.77 | loop fusion | flops 2293760 | bytes 65668 | tf_op jit(solution)/shard_map/convert_element_type | solution.py:135
  229.6 5.0 gather_fusion.4
  234.6 5.9 %all-to-all-done.2 = bf16[32,32,2048]{2,1,0:T(8,128)(2,1)} async-done(((bf16[32,32,2048]{2,1,0:T(8,128)(2,1)}), bf16[32,32,2048]{2,1,0:T(8,128)(2,1)}, u32[]{:S(2)}, u32[]{:S(2)}) %all-to-all-start.2) | async-done | bytes 4194336 | tf_op jit(solution)/shard_map/all_to_all | solution.py:173
  240.5 5.0 gather_fusion.6
  265.5 59.6 %all_gather.6 = f32[512,72]{1,0:T(8,128)S(1)} all-gather(f32[16,72]{1,0:T(8,128)S(1)} %add_convert_fusion), channel_id=1, replica_groups=mesh['inline'=4,'xline'=8] {'inline','xline'}, dimensions={0}, use_global_device_ids=true | all-gather | bytes 152064 | tf_op jit(solution)/shard_map/all_gather | solution.py:190
  331.3 6.0 %gather_fusion.2 = s32[512,8]{1,0:T(8,128)S(1)} fusion(s32[512,8,8]{1,2,0:T(8,128)} %copy.89, s32[512]{0:T(512)S(1)} %bitcast.122), kind=kCustom, calls=%fused_computation.6 | custom fusion | bytes 36864 | tf_op jit(solution)/shard_map/jit(take_along_axis)/gather | solution.py:260
  343.8 24.6 %fusion.8 = f32[2048,1024]{1,0:T(8,128)} fusion(f32[2048,1024]{1,0:T(8,128)S(1)} %bitcast_convert_fusion, f32[]{:T(128)} %bitcast.73, f32[]{:T(128)} %bitcast.72, f32[]{:T(128)} %bitcast.71, f32[]{:T(128)} %bitcast.70, f32[]{:T(128)} %bitcast.69, f32[]{:T(128)} %bitcast.68, f32[]{:T(128)} %bitcast.67, f32[]{:T(128)} %bitcast.66, f32[]{:T(128)} %bitcast.65), kind=kLoop, calls=%fused_computation.28 | loop fusion | flops 35651584 | bytes 16777252 | tf_op jit(solution)/shard_map/add | solution.py:166
  368.4 10.4 %all-gather.2.cloned.1.call-done = bf16[4096,2048]{1,0:T(8,128)(2,1)} async-done(((bf16[128,2048]{1,0:T(8,128)(2,1)}), bf16[4096,2048]{1,0:T(8,128)(2,1)}) %all-gather.2.cloned.1.call-update) | async-done | bytes 16777232 | tf_op jit(solution)/shard_map/all_gather | solution.py:244
  378.8 14.3 %gather_fusion.1 = bf16[256,8,2048]{2,1,0:T(8,128)(2,1)} fusion(bf16[512,8,2048]{2,1,0:T(8,128)(2,1)} %bitcast.132, s32[1024]{0:T(1024)S(1)} %pad_clamp_fusion.1), kind=kCustom, calls=%fused_computation.5 | custom fusion | bytes 16778240 | tf_op jit(solution)/shard_map/jit(_take)/gather | solution.py:266
  393.1 16.2 %fusion.19 = f32[2048,1024]{1,0:T(8,128)} fusion(f32[2048,1024]{1,0:T(8,128)} %fusion.8, bf16[256,8,2048]{2,1,0:T(8,128)(2,1)} %gather_fusion.1, pred[2048]{0:T(1024)(128)(4,1)S(1)} %broadcast_in_dim.240), kind=kOutput, calls=%fused_computation.41 | convolution fusion | flops 8600420352 | bytes 25167872 | tf_op jit(solution)/shard_map/dot_general | solution.py:271
  409.3 11.2 %fusion.21 = f32[2048,1024]{1,0:T(8,128)} fusion(f32[2048,1024]{1,0:T(8,128)S(1)} %copy-done, bf16[256,8,2048]{2,1,0:T(8,128)(2,1)S(1)} %copy-done.1, pred[2048]{0:T(1024)(128)(4,1)S(1)} %broadcast_in_dim.240), kind=kOutput, calls=%fused_computation.42 | convolution fusion | flops 8598323200 | bytes 25167872 | tf_op jit(solution)/shard_map/dot_general | solution.py:271
  420.5 23.1 %scatter_custom_fusion.2 = f32[2048,1024]{1,0:T(8,128)} fusion(s32[2048]{0:T(1024)S(1)} %bitcast.141, f32[2048,1024]{1,0:T(8,128)} %fusion.21, f32[2048,1024]{1,0:T(8,128)} %fusion.19, f32[]{:T(128)} %constant.62.clone.1), kind=kCustom, calls=%fused_computation.39 | custom fusion | flops 4194304 | bytes 25165828 | tf_op jit(solution)/shard_map/scatter-add | solution.py:277
  450.4 9.8 %collective-permute-done.low_ref = f32[4,64,1024]{2,1,0:T(8,128)S(1)} collective-permute-done((f32[4,64,1024]{2,1,0:T(8,128)S(1)}, f32[4,64,1024]{2,1,0:T(8,128)S(1)}, u32[]{:S(2)}, u32[]{:S(2)}) %collective-permute-start) | collective-permute-done | bytes 1048608 | tf_op jit(solution)/shard_map/ppermute | solution.py:103
  477.9 8.8 %shard_map.87.middle_ref = f32[32,48,1024]{2,1,0:T(8,128)} custom-call(f32[9]{0:T(128)} %taps_ref.5, f32[32,64,1024]{2,1,0:T(8,128)} %bitcast.121, f32[4,64,1024]{2,1,0:T(8,128)} %copy-done.2, f32[4,64,1024]{2,1,0:T(8,128)} %collective-permute-done.1.high_ref), custom_call_target="tpu_custom_call" | custom-call | flops 62914560 | bytes 15728640 | tf_op jit(solution)/shard_map/pallas_call | solution.py:31
  488.3 14.0 %shard_map.88 = f32[32,64,1024]{2,1,0:T(8,128)} custom-call(f32[9]{0:T(128)} %taps_ref.5, f32[32,16,1024]{2,1,0:T(8,128)} %shard_map.86.first_ref.last_ref, f32[32,48,1024]{2,1,0:T(8,128)} %shard_map.87.middle_ref, f32[32,16,1024]{2,1,0:T(8,128)} %shard_map.86.first_ref.last_ref, f32[32,4,1024]{2,1,0:T(4,128)} %copy-done.5, f32[32,4,1024]{2,1,0:T(4,128)} %copy-done.4), custom_call_target="tpu_custom_call" | custom-call | flops 37748736 | bytes 18454936 | tf_op jit(solution)/shard_map/pallas_call | solution.py:75
  (128 shorter events, 73.0 us)
Async XLA Ops:
  41.4 99.6 %all-to-all-start.1 = ((bf16[32,32,2048]{2,1,0:T(8,128)(2,1)}), bf16[32,32,2048]{2,1,0:T(8,128)(2,1)}, u32[]{:S(2)}, u32[]{:S(2)}) async-start(bf16[32,32,2048]{2,1,0:T(8,128)(2,1)} %bitcast.134), calls=%async_computation.1 | async-start | bytes 8388608 | tf_op jit(solution)/shard_map/all_to_all | solution.py:173
  61.6 83.3 %copy-start.3 = (f32[33]{0:T(128)S(1)}, f32[33]{0:T(128)}, u32[]{:S(2)}) copy-start(f32[33]{0:T(128)} %param.14) | copy-start | bytes 400
  61.6 166.9 %copy-start.6 = (bf16[128,2048]{1,0:T(8,128)(2,1)S(1)}, bf16[128,2048]{1,0:T(8,128)(2,1)}, u32[]{:S(2)}) copy-start(bf16[128,2048]{1,0:T(8,128)(2,1)} %param.13) | copy-start | bytes 1572868
  140.9 99.5 %all-to-all-start.2 = ((bf16[32,32,2048]{2,1,0:T(8,128)(2,1)}), bf16[32,32,2048]{2,1,0:T(8,128)(2,1)}, u32[]{:S(2)}, u32[]{:S(2)}) async-start(bf16[32,32,2048]{2,1,0:T(8,128)(2,1)} %bitcast.133), calls=%async_computation.2 | async-start | bytes 8388608 | tf_op jit(solution)/shard_map/all_to_all | solution.py:173
  144.7 234.1 %all-gather.2.cloned.1.call-start = ((), (), s32[]{:S(2)}) async-start(), calls=%async_computation.3 | async-start | bytes 17301504 | tf_op jit(solution)/shard_map/all_gather | solution.py:244
  258.4 6.8 %copy-start.8 = (s32[128,8]{0,1:T(8,128)S(1)}, s32[128,8]{0,1:T(8,128)}, u32[]{:S(2)}) copy-start(s32[128,8]{0,1:T(8,128)} %param.17) | copy-start | bytes 12292
  262.1 77.8 %copy-start.7 = (f32[9]{0:T(128)S(1)}, f32[9]{0:T(128)}, u32[]{:S(2)}) copy-start(f32[9]{0:T(128)} %taps_ref.5) | copy-start | bytes 112
  393.1 16.2 %copy-start = (f32[2048,1024]{1,0:T(8,128)S(1)}, f32[2048,1024]{1,0:T(8,128)}, u32[]{:S(2)}) copy-start(f32[2048,1024]{1,0:T(8,128)} %fusion.8) | copy-start | bytes 25165828
  393.1 16.2 %copy-start.1 = (bf16[256,8,2048]{2,1,0:T(8,128)(2,1)S(1)}, bf16[256,8,2048]{2,1,0:T(8,128)(2,1)}, u32[]{:S(2)}) copy-start(bf16[256,8,2048]{2,1,0:T(8,128)(2,1)} %gather_fusion.1) | copy-start | bytes 25165828
  445.2 14.9 %collective-permute-start = (f32[4,64,1024]{2,1,0:T(8,128)S(1)}, f32[4,64,1024]{2,1,0:T(8,128)S(1)}, u32[]{:S(2)}, u32[]{:S(2)}) collective-permute-start(f32[4,64,1024]{2,1,0:T(8,128)S(1)} %bitcast.137), channel_id=1, source_target_pairs={{0,8},{8,16},{16,24},{1,9},{9,17},{17,25},{2,10},{10,18},{18,26},{... | collective-permute-start | bytes 3145736 | tf_op jit(solution)/shard_map/ppermute | solution.py:103
  448.4 16.4 %collective-permute-start.1 = (f32[4,64,1024]{2,1,0:T(8,128)S(1)}, f32[4,64,1024]{2,1,0:T(8,128)}, u32[]{:S(2)}, u32[]{:S(2)}) collective-permute-start(f32[4,64,1024]{2,1,0:T(8,128)S(1)} %bitcast.136), channel_id=1, source_target_pairs={{8,0},{16,8},{24,16},{9,1},{17,9},{25,17},{10,2},{18,10},{26,18},{... | collective-permute-start | bytes 3145736 | tf_op jit(solution)/shard_map/ppermute | solution.py:106
  460.2 4.7 copy-start.2
  471.3 15.5 %collective-permute-start.3 = (f32[32,4,1024]{2,1,0:T(4,128)}, f32[32,4,1024]{2,1,0:T(4,128)S(1)}, u32[]{:S(2)}, u32[]{:S(2)}) collective-permute-start(f32[32,4,1024]{2,1,0:T(4,128)} %get-tuple-element.32), channel_id=1, source_target_pairs={{1,0},{2,1},{3,2},{4,3},{5,4},{6,5},{7,6},{9,8},{10,9},{11,10},{12... | collective-permute-start | bytes 1572872 | tf_op jit(solution)/shard_map/ppermute | solution.py:106
  472.6 14.2 %collective-permute-start.2 = (f32[32,4,1024]{2,1,0:T(4,128)S(1)}, f32[32,4,1024]{2,1,0:T(4,128)S(1)}, u32[]{:S(2)}, u32[]{:S(2)}) collective-permute-start(f32[32,4,1024]{2,1,0:T(4,128)S(1)} %get-tuple-element.33), channel_id=1, source_target_pairs={{0,1},{1,2},{2,3},{3,4},{4,5},{5,6},{6,7},{8,9},{9,10},{10,11},{11... | collective-permute-start | bytes 1572872 | tf_op jit(solution)/shard_map/ppermute | solution.py:103
  486.7 0.8 copy-start.4
  487.6 0.8 copy-start.5
Sparse Core Ops, SparseCore 0:
  265.3 113.4 all-gather.1

commit v13 on v12

--- a/solution.py
+++ b/solution.py
@@ -187,7 +187,6 @@
     tables = jnp.concatenate(
         [aperture, landing.reshape(block_count, per_block * aperture_len)], axis=1
     ).astype(jnp.float32)
-    tables_all = jnp.round(lax.all_gather(tables, axes, axis=0, tiled=True))
     target_tile = aperture.reshape(item_count)
     onehot = (target_tile[:, None] == jnp.arange(device_count, dtype=jnp.int32)[None, :]).astype(
         jnp.int32
@@ -223,6 +222,11 @@
             jnp.take(tile_rows, wanted, axis=0), weight_matrix, contract,
             preferred_element_type=jnp.float32,
         ).astype(jnp.bfloat16)
+        if part == 0:
+            predicted, late_tables = lax.optimization_barrier((predicted, tables))
+            tables_all = jnp.round(lax.all_gather(late_tables, axes, axis=0, tiled=True))
+        if part == 1:
+            predicted, tables_all = lax.optimization_barrier((predicted, tables_all))
         returned.append(
             traverse(predicted.reshape(device_count, half_cap * per_block, samples)).reshape(
                 device_count * half_cap, per_block, samples

time: 518 us -> 585 us (1.13)
  blocking collectives: 73.2 us -> 137 us
  waiting for transfers between devices: 110 us -> 95.9 us
  starting transfers between devices: 18.1 us -> 30.9 us
    all_to_all x2, waiting for transfers between devices: 85.3 us -> 5.94 us  [traverse(): lax.all_to_all(blocks, ('inline', 'xline'), split_axis=0, concat_axis=0,...]
    all_gather x1, blocking collectives: 59.6 us -> 137 us  [local(): lax.all_gather(late_tables, axes, axis=0, tiled=True)]
    all_gather x1, waiting for transfers between devices: 10.4 us -> 69.9 us  [local(): adjoint_all = lax.all_gather(adjoint, axes, axis=0, tiled=True)]
    all_to_all x1 -> x0, blocking collectives: 13.6 us -> none  [local(): lax.all_to_all(cell_send.reshape(device_count, capacity * per_block), axe...]
    all_to_all x0 -> x1, starting transfers between devices: none -> 7.1 us  [local(): lax.all_to_all(cell_send.reshape(device_count, capacity * per_block), axe...]
  transfers between devices with their start and end apart: 7 -> 8, of which waited for: 5 -> 6; matrix products, arithmetic and copies ran while one was open for 30% -> 26% of each run, Pallas kernels for 2% -> 2%
where the time goes in v13:
time: 585 us; the launch traced here: 576 us
  other arithmetic  145 us (25%)
  blocking collectives  137 us (23%)
  waiting for transfers between devices  95.9 us (16%)
  local copies, waits for them, and re-layouts  74.6 us (13%)
  matrix products  51.5 us (9%)
  starting transfers between devices  30.9 us (5%)
  Pallas kernels  26.7 us (5%)
  between operations  15.1 us (3%)
    all_gather x1, blocking collectives, local(): lax.all_gather(late_tables, axes, axis=0, tiled=True)  137 us
    convert_element_type x7, other arithmetic, split(): return (high.astype(jnp.bfloat16), (x - high).astype(jnp.bfloat16))  83.6 us
    all_gather x1, waiting for transfers between devices, local(): adjoint_all = lax.all_gather(adjoint, axes, axis=0, tiled=True)  69.9 us
    add x1, other arithmetic, filter_padded(): result + taps[offset] * lax.slice_in_dim(padded, offset, offset + length,...  24.8 us
    scatter-add x1, other arithmetic, local(): raw_gradient = jnp.zeros((cell_count, depth_len), jnp.float32).at[cells.r...  23.3 us
    dot_general x2, matrix products, local(): lax.dot_general(jnp.take(tile_rows, wanted, axis=0), weight_matrix, contr...  17.1 us
    dot_general x1, matrix products, local(): jnp.dot(flat, w_low, preferred_element_type=jnp.float32)  16.8 us
    gather x2, local copies, waits for them, and re-layouts, local(): jnp.take(tile_rows, wanted, axis=0)  15.4 us
  transfers between devices with their start and end apart: 8, of which 6 were waited for; matrix products, arithmetic and copies ran while one was open for 26% of the time, Pallas kernels for 2%

profile of v13, /device:TPU:1, one launch (start us, length us, event | category | flops | bytes accessed | tf_op | source)
XLA Modules:
  0.0 576.3 jit_solution(4046136475752219917)
XLA Ops:
  11.7 7.1 %all-to-all-start = ((s32[32,1,64]{2,1,0:T(1,128)}), s32[32,1,64]{2,1,0:T(1,128)S(1)}, u32[]{:S(2)}, u32[]{:S(2)}) async-start(s32[32,1,64]{2,1,0:T(1,128)} %bitcast.4), calls=%async_computation | async-start | bytes 32768 | tf_op jit(solution)/shard_map/all_to_all | solution.py:205
  19.8 5.7 all-to-all-done
  25.8 7.7 %gather_fusion.4 = bf16[1024,1024]{1,0:T(8,128)(2,1)S(1)} fusion(bf16[2048,1024]{1,0:T(8,128)(2,1)} %bitcast.118, s32[1024]{0:T(1024)S(1)} %fusion.81), kind=kCustom, calls=%fused_computation.2.clone | custom fusion | bytes 4198400 | tf_op jit(solution)/shard_map/jit(_take)/gather | solution.py:222
  33.5 8.6 %fusion.30 = bf16[1024,2048]{1,0:T(8,128)(2,1)} fusion(bf16[1,1,2048,1024]{3,2,1,0:T(8,128)(2,1)} %param.12, bf16[1024,1024]{1,0:T(8,128)(2,1)S(1)} %gather_fusion.4, pred[1024]{0:T(1024)(128)(4,1)S(1)} %compare_and_fusion), kind=kOutput, calls=%fused_computation.51 | convolution fusion | flops 4298113024 | bytes 10486784 | tf_op jit(solution)/shard_map/dot_general | solution.py:221
  46.1 7.7 %gather_fusion.3 = bf16[1024,1024]{1,0:T(8,128)(2,1)S(1)} fusion(bf16[2048,1024]{1,0:T(8,128)(2,1)} %bitcast.119, s32[1024]{0:T(1024)S(1)} %fusion.80), kind=kCustom, calls=%fused_computation.clone | custom fusion | bytes 4198400 | tf_op jit(solution)/shard_map/jit(_take)/gather | solution.py:222
  53.8 136.8 %all_gather.6 = f32[512,72]{1,0:T(8,128)S(1)} all-gather(f32[16,72]{1,0:T(8,128)S(1)} %add_convert_fusion), channel_id=1, replica_groups=mesh['inline'=4,'xline'=8] {'inline','xline'}, dimensions={0}, use_global_device_ids=true | all-gather | bytes 152064 | tf_op jit(solution)/shard_map/all_gather | solution.py:227
  190.8 8.5 %fusion.27 = bf16[1024,2048]{1,0:T(8,128)(2,1)} fusion(bf16[1,1,2048,1024]{3,2,1,0:T(8,128)(2,1)} %param.12, bf16[1024,1024]{1,0:T(8,128)(2,1)S(1)} %gather_fusion.3, pred[1024]{0:T(1024)(128)(4,1)S(1)} %compare_and_fusion.1), kind=kOutput, calls=%fused_computation.50 | convolution fusion | flops 4298113024 | bytes 10486784 | tf_op jit(solution)/shard_map/dot_general | solution.py:221
  199.3 9.4 %all-to-all-start.2 = ((bf16[32,32,2048]{2,1,0:T(8,128)(2,1)}), bf16[32,32,2048]{2,1,0:T(8,128)(2,1)}, u32[]{:S(2)}, u32[]{:S(2)}) async-start(bf16[32,32,2048]{2,1,0:T(8,128)(2,1)} %bitcast.133), calls=%async_computation.2 | async-start | bytes 8388608 | tf_op jit(solution)/shard_map/all_to_all | solution.py:173
  210.3 20.5 %fusion.43 = bf16[256,128]{1,0:T(8,128)(2,1)S(1)} fusion(f32[]{:T(128)} %bitcast.24, f32[]{:T(128)} %bitcast.25, f32[]{:T(128)} %bitcast.26, f32[]{:T(128)} %bitcast.27, f32[]{:T(128)} %bitcast.28, f32[]{:T(128)} %bitcast.29, f32[]{:T(128)} %bitcast.30, f32[]{:T(128)} %bitcast.31, f32[]{:T(128)} %bitcast.32, f32[]{:T(128)} %bitcast.33, f32[]{:T(128)} %bitcast.34, ...), kind=kLoop, calls=%fused_computation.79 | loop fusion | flops 2326528 | bytes 65668 | tf_op jit(solution)/shard_map/convert_element_type | solution.py:135
  230.9 20.5 %reduce-precision_convert_fusion.4 = bf16[256,128]{1,0:T(8,128)(2,1)S(1)} fusion(f32[]{:T(128)} %bitcast.24, f32[]{:T(128)} %bitcast.25, f32[]{:T(128)} %bitcast.26, f32[]{:T(128)} %bitcast.27, f32[]{:T(128)} %bitcast.28, f32[]{:T(128)} %bitcast.29, f32[]{:T(128)} %bitcast.30, f32[]{:T(128)} %bitcast.31, f32[]{:T(128)} %bitcast.32, f32[]{:T(128)} %bitcast.33, ...), kind=kLoop, calls=%fused_computation.75 | loop fusion | flops 2293760 | bytes 65668 | tf_op jit(solution)/shard_map/convert_element_type | solution.py:135
  251.4 20.5 %fusion.42 = bf16[256,128]{1,0:T(8,128)(2,1)S(1)} fusion(f32[]{:T(128)} %bitcast.56, f32[]{:T(128)} %bitcast.55, f32[]{:T(128)} %bitcast.54, f32[]{:T(128)} %bitcast.53, f32[]{:T(128)} %bitcast.52, f32[]{:T(128)} %bitcast.51, f32[]{:T(128)} %bitcast.50, f32[]{:T(128)} %bitcast.49, f32[]{:T(128)} %bitcast.48, f32[]{:T(128)} %bitcast.47, f32[]{:T(128)} %bitcast.46, ...), kind=kLoop, calls=%fused_computation.78 | loop fusion | flops 2326528 | bytes 65668 | tf_op jit(solution)/shard_map/convert_element_type | solution.py:135
  272.0 20.5 %reduce-precision_convert_fusion.5 = bf16[256,128]{1,0:T(8,128)(2,1)S(1)} fusion(f32[]{:T(128)} %bitcast.56, f32[]{:T(128)} %bitcast.55, f32[]{:T(128)} %bitcast.54, f32[]{:T(128)} %bitcast.53, f32[]{:T(128)} %bitcast.52, f32[]{:T(128)} %bitcast.51, f32[]{:T(128)} %bitcast.50, f32[]{:T(128)} %bitcast.49, f32[]{:T(128)} %bitcast.48, f32[]{:T(128)} %bitcast.47, ...), kind=kLoop, calls=%fused_computation.77 | loop fusion | flops 2293760 | bytes 65668 | tf_op jit(solution)/shard_map/convert_element_type | solution.py:135
  298.5 5.9 %all-to-all-done.2 = bf16[32,32,2048]{2,1,0:T(8,128)(2,1)} async-done(((bf16[32,32,2048]{2,1,0:T(8,128)(2,1)}), bf16[32,32,2048]{2,1,0:T(8,128)(2,1)}, u32[]{:S(2)}, u32[]{:S(2)}) %all-to-all-start.2) | async-done | bytes 4194336 | tf_op jit(solution)/shard_map/all_to_all | solution.py:173
  304.5 5.0 gather_fusion.6
  333.1 24.8 %fusion.8 = f32[2048,1024]{1,0:T(8,128)} fusion(f32[2048,1024]{1,0:T(8,128)S(1)} %bitcast_convert_fusion, f32[]{:T(128)} %bitcast.73, f32[]{:T(128)} %bitcast.72, f32[]{:T(128)} %bitcast.71, f32[]{:T(128)} %bitcast.70, f32[]{:T(128)} %bitcast.69, f32[]{:T(128)} %bitcast.68, f32[]{:T(128)} %bitcast.67, f32[]{:T(128)} %bitcast.66, f32[]{:T(128)} %bitcast.65), kind=kLoop, calls=%fused_computation.28 | loop fusion | flops 35651584 | bytes 16777252 | tf_op jit(solution)/shard_map/add | solution.py:166
  365.3 5.6 gather_fusion.2
  372.1 69.9 %all-gather.2.cloned.1.call-done = bf16[4096,2048]{1,0:T(8,128)(2,1)} async-done(((bf16[128,2048]{1,0:T(8,128)(2,1)}), bf16[4096,2048]{1,0:T(8,128)(2,1)}) %all-gather.2.cloned.1.call-update) | async-done | bytes 16777232 | tf_op jit(solution)/shard_map/all_gather | solution.py:248
  442.1 14.2 %gather_fusion.1 = bf16[256,8,2048]{2,1,0:T(8,128)(2,1)} fusion(bf16[512,8,2048]{2,1,0:T(8,128)(2,1)} %bitcast.132, s32[1024]{0:T(1024)S(1)} %pad_clamp_fusion.1), kind=kCustom, calls=%fused_computation.5 | custom fusion | bytes 16778240 | tf_op jit(solution)/shard_map/jit(_take)/gather | solution.py:270
  456.3 16.8 %fusion.19 = f32[2048,1024]{1,0:T(8,128)} fusion(f32[2048,1024]{1,0:T(8,128)} %fusion.8, bf16[256,8,2048]{2,1,0:T(8,128)(2,1)} %gather_fusion.1, pred[2048]{0:T(1024)(128)(4,1)S(1)} %broadcast_in_dim.241), kind=kOutput, calls=%fused_computation.41 | convolution fusion | flops 8600420352 | bytes 25167872 | tf_op jit(solution)/shard_map/dot_general | solution.py:275
  473.0 13.8 %fusion.21 = f32[2048,1024]{1,0:T(8,128)} fusion(f32[2048,1024]{1,0:T(8,128)} %fusion.8, bf16[256,8,2048]{2,1,0:T(8,128)(2,1)S(1)} %copy-done, pred[2048]{0:T(1024)(128)(4,1)S(1)} %broadcast_in_dim.241), kind=kOutput, calls=%fused_computation.42 | convolution fusion | flops 8598323200 | bytes 25167872 | tf_op jit(solution)/shard_map/dot_general | solution.py:275
  486.9 23.3 %scatter_custom_fusion.2 = f32[2048,1024]{1,0:T(8,128)} fusion(s32[2048]{0:T(1024)S(1)} %bitcast.140, f32[2048,1024]{1,0:T(8,128)} %fusion.21, f32[2048,1024]{1,0:T(8,128)} %fusion.19, f32[]{:T(128)} %constant.62.clone.1), kind=kCustom, calls=%fused_computation.39 | custom fusion | flops 4194304 | bytes 25165828 | tf_op jit(solution)/shard_map/scatter-add | solution.py:281
  517.0 9.8 %collective-permute-done.low_ref = f32[4,64,1024]{2,1,0:T(8,128)S(1)} collective-permute-done((f32[4,64,1024]{2,1,0:T(8,128)S(1)}, f32[4,64,1024]{2,1,0:T(8,128)S(1)}, u32[]{:S(2)}, u32[]{:S(2)}) %collective-permute-start) | collective-permute-done | bytes 1048608 | tf_op jit(solution)/shard_map/ppermute | solution.py:103
  544.3 8.8 %shard_map.87.middle_ref = f32[32,48,1024]{2,1,0:T(8,128)} custom-call(f32[9]{0:T(128)} %taps_ref.5, f32[32,64,1024]{2,1,0:T(8,128)} %bitcast.121, f32[4,64,1024]{2,1,0:T(8,128)} %copy-done.1, f32[4,64,1024]{2,1,0:T(8,128)} %collective-permute-done.1.high_ref), custom_call_target="tpu_custom_call" | custom-call | flops 62914560 | bytes 15728640 | tf_op jit(solution)/shard_map/pallas_call | solution.py:31
  554.9 14.0 %shard_map.88 = f32[32,64,1024]{2,1,0:T(8,128)} custom-call(f32[9]{0:T(128)} %taps_ref.5, f32[32,16,1024]{2,1,0:T(8,128)} %shard_map.86.first_ref.last_ref, f32[32,48,1024]{2,1,0:T(8,128)} %shard_map.87.middle_ref, f32[32,16,1024]{2,1,0:T(8,128)} %shard_map.86.first_ref.last_ref, f32[32,4,1024]{2,1,0:T(4,128)} %copy-done.4, f32[32,4,1024]{2,1,0:T(4,128)} %copy-done.3), custom_call_target="tpu_custom_call" | custom-call | flops 37748736 | bytes 18454936 | tf_op jit(solution)/shard_map/pallas_call | solution.py:75
  (124 shorter events, 75.5 us)
Async XLA Ops:
  11.7 13.7 %all-to-all-start = ((s32[32,1,64]{2,1,0:T(1,128)}), s32[32,1,64]{2,1,0:T(1,128)S(1)}, u32[]{:S(2)}, u32[]{:S(2)}) async-start(s32[32,1,64]{2,1,0:T(1,128)} %bitcast.4), calls=%async_computation | async-start | bytes 32768 | tf_op jit(solution)/shard_map/all_to_all | solution.py:205
  42.1 157.2 %all-to-all-start.1 = ((bf16[32,32,2048]{2,1,0:T(8,128)(2,1)}), bf16[32,32,2048]{2,1,0:T(8,128)(2,1)}, u32[]{:S(2)}, u32[]{:S(2)}) async-start(bf16[32,32,2048]{2,1,0:T(8,128)(2,1)} %bitcast.134), calls=%async_computation.1 | async-start | bytes 8388608 | tf_op jit(solution)/shard_map/all_to_all | solution.py:173
  199.3 9.6 %copy-start.2 = (f32[33]{0:T(128)S(1)}, f32[33]{0:T(128)}, u32[]{:S(2)}) copy-start(f32[33]{0:T(128)} %param.14) | copy-start | bytes 400
  199.3 93.3 %copy-start.5 = (bf16[128,2048]{1,0:T(8,128)(2,1)S(1)}, bf16[128,2048]{1,0:T(8,128)(2,1)}, u32[]{:S(2)}) copy-start(bf16[128,2048]{1,0:T(8,128)(2,1)} %param.13) | copy-start | bytes 1572868
  199.3 105.2 %all-to-all-start.2 = ((bf16[32,32,2048]{2,1,0:T(8,128)(2,1)}), bf16[32,32,2048]{2,1,0:T(8,128)(2,1)}, u32[]{:S(2)}, u32[]{:S(2)}) async-start(bf16[32,32,2048]{2,1,0:T(8,128)(2,1)} %bitcast.133), calls=%async_computation.2 | async-start | bytes 8388608 | tf_op jit(solution)/shard_map/all_to_all | solution.py:173
  208.7 233.4 %all-gather.2.cloned.1.call-start = ((), (), s32[]{:S(2)}) async-start(), calls=%async_computation.3 | async-start | bytes 17301504 | tf_op jit(solution)/shard_map/all_gather | solution.py:248
  322.4 6.8 %copy-start.6 = (f32[9]{0:T(128)S(1)}, f32[9]{0:T(128)}, u32[]{:S(2)}) copy-start(f32[9]{0:T(128)} %taps_ref.5) | copy-start | bytes 112
  456.3 16.8 %copy-start = (bf16[256,8,2048]{2,1,0:T(8,128)(2,1)S(1)}, bf16[256,8,2048]{2,1,0:T(8,128)(2,1)}, u32[]{:S(2)}) copy-start(bf16[256,8,2048]{2,1,0:T(8,128)(2,1)} %gather_fusion.1) | copy-start | bytes 25165828
  511.8 15.0 %collective-permute-start = (f32[4,64,1024]{2,1,0:T(8,128)S(1)}, f32[4,64,1024]{2,1,0:T(8,128)S(1)}, u32[]{:S(2)}, u32[]{:S(2)}) collective-permute-start(f32[4,64,1024]{2,1,0:T(8,128)S(1)} %bitcast.137), channel_id=1, source_target_pairs={{0,8},{8,16},{16,24},{1,9},{9,17},{17,25},{2,10},{10,18},{18,26},{... | collective-permute-start | bytes 3145736 | tf_op jit(solution)/shard_map/ppermute | solution.py:103
  515.0 16.2 %collective-permute-start.1 = (f32[4,64,1024]{2,1,0:T(8,128)S(1)}, f32[4,64,1024]{2,1,0:T(8,128)}, u32[]{:S(2)}, u32[]{:S(2)}) collective-permute-start(f32[4,64,1024]{2,1,0:T(8,128)S(1)} %bitcast.136), channel_id=1, source_target_pairs={{8,0},{16,8},{24,16},{9,1},{17,9},{25,17},{10,2},{18,10},{26,18},{... | collective-permute-start | bytes 3145736 | tf_op jit(solution)/shard_map/ppermute | solution.py:106
  526.8 4.5 copy-start.1
  537.7 15.5 %collective-permute-start.3 = (f32[32,4,1024]{2,1,0:T(4,128)}, f32[32,4,1024]{2,1,0:T(4,128)S(1)}, u32[]{:S(2)}, u32[]{:S(2)}) collective-permute-start(f32[32,4,1024]{2,1,0:T(4,128)} %get-tuple-element.40), channel_id=1, source_target_pairs={{1,0},{2,1},{3,2},{4,3},{5,4},{6,5},{7,6},{9,8},{10,9},{11,10},{12... | collective-permute-start | bytes 1572872 | tf_op jit(solution)/shard_map/ppermute | solution.py:106
  539.0 14.2 %collective-permute-start.2 = (f32[32,4,1024]{2,1,0:T(4,128)S(1)}, f32[32,4,1024]{2,1,0:T(4,128)S(1)}, u32[]{:S(2)}, u32[]{:S(2)}) collective-permute-start(f32[32,4,1024]{2,1,0:T(4,128)S(1)} %get-tuple-element.41), channel_id=1, source_target_pairs={{0,1},{1,2},{2,3},{3,4},{4,5},{5,6},{6,7},{8,9},{9,10},{10,11},{11... | collective-permute-start | bytes 1572872 | tf_op jit(solution)/shard_map/ppermute | solution.py:103
  553.2 0.9 copy-start.3
  554.1 0.8 copy-start.4
Sparse Core Ops, SparseCore 0:
  329.3 112.6 all-gather.1

commit v14 on v12

--- a/solution.py
+++ b/solution.py
@@ -68,7 +68,7 @@
     lax.fori_loop(0, out_ref.shape[2] // lanes, lane_chunk, 0)
 
 
-def smooth_y(edges, middle, low, high, taps, tx=4):
+def smooth_y(edges, middle, low, high, taps, tx=8):
     nx, two_edge, nz = edges.shape
     edge = two_edge // 2
     ny = middle.shape[1] + two_edge

time: 518 us -> 517 us (level)
  no operation moved by 1% of the time
where the time goes in v14:
time: 517 us; the launch traced here: 509 us
  other arithmetic  144 us (28%)
  waiting for transfers between devices  110 us (21%)
  local copies, waits for them, and re-layouts  73.8 us (14%)
  blocking collectives  73.2 us (14%)
  matrix products  48.3 us (9%)
  Pallas kernels  26.3 us (5%)
  starting transfers between devices  18 us (3%)
  between operations  15.1 us (3%)
    all_to_all x2, waiting for transfers between devices, traverse(): lax.all_to_all(blocks, ('inline', 'xline'), split_axis=0, concat_axis=0,...  85.3 us
    convert_element_type x7, other arithmetic, split(): return (high.astype(jnp.bfloat16), (x - high).astype(jnp.bfloat16))  83.6 us
    all_gather x1, blocking collectives, local(): tables_all = jnp.round(lax.all_gather(tables, axes, axis=0, tiled=True))  59.6 us
    add x1, other arithmetic, filter_padded(): result + taps[offset] * lax.slice_in_dim(padded, offset, offset + length,...  24.6 us
    scatter-add x1, other arithmetic, local(): raw_gradient = jnp.zeros((cell_count, depth_len), jnp.float32).at[cells.r...  23.1 us
    dot_general x2, matrix products, local(): lax.dot_general(jnp.take(tile_rows, wanted, axis=0), weight_matrix, contr...  17.1 us
    dot_general x1, matrix products, local(): jnp.dot(flat, w_low, preferred_element_type=jnp.float32)  16.2 us
    gather x2, local copies, waits for them, and re-layouts, local(): jnp.take(tile_rows, wanted, axis=0)  15.4 us
  transfers between devices with their start and end apart: 7, of which 5 were waited for; matrix products, arithmetic and copies ran while one was open for 30% of the time, Pallas kernels for 2%

profile of v14, /device:TPU:1, one launch (start us, length us, event | category | flops | bytes accessed | tf_op | source)
XLA Modules:
  0.0 509.2 jit_solution(6767251467540957528)
XLA Ops:
  11.1 13.6 %all_to_all.19 = s32[32,1,64]{2,1,0:T(1,128)S(1)} all-to-all(s32[32,1,64]{2,1,0:T(1,128)S(1)} %bitcast.140), channel_id=1, replica_groups=mesh['inline'=4,'xline'=8] {'inline','xline'}, dimensions={0} | all-to-all | bytes 16384 | tf_op jit(solution)/shard_map/all_to_all | solution.py:206
  25.1 7.7 %gather_fusion.3 = bf16[1024,1024]{1,0:T(8,128)(2,1)S(1)} fusion(bf16[2048,1024]{1,0:T(8,128)(2,1)} %bitcast.118, s32[1024]{0:T(1024)S(1)} %fusion.82), kind=kCustom, calls=%fused_computation.clone | custom fusion | bytes 4198400 | tf_op jit(solution)/shard_map/jit(_take)/gather | solution.py:223
  32.8 8.6 %fusion.27 = bf16[1024,2048]{1,0:T(8,128)(2,1)} fusion(bf16[1,1,2048,1024]{3,2,1,0:T(8,128)(2,1)} %param.12, bf16[1024,1024]{1,0:T(8,128)(2,1)S(1)} %gather_fusion.3, pred[1024]{0:T(1024)(128)(4,1)S(1)} %compare_and_fusion.1), kind=kOutput, calls=%fused_computation.50 | convolution fusion | flops 4298113024 | bytes 10486784 | tf_op jit(solution)/shard_map/dot_general | solution.py:222
  45.3 7.7 %gather_fusion.5 = bf16[1024,1024]{1,0:T(8,128)(2,1)S(1)} fusion(bf16[2048,1024]{1,0:T(8,128)(2,1)} %bitcast.119, s32[1024]{0:T(1024)S(1)} %fusion.83), kind=kCustom, calls=%fused_computation.2.clone | custom fusion | bytes 4198400 | tf_op jit(solution)/shard_map/jit(_take)/gather | solution.py:223
  53.1 8.5 %fusion.30 = bf16[1024,2048]{1,0:T(8,128)(2,1)} fusion(bf16[1,1,2048,1024]{3,2,1,0:T(8,128)(2,1)} %param.12, bf16[1024,1024]{1,0:T(8,128)(2,1)S(1)} %gather_fusion.5, pred[1024]{0:T(1024)(128)(4,1)S(1)} %compare_and_fusion), kind=kOutput, calls=%fused_computation.51 | convolution fusion | flops 4298113024 | bytes 10486784 | tf_op jit(solution)/shard_map/dot_general | solution.py:222
  61.6 79.3 %all-to-all-done.1 = bf16[32,32,2048]{2,1,0:T(8,128)(2,1)} async-done(((bf16[32,32,2048]{2,1,0:T(8,128)(2,1)}), bf16[32,32,2048]{2,1,0:T(8,128)(2,1)}, u32[]{:S(2)}, u32[]{:S(2)}) %all-to-all-start.1) | async-done | bytes 4194336 | tf_op jit(solution)/shard_map/all_to_all | solution.py:173
  146.3 20.5 %fusion.43 = bf16[256,128]{1,0:T(8,128)(2,1)S(1)} fusion(f32[]{:T(128)} %bitcast.24, f32[]{:T(128)} %bitcast.25, f32[]{:T(128)} %bitcast.26, f32[]{:T(128)} %bitcast.27, f32[]{:T(128)} %bitcast.28, f32[]{:T(128)} %bitcast.29, f32[]{:T(128)} %bitcast.30, f32[]{:T(128)} %bitcast.31, f32[]{:T(128)} %bitcast.32, f32[]{:T(128)} %bitcast.33, f32[]{:T(128)} %bitcast.34, ...), kind=kLoop, calls=%fused_computation.79 | loop fusion | flops 2326528 | bytes 65668 | tf_op jit(solution)/shard_map/convert_element_type | solution.py:135
  166.9 20.5 %reduce-precision_convert_fusion.4 = bf16[256,128]{1,0:T(8,128)(2,1)S(1)} fusion(f32[]{:T(128)} %bitcast.24, f32[]{:T(128)} %bitcast.25, f32[]{:T(128)} %bitcast.26, f32[]{:T(128)} %bitcast.27, f32[]{:T(128)} %bitcast.28, f32[]{:T(128)} %bitcast.29, f32[]{:T(128)} %bitcast.30, f32[]{:T(128)} %bitcast.31, f32[]{:T(128)} %bitcast.32, f32[]{:T(128)} %bitcast.33, ...), kind=kLoop, calls=%fused_computation.75 | loop fusion | flops 2293760 | bytes 65668 | tf_op jit(solution)/shard_map/convert_element_type | solution.py:135
  187.4 20.5 %fusion.42 = bf16[256,128]{1,0:T(8,128)(2,1)S(1)} fusion(f32[]{:T(128)} %bitcast.56, f32[]{:T(128)} %bitcast.55, f32[]{:T(128)} %bitcast.54, f32[]{:T(128)} %bitcast.53, f32[]{:T(128)} %bitcast.52, f32[]{:T(128)} %bitcast.51, f32[]{:T(128)} %bitcast.50, f32[]{:T(128)} %bitcast.49, f32[]{:T(128)} %bitcast.48, f32[]{:T(128)} %bitcast.47, f32[]{:T(128)} %bitcast.46, ...), kind=kLoop, calls=%fused_computation.78 | loop fusion | flops 2326528 | bytes 65668 | tf_op jit(solution)/shard_map/convert_element_type | solution.py:135
  208.0 20.5 %reduce-precision_convert_fusion.5 = bf16[256,128]{1,0:T(8,128)(2,1)S(1)} fusion(f32[]{:T(128)} %bitcast.56, f32[]{:T(128)} %bitcast.55, f32[]{:T(128)} %bitcast.54, f32[]{:T(128)} %bitcast.53, f32[]{:T(128)} %bitcast.52, f32[]{:T(128)} %bitcast.51, f32[]{:T(128)} %bitcast.50, f32[]{:T(128)} %bitcast.49, f32[]{:T(128)} %bitcast.48, f32[]{:T(128)} %bitcast.47, ...), kind=kLoop, calls=%fused_computation.77 | loop fusion | flops 2293760 | bytes 65668 | tf_op jit(solution)/shard_map/convert_element_type | solution.py:135
  229.6 5.0 gather_fusion.4
  234.6 5.9 %all-to-all-done.2 = bf16[32,32,2048]{2,1,0:T(8,128)(2,1)} async-done(((bf16[32,32,2048]{2,1,0:T(8,128)(2,1)}), bf16[32,32,2048]{2,1,0:T(8,128)(2,1)}, u32[]{:S(2)}, u32[]{:S(2)}) %all-to-all-start.2) | async-done | bytes 4194336 | tf_op jit(solution)/shard_map/all_to_all | solution.py:173
  240.5 5.0 gather_fusion.6
  265.5 59.6 %all_gather.6 = f32[512,72]{1,0:T(8,128)S(1)} all-gather(f32[16,72]{1,0:T(8,128)S(1)} %add_convert_fusion), channel_id=1, replica_groups=mesh['inline'=4,'xline'=8] {'inline','xline'}, dimensions={0}, use_global_device_ids=true | all-gather | bytes 152064 | tf_op jit(solution)/shard_map/all_gather | solution.py:190
  331.3 6.0 %gather_fusion.2 = s32[512,8]{1,0:T(8,128)S(1)} fusion(s32[512,8,8]{1,2,0:T(8,128)} %copy.89, s32[512]{0:T(512)S(1)} %bitcast.122), kind=kCustom, calls=%fused_computation.6 | custom fusion | bytes 36864 | tf_op jit(solution)/shard_map/jit(take_along_axis)/gather | solution.py:260
  343.8 24.6 %fusion.8 = f32[2048,1024]{1,0:T(8,128)} fusion(f32[2048,1024]{1,0:T(8,128)S(1)} %bitcast_convert_fusion, f32[]{:T(128)} %bitcast.73, f32[]{:T(128)} %bitcast.72, f32[]{:T(128)} %bitcast.71, f32[]{:T(128)} %bitcast.70, f32[]{:T(128)} %bitcast.69, f32[]{:T(128)} %bitcast.68, f32[]{:T(128)} %bitcast.67, f32[]{:T(128)} %bitcast.66, f32[]{:T(128)} %bitcast.65), kind=kLoop, calls=%fused_computation.28 | loop fusion | flops 35651584 | bytes 16777252 | tf_op jit(solution)/shard_map/add | solution.py:166
  368.4 10.4 %all-gather.2.cloned.1.call-done = bf16[4096,2048]{1,0:T(8,128)(2,1)} async-done(((bf16[128,2048]{1,0:T(8,128)(2,1)}), bf16[4096,2048]{1,0:T(8,128)(2,1)}) %all-gather.2.cloned.1.call-update) | async-done | bytes 16777232 | tf_op jit(solution)/shard_map/all_gather | solution.py:244
  378.8 14.2 %gather_fusion.1 = bf16[256,8,2048]{2,1,0:T(8,128)(2,1)} fusion(bf16[512,8,2048]{2,1,0:T(8,128)(2,1)} %bitcast.132, s32[1024]{0:T(1024)S(1)} %pad_clamp_fusion.1), kind=kCustom, calls=%fused_computation.5 | custom fusion | bytes 16778240 | tf_op jit(solution)/shard_map/jit(_take)/gather | solution.py:266
  393.0 16.2 %fusion.19 = f32[2048,1024]{1,0:T(8,128)} fusion(f32[2048,1024]{1,0:T(8,128)} %fusion.8, bf16[256,8,2048]{2,1,0:T(8,128)(2,1)} %gather_fusion.1, pred[2048]{0:T(1024)(128)(4,1)S(1)} %broadcast_in_dim.240), kind=kOutput, calls=%fused_computation.41 | convolution fusion | flops 8600420352 | bytes 25167872 | tf_op jit(solution)/shard_map/dot_general | solution.py:271
  409.3 11.2 %fusion.21 = f32[2048,1024]{1,0:T(8,128)} fusion(f32[2048,1024]{1,0:T(8,128)S(1)} %copy-done, bf16[256,8,2048]{2,1,0:T(8,128)(2,1)S(1)} %copy-done.1, pred[2048]{0:T(1024)(128)(4,1)S(1)} %broadcast_in_dim.240), kind=kOutput, calls=%fused_computation.42 | convolution fusion | flops 8598323200 | bytes 25167872 | tf_op jit(solution)/shard_map/dot_general | solution.py:271
  420.4 23.1 %scatter_custom_fusion.2 = f32[2048,1024]{1,0:T(8,128)} fusion(s32[2048]{0:T(1024)S(1)} %bitcast.141, f32[2048,1024]{1,0:T(8,128)} %fusion.21, f32[2048,1024]{1,0:T(8,128)} %fusion.19, f32[]{:T(128)} %constant.62.clone.1), kind=kCustom, calls=%fused_computation.39 | custom fusion | flops 4194304 | bytes 25165828 | tf_op jit(solution)/shard_map/scatter-add | solution.py:277
  450.2 9.8 %collective-permute-done.low_ref = f32[4,64,1024]{2,1,0:T(8,128)S(1)} collective-permute-done((f32[4,64,1024]{2,1,0:T(8,128)S(1)}, f32[4,64,1024]{2,1,0:T(8,128)S(1)}, u32[]{:S(2)}, u32[]{:S(2)}) %collective-permute-start) | collective-permute-done | bytes 1048608 | tf_op jit(solution)/shard_map/ppermute | solution.py:103
  477.8 8.8 %shard_map.87.middle_ref = f32[32,48,1024]{2,1,0:T(8,128)} custom-call(f32[9]{0:T(128)} %taps_ref.5, f32[32,64,1024]{2,1,0:T(8,128)} %bitcast.121, f32[4,64,1024]{2,1,0:T(8,128)} %copy-done.2, f32[4,64,1024]{2,1,0:T(8,128)} %collective-permute-done.1.high_ref), custom_call_target="tpu_custom_call" | custom-call | flops 62914560 | bytes 15728640 | tf_op jit(solution)/shard_map/pallas_call | solution.py:31
  488.2 13.7 %shard_map.88 = f32[32,64,1024]{2,1,0:T(8,128)} custom-call(f32[9]{0:T(128)} %taps_ref.5, f32[32,16,1024]{2,1,0:T(8,128)} %shard_map.86.first_ref.last_ref, f32[32,48,1024]{2,1,0:T(8,128)} %shard_map.87.middle_ref, f32[32,16,1024]{2,1,0:T(8,128)} %shard_map.86.first_ref.last_ref, f32[32,4,1024]{2,1,0:T(4,128)} %copy-done.5, f32[32,4,1024]{2,1,0:T(4,128)} %copy-done.4), custom_call_target="tpu_custom_call" | custom-call | flops 37748736 | bytes 18454936 | tf_op jit(solution)/shard_map/pallas_call | solution.py:75
  (128 shorter events, 72.9 us)
Async XLA Ops:
  41.4 99.6 %all-to-all-start.1 = ((bf16[32,32,2048]{2,1,0:T(8,128)(2,1)}), bf16[32,32,2048]{2,1,0:T(8,128)(2,1)}, u32[]{:S(2)}, u32[]{:S(2)}) async-start(bf16[32,32,2048]{2,1,0:T(8,128)(2,1)} %bitcast.134), calls=%async_computation.1 | async-start | bytes 8388608 | tf_op jit(solution)/shard_map/all_to_all | solution.py:173
  61.6 83.3 %copy-start.3 = (f32[33]{0:T(128)S(1)}, f32[33]{0:T(128)}, u32[]{:S(2)}) copy-start(f32[33]{0:T(128)} %param.14) | copy-start | bytes 400
  61.6 166.9 %copy-start.6 = (bf16[128,2048]{1,0:T(8,128)(2,1)S(1)}, bf16[128,2048]{1,0:T(8,128)(2,1)}, u32[]{:S(2)}) copy-start(bf16[128,2048]{1,0:T(8,128)(2,1)} %param.13) | copy-start | bytes 1572868
  140.9 99.5 %all-to-all-start.2 = ((bf16[32,32,2048]{2,1,0:T(8,128)(2,1)}), bf16[32,32,2048]{2,1,0:T(8,128)(2,1)}, u32[]{:S(2)}, u32[]{:S(2)}) async-start(bf16[32,32,2048]{2,1,0:T(8,128)(2,1)} %bitcast.133), calls=%async_computation.2 | async-start | bytes 8388608 | tf_op jit(solution)/shard_map/all_to_all | solution.py:173
  144.7 234.1 %all-gather.2.cloned.1.call-start = ((), (), s32[]{:S(2)}) async-start(), calls=%async_computation.3 | async-start | bytes 17301504 | tf_op jit(solution)/shard_map/all_gather | solution.py:244
  258.4 6.8 %copy-start.8 = (s32[128,8]{0,1:T(8,128)S(1)}, s32[128,8]{0,1:T(8,128)}, u32[]{:S(2)}) copy-start(s32[128,8]{0,1:T(8,128)} %param.17) | copy-start | bytes 12292
  262.1 77.8 %copy-start.7 = (f32[9]{0:T(128)S(1)}, f32[9]{0:T(128)}, u32[]{:S(2)}) copy-start(f32[9]{0:T(128)} %taps_ref.5) | copy-start | bytes 112
  393.0 16.2 %copy-start = (f32[2048,1024]{1,0:T(8,128)S(1)}, f32[2048,1024]{1,0:T(8,128)}, u32[]{:S(2)}) copy-start(f32[2048,1024]{1,0:T(8,128)} %fusion.8) | copy-start | bytes 25165828
  393.0 16.2 %copy-start.1 = (bf16[256,8,2048]{2,1,0:T(8,128)(2,1)S(1)}, bf16[256,8,2048]{2,1,0:T(8,128)(2,1)}, u32[]{:S(2)}) copy-start(bf16[256,8,2048]{2,1,0:T(8,128)(2,1)} %gather_fusion.1) | copy-start | bytes 25165828
  445.2 14.9 %collective-permute-start = (f32[4,64,1024]{2,1,0:T(8,128)S(1)}, f32[4,64,1024]{2,1,0:T(8,128)S(1)}, u32[]{:S(2)}, u32[]{:S(2)}) collective-permute-start(f32[4,64,1024]{2,1,0:T(8,128)S(1)} %bitcast.137), channel_id=1, source_target_pairs={{0,8},{8,16},{16,24},{1,9},{9,17},{17,25},{2,10},{10,18},{18,26},{... | collective-permute-start | bytes 3145736 | tf_op jit(solution)/shard_map/ppermute | solution.py:103
  448.3 16.4 %collective-permute-start.1 = (f32[4,64,1024]{2,1,0:T(8,128)S(1)}, f32[4,64,1024]{2,1,0:T(8,128)}, u32[]{:S(2)}, u32[]{:S(2)}) collective-permute-start(f32[4,64,1024]{2,1,0:T(8,128)S(1)} %bitcast.136), channel_id=1, source_target_pairs={{8,0},{16,8},{24,16},{9,1},{17,9},{25,17},{10,2},{18,10},{26,18},{... | collective-permute-start | bytes 3145736 | tf_op jit(solution)/shard_map/ppermute | solution.py:106
  460.0 4.7 copy-start.2
  471.2 15.5 %collective-permute-start.3 = (f32[32,4,1024]{2,1,0:T(4,128)}, f32[32,4,1024]{2,1,0:T(4,128)S(1)}, u32[]{:S(2)}, u32[]{:S(2)}) collective-permute-start(f32[32,4,1024]{2,1,0:T(4,128)} %get-tuple-element.32), channel_id=1, source_target_pairs={{1,0},{2,1},{3,2},{4,3},{5,4},{6,5},{7,6},{9,8},{10,9},{11,10},{12... | collective-permute-start | bytes 1572872 | tf_op jit(solution)/shard_map/ppermute | solution.py:106
  472.4 14.2 %collective-permute-start.2 = (f32[32,4,1024]{2,1,0:T(4,128)S(1)}, f32[32,4,1024]{2,1,0:T(4,128)S(1)}, u32[]{:S(2)}, u32[]{:S(2)}) collective-permute-start(f32[32,4,1024]{2,1,0:T(4,128)S(1)} %get-tuple-element.33), channel_id=1, source_target_pairs={{0,1},{1,2},{2,3},{3,4},{4,5},{5,6},{6,7},{8,9},{9,10},{10,11},{11... | collective-permute-start | bytes 1572872 | tf_op jit(solution)/shard_map/ppermute | solution.py:103
  486.6 0.8 copy-start.4
  487.4 0.8 copy-start.5
Sparse Core Ops, SparseCore 0:
  265.3 113.4 all-gather.1

commit v15 on v14

--- a/solution.py
+++ b/solution.py
@@ -59,10 +59,11 @@
 
     def lane_chunk(c, carry):
         cols = pl.ds(pl.multiple_of(c * lanes, lanes), lanes)
-        out = taps_ref[0] * ext_ref[:, pl.ds(HW, ny), cols]
-        for j in range(1, 2 * HW + 1):
-            out = out + taps_ref[j] * ext_ref[:, pl.ds(HW + j, ny), cols]
-        out_ref[:, :, cols] = out
+        for row in range(out_ref.shape[0]):
+            out = taps_ref[0] * ext_ref[row, pl.ds(HW, ny), cols]
+            for j in range(1, 2 * HW + 1):
+                out = out + taps_ref[j] * ext_ref[row, pl.ds(HW + j, ny), cols]
+            out_ref[row, :, cols] = out
         return carry
 
     lax.fori_loop(0, out_ref.shape[2] // lanes, lane_chunk, 0)

time: 517 us -> 518 us (level)
  no operation moved by 1% of the time
where the time goes in v15:
time: 518 us; the launch traced here: 509 us
  other arithmetic  144 us (28%)
  waiting for transfers between devices  110 us (21%)
  local copies, waits for them, and re-layouts  73.9 us (14%)
  blocking collectives  73.2 us (14%)
  matrix products  48.3 us (9%)
  Pallas kernels  26.5 us (5%)
  starting transfers between devices  18.1 us (3%)
  between operations  15.1 us (3%)
    all_to_all x2, waiting for transfers between devices, traverse(): lax.all_to_all(blocks, ('inline', 'xline'), split_axis=0, concat_axis=0,...  85.3 us
    convert_element_type x7, other arithmetic, split(): return (high.astype(jnp.bfloat16), (x - high).astype(jnp.bfloat16))  83.6 us
    all_gather x1, blocking collectives, local(): tables_all = jnp.round(lax.all_gather(tables, axes, axis=0, tiled=True))  59.6 us
    add x1, other arithmetic, filter_padded(): result + taps[offset] * lax.slice_in_dim(padded, offset, offset + length,...  24.6 us
    scatter-add x1, other arithmetic, local(): raw_gradient = jnp.zeros((cell_count, depth_len), jnp.float32).at[cells.r...  23.1 us
    dot_general x2, matrix products, local(): lax.dot_general(jnp.take(tile_rows, wanted, axis=0), weight_matrix, contr...  17.1 us
    dot_general x1, matrix products, local(): jnp.dot(flat, w_low, preferred_element_type=jnp.float32)  16.2 us
    gather x2, local copies, waits for them, and re-layouts, local(): jnp.take(tile_rows, wanted, axis=0)  15.4 us
  transfers between devices with their start and end apart: 7, of which 5 were waited for; matrix products, arithmetic and copies ran while one was open for 30% of the time, Pallas kernels for 2%

profile of v15, /device:TPU:1, one launch (start us, length us, event | category | flops | bytes accessed | tf_op | source)
XLA Modules:
  0.0 509.5 jit_solution(4829487454051239096)
XLA Ops:
  11.1 13.6 %all_to_all.19 = s32[32,1,64]{2,1,0:T(1,128)S(1)} all-to-all(s32[32,1,64]{2,1,0:T(1,128)S(1)} %bitcast.140), channel_id=1, replica_groups=mesh['inline'=4,'xline'=8] {'inline','xline'}, dimensions={0} | all-to-all | bytes 16384 | tf_op jit(solution)/shard_map/all_to_all | solution.py:207
  25.1 7.7 %gather_fusion.3 = bf16[1024,1024]{1,0:T(8,128)(2,1)S(1)} fusion(bf16[2048,1024]{1,0:T(8,128)(2,1)} %bitcast.118, s32[1024]{0:T(1024)S(1)} %fusion.82), kind=kCustom, calls=%fused_computation.clone | custom fusion | bytes 4198400 | tf_op jit(solution)/shard_map/jit(_take)/gather | solution.py:224
  32.8 8.6 %fusion.27 = bf16[1024,2048]{1,0:T(8,128)(2,1)} fusion(bf16[1,1,2048,1024]{3,2,1,0:T(8,128)(2,1)} %param.12, bf16[1024,1024]{1,0:T(8,128)(2,1)S(1)} %gather_fusion.3, pred[1024]{0:T(1024)(128)(4,1)S(1)} %compare_and_fusion.1), kind=kOutput, calls=%fused_computation.50 | convolution fusion | flops 4298113024 | bytes 10486784 | tf_op jit(solution)/shard_map/dot_general | solution.py:223
  45.3 7.7 %gather_fusion.5 = bf16[1024,1024]{1,0:T(8,128)(2,1)S(1)} fusion(bf16[2048,1024]{1,0:T(8,128)(2,1)} %bitcast.119, s32[1024]{0:T(1024)S(1)} %fusion.83), kind=kCustom, calls=%fused_computation.2.clone | custom fusion | bytes 4198400 | tf_op jit(solution)/shard_map/jit(_take)/gather | solution.py:224
  53.1 8.5 %fusion.30 = bf16[1024,2048]{1,0:T(8,128)(2,1)} fusion(bf16[1,1,2048,1024]{3,2,1,0:T(8,128)(2,1)} %param.12, bf16[1024,1024]{1,0:T(8,128)(2,1)S(1)} %gather_fusion.5, pred[1024]{0:T(1024)(128)(4,1)S(1)} %compare_and_fusion), kind=kOutput, calls=%fused_computation.51 | convolution fusion | flops 4298113024 | bytes 10486784 | tf_op jit(solution)/shard_map/dot_general | solution.py:223
  61.6 79.3 %all-to-all-done.1 = bf16[32,32,2048]{2,1,0:T(8,128)(2,1)} async-done(((bf16[32,32,2048]{2,1,0:T(8,128)(2,1)}), bf16[32,32,2048]{2,1,0:T(8,128)(2,1)}, u32[]{:S(2)}, u32[]{:S(2)}) %all-to-all-start.1) | async-done | bytes 4194336 | tf_op jit(solution)/shard_map/all_to_all | solution.py:174
  146.3 20.5 %fusion.43 = bf16[256,128]{1,0:T(8,128)(2,1)S(1)} fusion(f32[]{:T(128)} %bitcast.24, f32[]{:T(128)} %bitcast.25, f32[]{:T(128)} %bitcast.26, f32[]{:T(128)} %bitcast.27, f32[]{:T(128)} %bitcast.28, f32[]{:T(128)} %bitcast.29, f32[]{:T(128)} %bitcast.30, f32[]{:T(128)} %bitcast.31, f32[]{:T(128)} %bitcast.32, f32[]{:T(128)} %bitcast.33, f32[]{:T(128)} %bitcast.34, ...), kind=kLoop, calls=%fused_computation.79 | loop fusion | flops 2326528 | bytes 65668 | tf_op jit(solution)/shard_map/convert_element_type | solution.py:136
  166.9 20.5 %reduce-precision_convert_fusion.4 = bf16[256,128]{1,0:T(8,128)(2,1)S(1)} fusion(f32[]{:T(128)} %bitcast.24, f32[]{:T(128)} %bitcast.25, f32[]{:T(128)} %bitcast.26, f32[]{:T(128)} %bitcast.27, f32[]{:T(128)} %bitcast.28, f32[]{:T(128)} %bitcast.29, f32[]{:T(128)} %bitcast.30, f32[]{:T(128)} %bitcast.31, f32[]{:T(128)} %bitcast.32, f32[]{:T(128)} %bitcast.33, ...), kind=kLoop, calls=%fused_computation.75 | loop fusion | flops 2293760 | bytes 65668 | tf_op jit(solution)/shard_map/convert_element_type | solution.py:136
  187.4 20.5 %fusion.42 = bf16[256,128]{1,0:T(8,128)(2,1)S(1)} fusion(f32[]{:T(128)} %bitcast.56, f32[]{:T(128)} %bitcast.55, f32[]{:T(128)} %bitcast.54, f32[]{:T(128)} %bitcast.53, f32[]{:T(128)} %bitcast.52, f32[]{:T(128)} %bitcast.51, f32[]{:T(128)} %bitcast.50, f32[]{:T(128)} %bitcast.49, f32[]{:T(128)} %bitcast.48, f32[]{:T(128)} %bitcast.47, f32[]{:T(128)} %bitcast.46, ...), kind=kLoop, calls=%fused_computation.78 | loop fusion | flops 2326528 | bytes 65668 | tf_op jit(solution)/shard_map/convert_element_type | solution.py:136
  208.0 20.5 %reduce-precision_convert_fusion.5 = bf16[256,128]{1,0:T(8,128)(2,1)S(1)} fusion(f32[]{:T(128)} %bitcast.56, f32[]{:T(128)} %bitcast.55, f32[]{:T(128)} %bitcast.54, f32[]{:T(128)} %bitcast.53, f32[]{:T(128)} %bitcast.52, f32[]{:T(128)} %bitcast.51, f32[]{:T(128)} %bitcast.50, f32[]{:T(128)} %bitcast.49, f32[]{:T(128)} %bitcast.48, f32[]{:T(128)} %bitcast.47, ...), kind=kLoop, calls=%fused_computation.77 | loop fusion | flops 2293760 | bytes 65668 | tf_op jit(solution)/shard_map/convert_element_type | solution.py:136
  229.6 5.0 gather_fusion.4
  234.6 5.9 %all-to-all-done.2 = bf16[32,32,2048]{2,1,0:T(8,128)(2,1)} async-done(((bf16[32,32,2048]{2,1,0:T(8,128)(2,1)}), bf16[32,32,2048]{2,1,0:T(8,128)(2,1)}, u32[]{:S(2)}, u32[]{:S(2)}) %all-to-all-start.2) | async-done | bytes 4194336 | tf_op jit(solution)/shard_map/all_to_all | solution.py:174
  240.5 5.0 gather_fusion.6
  265.5 59.6 %all_gather.6 = f32[512,72]{1,0:T(8,128)S(1)} all-gather(f32[16,72]{1,0:T(8,128)S(1)} %add_convert_fusion), channel_id=1, replica_groups=mesh['inline'=4,'xline'=8] {'inline','xline'}, dimensions={0}, use_global_device_ids=true | all-gather | bytes 152064 | tf_op jit(solution)/shard_map/all_gather | solution.py:191
  331.3 6.0 %gather_fusion.2 = s32[512,8]{1,0:T(8,128)S(1)} fusion(s32[512,8,8]{1,2,0:T(8,128)} %copy.89, s32[512]{0:T(512)S(1)} %bitcast.122), kind=kCustom, calls=%fused_computation.6 | custom fusion | bytes 36864 | tf_op jit(solution)/shard_map/jit(take_along_axis)/gather | solution.py:261
  343.8 24.6 %fusion.8 = f32[2048,1024]{1,0:T(8,128)} fusion(f32[2048,1024]{1,0:T(8,128)S(1)} %bitcast_convert_fusion, f32[]{:T(128)} %bitcast.73, f32[]{:T(128)} %bitcast.72, f32[]{:T(128)} %bitcast.71, f32[]{:T(128)} %bitcast.70, f32[]{:T(128)} %bitcast.69, f32[]{:T(128)} %bitcast.68, f32[]{:T(128)} %bitcast.67, f32[]{:T(128)} %bitcast.66, f32[]{:T(128)} %bitcast.65), kind=kLoop, calls=%fused_computation.28 | loop fusion | flops 35651584 | bytes 16777252 | tf_op jit(solution)/shard_map/add | solution.py:167
  368.4 10.4 %all-gather.2.cloned.1.call-done = bf16[4096,2048]{1,0:T(8,128)(2,1)} async-done(((bf16[128,2048]{1,0:T(8,128)(2,1)}), bf16[4096,2048]{1,0:T(8,128)(2,1)}) %all-gather.2.cloned.1.call-update) | async-done | bytes 16777232 | tf_op jit(solution)/shard_map/all_gather | solution.py:245
  378.8 14.3 %gather_fusion.1 = bf16[256,8,2048]{2,1,0:T(8,128)(2,1)} fusion(bf16[512,8,2048]{2,1,0:T(8,128)(2,1)} %bitcast.132, s32[1024]{0:T(1024)S(1)} %pad_clamp_fusion.1), kind=kCustom, calls=%fused_computation.5 | custom fusion | bytes 16778240 | tf_op jit(solution)/shard_map/jit(_take)/gather | solution.py:267
  393.1 16.2 %fusion.19 = f32[2048,1024]{1,0:T(8,128)} fusion(f32[2048,1024]{1,0:T(8,128)} %fusion.8, bf16[256,8,2048]{2,1,0:T(8,128)(2,1)} %gather_fusion.1, pred[2048]{0:T(1024)(128)(4,1)S(1)} %broadcast_in_dim.240), kind=kOutput, calls=%fused_computation.41 | convolution fusion | flops 8600420352 | bytes 25167872 | tf_op jit(solution)/shard_map/dot_general | solution.py:272
  409.3 11.2 %fusion.21 = f32[2048,1024]{1,0:T(8,128)} fusion(f32[2048,1024]{1,0:T(8,128)S(1)} %copy-done, bf16[256,8,2048]{2,1,0:T(8,128)(2,1)S(1)} %copy-done.1, pred[2048]{0:T(1024)(128)(4,1)S(1)} %broadcast_in_dim.240), kind=kOutput, calls=%fused_computation.42 | convolution fusion | flops 8598323200 | bytes 25167872 | tf_op jit(solution)/shard_map/dot_general | solution.py:272
  420.5 23.1 %scatter_custom_fusion.2 = f32[2048,1024]{1,0:T(8,128)} fusion(s32[2048]{0:T(1024)S(1)} %bitcast.141, f32[2048,1024]{1,0:T(8,128)} %fusion.21, f32[2048,1024]{1,0:T(8,128)} %fusion.19, f32[]{:T(128)} %constant.62.clone.1), kind=kCustom, calls=%fused_computation.39 | custom fusion | flops 4194304 | bytes 25165828 | tf_op jit(solution)/shard_map/scatter-add | solution.py:278
  450.4 9.8 %collective-permute-done.low_ref = f32[4,64,1024]{2,1,0:T(8,128)S(1)} collective-permute-done((f32[4,64,1024]{2,1,0:T(8,128)S(1)}, f32[4,64,1024]{2,1,0:T(8,128)S(1)}, u32[]{:S(2)}, u32[]{:S(2)}) %collective-permute-start) | collective-permute-done | bytes 1048608 | tf_op jit(solution)/shard_map/ppermute | solution.py:104
  477.9 8.8 %shard_map.87.middle_ref = f32[32,48,1024]{2,1,0:T(8,128)} custom-call(f32[9]{0:T(128)} %taps_ref.5, f32[32,64,1024]{2,1,0:T(8,128)} %bitcast.121, f32[4,64,1024]{2,1,0:T(8,128)} %copy-done.2, f32[4,64,1024]{2,1,0:T(8,128)} %collective-permute-done.1.high_ref), custom_call_target="tpu_custom_call" | custom-call | flops 62914560 | bytes 15728640 | tf_op jit(solution)/shard_map/pallas_call | solution.py:31
  488.3 13.8 %shard_map.88 = f32[32,64,1024]{2,1,0:T(8,128)} custom-call(f32[9]{0:T(128)} %taps_ref.5, f32[32,16,1024]{2,1,0:T(8,128)} %shard_map.86.first_ref.last_ref, f32[32,48,1024]{2,1,0:T(8,128)} %shard_map.87.middle_ref, f32[32,16,1024]{2,1,0:T(8,128)} %shard_map.86.first_ref.last_ref, f32[32,4,1024]{2,1,0:T(4,128)} %copy-done.5, f32[32,4,1024]{2,1,0:T(4,128)} %copy-done.4), custom_call_target="tpu_custom_call" | custom-call | flops 37748736 | bytes 18454936 | tf_op jit(solution)/shard_map/pallas_call | solution.py:76
  (128 shorter events, 73.0 us)
Async XLA Ops:
  41.4 99.6 %all-to-all-start.1 = ((bf16[32,32,2048]{2,1,0:T(8,128)(2,1)}), bf16[32,32,2048]{2,1,0:T(8,128)(2,1)}, u32[]{:S(2)}, u32[]{:S(2)}) async-start(bf16[32,32,2048]{2,1,0:T(8,128)(2,1)} %bitcast.134), calls=%async_computation.1 | async-start | bytes 8388608 | tf_op jit(solution)/shard_map/all_to_all | solution.py:174
  61.6 83.3 %copy-start.3 = (f32[33]{0:T(128)S(1)}, f32[33]{0:T(128)}, u32[]{:S(2)}) copy-start(f32[33]{0:T(128)} %param.14) | copy-start | bytes 400
  61.6 166.9 %copy-start.6 = (bf16[128,2048]{1,0:T(8,128)(2,1)S(1)}, bf16[128,2048]{1,0:T(8,128)(2,1)}, u32[]{:S(2)}) copy-start(bf16[128,2048]{1,0:T(8,128)(2,1)} %param.13) | copy-start | bytes 1572868
  140.9 99.5 %all-to-all-start.2 = ((bf16[32,32,2048]{2,1,0:T(8,128)(2,1)}), bf16[32,32,2048]{2,1,0:T(8,128)(2,1)}, u32[]{:S(2)}, u32[]{:S(2)}) async-start(bf16[32,32,2048]{2,1,0:T(8,128)(2,1)} %bitcast.133), calls=%async_computation.2 | async-start | bytes 8388608 | tf_op jit(solution)/shard_map/all_to_all | solution.py:174
  144.7 234.1 %all-gather.2.cloned.1.call-start = ((), (), s32[]{:S(2)}) async-start(), calls=%async_computation.3 | async-start | bytes 17301504 | tf_op jit(solution)/shard_map/all_gather | solution.py:245
  258.4 6.8 %copy-start.8 = (s32[128,8]{0,1:T(8,128)S(1)}, s32[128,8]{0,1:T(8,128)}, u32[]{:S(2)}) copy-start(s32[128,8]{0,1:T(8,128)} %param.17) | copy-start | bytes 12292
  262.1 77.8 %copy-start.7 = (f32[9]{0:T(128)S(1)}, f32[9]{0:T(128)}, u32[]{:S(2)}) copy-start(f32[9]{0:T(128)} %taps_ref.5) | copy-start | bytes 112
  393.1 16.2 %copy-start = (f32[2048,1024]{1,0:T(8,128)S(1)}, f32[2048,1024]{1,0:T(8,128)}, u32[]{:S(2)}) copy-start(f32[2048,1024]{1,0:T(8,128)} %fusion.8) | copy-start | bytes 25165828
  393.1 16.2 %copy-start.1 = (bf16[256,8,2048]{2,1,0:T(8,128)(2,1)S(1)}, bf16[256,8,2048]{2,1,0:T(8,128)(2,1)}, u32[]{:S(2)}) copy-start(bf16[256,8,2048]{2,1,0:T(8,128)(2,1)} %gather_fusion.1) | copy-start | bytes 25165828
  445.2 14.9 %collective-permute-start = (f32[4,64,1024]{2,1,0:T(8,128)S(1)}, f32[4,64,1024]{2,1,0:T(8,128)S(1)}, u32[]{:S(2)}, u32[]{:S(2)}) collective-permute-start(f32[4,64,1024]{2,1,0:T(8,128)S(1)} %bitcast.137), channel_id=1, source_target_pairs={{0,8},{8,16},{16,24},{1,9},{9,17},{17,25},{2,10},{10,18},{18,26},{... | collective-permute-start | bytes 3145736 | tf_op jit(solution)/shard_map/ppermute | solution.py:104
  448.4 16.4 %collective-permute-start.1 = (f32[4,64,1024]{2,1,0:T(8,128)S(1)}, f32[4,64,1024]{2,1,0:T(8,128)}, u32[]{:S(2)}, u32[]{:S(2)}) collective-permute-start(f32[4,64,1024]{2,1,0:T(8,128)S(1)} %bitcast.136), channel_id=1, source_target_pairs={{8,0},{16,8},{24,16},{9,1},{17,9},{25,17},{10,2},{18,10},{26,18},{... | collective-permute-start | bytes 3145736 | tf_op jit(solution)/shard_map/ppermute | solution.py:107
  460.2 4.7 copy-start.2
  471.3 15.5 %collective-permute-start.3 = (f32[32,4,1024]{2,1,0:T(4,128)}, f32[32,4,1024]{2,1,0:T(4,128)S(1)}, u32[]{:S(2)}, u32[]{:S(2)}) collective-permute-start(f32[32,4,1024]{2,1,0:T(4,128)} %get-tuple-element.32), channel_id=1, source_target_pairs={{1,0},{2,1},{3,2},{4,3},{5,4},{6,5},{7,6},{9,8},{10,9},{11,10},{12... | collective-permute-start | bytes 1572872 | tf_op jit(solution)/shard_map/ppermute | solution.py:107
  472.6 14.2 %collective-permute-start.2 = (f32[32,4,1024]{2,1,0:T(4,128)S(1)}, f32[32,4,1024]{2,1,0:T(4,128)S(1)}, u32[]{:S(2)}, u32[]{:S(2)}) collective-permute-start(f32[32,4,1024]{2,1,0:T(4,128)S(1)} %get-tuple-element.33), channel_id=1, source_target_pairs={{0,1},{1,2},{2,3},{3,4},{4,5},{5,6},{6,7},{8,9},{9,10},{10,11},{11... | collective-permute-start | bytes 1572872 | tf_op jit(solution)/shard_map/ppermute | solution.py:104
  486.7 0.8 copy-start.4
  487.6 0.8 copy-start.5
Sparse Core Ops, SparseCore 0:
  265.3 113.4 all-gather.1

commit v16 on v15

--- a/solution.py
+++ b/solution.py
@@ -17,10 +17,11 @@
 
     def lane_chunk(c, carry):
         cols = pl.ds(pl.multiple_of(c * lanes, lanes), lanes)
-        out = taps_ref[0] * ext_ref[0:nx, :, cols]
-        for j in range(1, 2 * HW + 1):
-            out = out + taps_ref[j] * ext_ref[j:j + nx, :, cols]
-        out_ref[:, :, cols] = out
+        for first in range(0, nx, 8):
+            out = taps_ref[0] * ext_ref[first:first + 8, :, cols]
+            for j in range(1, 2 * HW + 1):
+                out = out + taps_ref[j] * ext_ref[first + j:first + j + 8, :, cols]
+            out_ref[first:first + 8, :, cols] = out
         return carry
 
     lax.fori_loop(0, main_ref.shape[2] // lanes, lane_chunk, 0)

time: 518 us -> 518 us (level)
  no operation moved by 1% of the time
where the time goes in v16:
time: 518 us; the launch traced here: 509 us
  other arithmetic  144 us (28%)
  waiting for transfers between devices  110 us (21%)
  local copies, waits for them, and re-layouts  74 us (14%)
  blocking collectives  73.2 us (14%)
  matrix products  48.3 us (9%)
  Pallas kernels  26.5 us (5%)
  starting transfers between devices  17.9 us (3%)
  between operations  15.1 us (3%)
    all_to_all x2, waiting for transfers between devices, traverse(): lax.all_to_all(blocks, ('inline', 'xline'), split_axis=0, concat_axis=0,...  85.3 us
    convert_element_type x7, other arithmetic, split(): return (high.astype(jnp.bfloat16), (x - high).astype(jnp.bfloat16))  83.6 us
    all_gather x1, blocking collectives, local(): tables_all = jnp.round(lax.all_gather(tables, axes, axis=0, tiled=True))  59.6 us
    add x1, other arithmetic, filter_padded(): result + taps[offset] * lax.slice_in_dim(padded, offset, offset + length,...  24.6 us
    scatter-add x1, other arithmetic, local(): raw_gradient = jnp.zeros((cell_count, depth_len), jnp.float32).at[cells.r...  23.1 us
    dot_general x2, matrix products, local(): lax.dot_general(jnp.take(tile_rows, wanted, axis=0), weight_matrix, contr...  17.1 us
    dot_general x1, matrix products, local(): jnp.dot(flat, w_low, preferred_element_type=jnp.float32)  16.2 us
    gather x2, local copies, waits for them, and re-layouts, local(): jnp.take(tile_rows, wanted, axis=0)  15.4 us
  transfers between devices with their start and end apart: 7, of which 5 were waited for; matrix products, arithmetic and copies ran while one was open for 30% of the time, Pallas kernels for 2%

profile of v16, /device:TPU:1, one launch (start us, length us, event | category | flops | bytes accessed | tf_op | source)
XLA Modules:
  0.0 509.4 jit_solution(15174354491468963058)
XLA Ops:
  11.1 13.6 %all_to_all.19 = s32[32,1,64]{2,1,0:T(1,128)S(1)} all-to-all(s32[32,1,64]{2,1,0:T(1,128)S(1)} %bitcast.140), channel_id=1, replica_groups=mesh['inline'=4,'xline'=8] {'inline','xline'}, dimensions={0} | all-to-all | bytes 16384 | tf_op jit(solution)/shard_map/all_to_all | solution.py:208
  25.1 7.7 %gather_fusion.3 = bf16[1024,1024]{1,0:T(8,128)(2,1)S(1)} fusion(bf16[2048,1024]{1,0:T(8,128)(2,1)} %bitcast.118, s32[1024]{0:T(1024)S(1)} %fusion.82), kind=kCustom, calls=%fused_computation.clone | custom fusion | bytes 4198400 | tf_op jit(solution)/shard_map/jit(_take)/gather | solution.py:225
  32.8 8.6 %fusion.27 = bf16[1024,2048]{1,0:T(8,128)(2,1)} fusion(bf16[1,1,2048,1024]{3,2,1,0:T(8,128)(2,1)} %param.12, bf16[1024,1024]{1,0:T(8,128)(2,1)S(1)} %gather_fusion.3, pred[1024]{0:T(1024)(128)(4,1)S(1)} %compare_and_fusion.1), kind=kOutput, calls=%fused_computation.50 | convolution fusion | flops 4298113024 | bytes 10486784 | tf_op jit(solution)/shard_map/dot_general | solution.py:224
  45.3 7.7 %gather_fusion.5 = bf16[1024,1024]{1,0:T(8,128)(2,1)S(1)} fusion(bf16[2048,1024]{1,0:T(8,128)(2,1)} %bitcast.119, s32[1024]{0:T(1024)S(1)} %fusion.83), kind=kCustom, calls=%fused_computation.2.clone | custom fusion | bytes 4198400 | tf_op jit(solution)/shard_map/jit(_take)/gather | solution.py:225
  53.1 8.5 %fusion.30 = bf16[1024,2048]{1,0:T(8,128)(2,1)} fusion(bf16[1,1,2048,1024]{3,2,1,0:T(8,128)(2,1)} %param.12, bf16[1024,1024]{1,0:T(8,128)(2,1)S(1)} %gather_fusion.5, pred[1024]{0:T(1024)(128)(4,1)S(1)} %compare_and_fusion), kind=kOutput, calls=%fused_computation.51 | convolution fusion | flops 4298113024 | bytes 10486784 | tf_op jit(solution)/shard_map/dot_general | solution.py:224
  61.6 79.3 %all-to-all-done.1 = bf16[32,32,2048]{2,1,0:T(8,128)(2,1)} async-done(((bf16[32,32,2048]{2,1,0:T(8,128)(2,1)}), bf16[32,32,2048]{2,1,0:T(8,128)(2,1)}, u32[]{:S(2)}, u32[]{:S(2)}) %all-to-all-start.1) | async-done | bytes 4194336 | tf_op jit(solution)/shard_map/all_to_all | solution.py:175
  146.3 20.5 %fusion.43 = bf16[256,128]{1,0:T(8,128)(2,1)S(1)} fusion(f32[]{:T(128)} %bitcast.24, f32[]{:T(128)} %bitcast.25, f32[]{:T(128)} %bitcast.26, f32[]{:T(128)} %bitcast.27, f32[]{:T(128)} %bitcast.28, f32[]{:T(128)} %bitcast.29, f32[]{:T(128)} %bitcast.30, f32[]{:T(128)} %bitcast.31, f32[]{:T(128)} %bitcast.32, f32[]{:T(128)} %bitcast.33, f32[]{:T(128)} %bitcast.34, ...), kind=kLoop, calls=%fused_computation.79 | loop fusion | flops 2326528 | bytes 65668 | tf_op jit(solution)/shard_map/convert_element_type | solution.py:137
  166.9 20.5 %reduce-precision_convert_fusion.4 = bf16[256,128]{1,0:T(8,128)(2,1)S(1)} fusion(f32[]{:T(128)} %bitcast.24, f32[]{:T(128)} %bitcast.25, f32[]{:T(128)} %bitcast.26, f32[]{:T(128)} %bitcast.27, f32[]{:T(128)} %bitcast.28, f32[]{:T(128)} %bitcast.29, f32[]{:T(128)} %bitcast.30, f32[]{:T(128)} %bitcast.31, f32[]{:T(128)} %bitcast.32, f32[]{:T(128)} %bitcast.33, ...), kind=kLoop, calls=%fused_computation.75 | loop fusion | flops 2293760 | bytes 65668 | tf_op jit(solution)/shard_map/convert_element_type | solution.py:137
  187.4 20.5 %fusion.42 = bf16[256,128]{1,0:T(8,128)(2,1)S(1)} fusion(f32[]{:T(128)} %bitcast.56, f32[]{:T(128)} %bitcast.55, f32[]{:T(128)} %bitcast.54, f32[]{:T(128)} %bitcast.53, f32[]{:T(128)} %bitcast.52, f32[]{:T(128)} %bitcast.51, f32[]{:T(128)} %bitcast.50, f32[]{:T(128)} %bitcast.49, f32[]{:T(128)} %bitcast.48, f32[]{:T(128)} %bitcast.47, f32[]{:T(128)} %bitcast.46, ...), kind=kLoop, calls=%fused_computation.78 | loop fusion | flops 2326528 | bytes 65668 | tf_op jit(solution)/shard_map/convert_element_type | solution.py:137
  208.0 20.5 %reduce-precision_convert_fusion.5 = bf16[256,128]{1,0:T(8,128)(2,1)S(1)} fusion(f32[]{:T(128)} %bitcast.56, f32[]{:T(128)} %bitcast.55, f32[]{:T(128)} %bitcast.54, f32[]{:T(128)} %bitcast.53, f32[]{:T(128)} %bitcast.52, f32[]{:T(128)} %bitcast.51, f32[]{:T(128)} %bitcast.50, f32[]{:T(128)} %bitcast.49, f32[]{:T(128)} %bitcast.48, f32[]{:T(128)} %bitcast.47, ...), kind=kLoop, calls=%fused_computation.77 | loop fusion | flops 2293760 | bytes 65668 | tf_op jit(solution)/shard_map/convert_element_type | solution.py:137
  229.6 5.0 gather_fusion.4
  234.6 5.9 %all-to-all-done.2 = bf16[32,32,2048]{2,1,0:T(8,128)(2,1)} async-done(((bf16[32,32,2048]{2,1,0:T(8,128)(2,1)}), bf16[32,32,2048]{2,1,0:T(8,128)(2,1)}, u32[]{:S(2)}, u32[]{:S(2)}) %all-to-all-start.2) | async-done | bytes 4194336 | tf_op jit(solution)/shard_map/all_to_all | solution.py:175
  240.5 5.0 gather_fusion.6
  265.5 59.6 %all_gather.6 = f32[512,72]{1,0:T(8,128)S(1)} all-gather(f32[16,72]{1,0:T(8,128)S(1)} %add_convert_fusion), channel_id=1, replica_groups=mesh['inline'=4,'xline'=8] {'inline','xline'}, dimensions={0}, use_global_device_ids=true | all-gather | bytes 152064 | tf_op jit(solution)/shard_map/all_gather | solution.py:192
  331.3 6.0 %gather_fusion.2 = s32[512,8]{1,0:T(8,128)S(1)} fusion(s32[512,8,8]{1,2,0:T(8,128)} %copy.89, s32[512]{0:T(512)S(1)} %bitcast.122), kind=kCustom, calls=%fused_computation.6 | custom fusion | bytes 36864 | tf_op jit(solution)/shard_map/jit(take_along_axis)/gather | solution.py:262
  343.8 24.6 %fusion.8 = f32[2048,1024]{1,0:T(8,128)} fusion(f32[2048,1024]{1,0:T(8,128)S(1)} %bitcast_convert_fusion, f32[]{:T(128)} %bitcast.73, f32[]{:T(128)} %bitcast.72, f32[]{:T(128)} %bitcast.71, f32[]{:T(128)} %bitcast.70, f32[]{:T(128)} %bitcast.69, f32[]{:T(128)} %bitcast.68, f32[]{:T(128)} %bitcast.67, f32[]{:T(128)} %bitcast.66, f32[]{:T(128)} %bitcast.65), kind=kLoop, calls=%fused_computation.28 | loop fusion | flops 35651584 | bytes 16777252 | tf_op jit(solution)/shard_map/add | solution.py:168
  368.4 10.4 %all-gather.2.cloned.1.call-done = bf16[4096,2048]{1,0:T(8,128)(2,1)} async-done(((bf16[128,2048]{1,0:T(8,128)(2,1)}), bf16[4096,2048]{1,0:T(8,128)(2,1)}) %all-gather.2.cloned.1.call-update) | async-done | bytes 16777232 | tf_op jit(solution)/shard_map/all_gather | solution.py:246
  378.8 14.4 %gather_fusion.1 = bf16[256,8,2048]{2,1,0:T(8,128)(2,1)} fusion(bf16[512,8,2048]{2,1,0:T(8,128)(2,1)} %bitcast.132, s32[1024]{0:T(1024)S(1)} %pad_clamp_fusion.1), kind=kCustom, calls=%fused_computation.5 | custom fusion | bytes 16778240 | tf_op jit(solution)/shard_map/jit(_take)/gather | solution.py:268
  393.2 16.2 %fusion.19 = f32[2048,1024]{1,0:T(8,128)} fusion(f32[2048,1024]{1,0:T(8,128)} %fusion.8, bf16[256,8,2048]{2,1,0:T(8,128)(2,1)} %gather_fusion.1, pred[2048]{0:T(1024)(128)(4,1)S(1)} %broadcast_in_dim.240), kind=kOutput, calls=%fused_computation.41 | convolution fusion | flops 8600420352 | bytes 25167872 | tf_op jit(solution)/shard_map/dot_general | solution.py:273
  409.4 11.1 %fusion.21 = f32[2048,1024]{1,0:T(8,128)} fusion(f32[2048,1024]{1,0:T(8,128)S(1)} %copy-done, bf16[256,8,2048]{2,1,0:T(8,128)(2,1)S(1)} %copy-done.1, pred[2048]{0:T(1024)(128)(4,1)S(1)} %broadcast_in_dim.240), kind=kOutput, calls=%fused_computation.42 | convolution fusion | flops 8598323200 | bytes 25167872 | tf_op jit(solution)/shard_map/dot_general | solution.py:273
  420.6 23.1 %scatter_custom_fusion.2 = f32[2048,1024]{1,0:T(8,128)} fusion(s32[2048]{0:T(1024)S(1)} %bitcast.141, f32[2048,1024]{1,0:T(8,128)} %fusion.21, f32[2048,1024]{1,0:T(8,128)} %fusion.19, f32[]{:T(128)} %constant.62.clone.1), kind=kCustom, calls=%fused_computation.39 | custom fusion | flops 4194304 | bytes 25165828 | tf_op jit(solution)/shard_map/scatter-add | solution.py:279
  450.3 9.8 %collective-permute-done.low_ref = f32[4,64,1024]{2,1,0:T(8,128)S(1)} collective-permute-done((f32[4,64,1024]{2,1,0:T(8,128)S(1)}, f32[4,64,1024]{2,1,0:T(8,128)S(1)}, u32[]{:S(2)}, u32[]{:S(2)}) %collective-permute-start) | collective-permute-done | bytes 1048608 | tf_op jit(solution)/shard_map/ppermute | solution.py:105
  477.8 8.9 %shard_map.87.middle_ref = f32[32,48,1024]{2,1,0:T(8,128)} custom-call(f32[9]{0:T(128)} %taps_ref.5, f32[32,64,1024]{2,1,0:T(8,128)} %bitcast.121, f32[4,64,1024]{2,1,0:T(8,128)} %copy-done.2, f32[4,64,1024]{2,1,0:T(8,128)} %collective-permute-done.1.high_ref), custom_call_target="tpu_custom_call" | custom-call | flops 62914560 | bytes 15728640 | tf_op jit(solution)/shard_map/pallas_call | solution.py:32
  488.3 13.8 %shard_map.88 = f32[32,64,1024]{2,1,0:T(8,128)} custom-call(f32[9]{0:T(128)} %taps_ref.5, f32[32,16,1024]{2,1,0:T(8,128)} %shard_map.86.first_ref.last_ref, f32[32,48,1024]{2,1,0:T(8,128)} %shard_map.87.middle_ref, f32[32,16,1024]{2,1,0:T(8,128)} %shard_map.86.first_ref.last_ref, f32[32,4,1024]{2,1,0:T(4,128)} %copy-done.5, f32[32,4,1024]{2,1,0:T(4,128)} %copy-done.4), custom_call_target="tpu_custom_call" | custom-call | flops 37748736 | bytes 18454936 | tf_op jit(solution)/shard_map/pallas_call | solution.py:77
  (128 shorter events, 72.8 us)
Async XLA Ops:
  41.4 99.6 %all-to-all-start.1 = ((bf16[32,32,2048]{2,1,0:T(8,128)(2,1)}), bf16[32,32,2048]{2,1,0:T(8,128)(2,1)}, u32[]{:S(2)}, u32[]{:S(2)}) async-start(bf16[32,32,2048]{2,1,0:T(8,128)(2,1)} %bitcast.134), calls=%async_computation.1 | async-start | bytes 8388608 | tf_op jit(solution)/shard_map/all_to_all | solution.py:175
  61.6 83.3 %copy-start.3 = (f32[33]{0:T(128)S(1)}, f32[33]{0:T(128)}, u32[]{:S(2)}) copy-start(f32[33]{0:T(128)} %param.14) | copy-start | bytes 400
  61.6 166.9 %copy-start.6 = (bf16[128,2048]{1,0:T(8,128)(2,1)S(1)}, bf16[128,2048]{1,0:T(8,128)(2,1)}, u32[]{:S(2)}) copy-start(bf16[128,2048]{1,0:T(8,128)(2,1)} %param.13) | copy-start | bytes 1572868
  140.9 99.5 %all-to-all-start.2 = ((bf16[32,32,2048]{2,1,0:T(8,128)(2,1)}), bf16[32,32,2048]{2,1,0:T(8,128)(2,1)}, u32[]{:S(2)}, u32[]{:S(2)}) async-start(bf16[32,32,2048]{2,1,0:T(8,128)(2,1)} %bitcast.133), calls=%async_computation.2 | async-start | bytes 8388608 | tf_op jit(solution)/shard_map/all_to_all | solution.py:175
  144.7 234.1 %all-gather.2.cloned.1.call-start = ((), (), s32[]{:S(2)}) async-start(), calls=%async_computation.3 | async-start | bytes 17301504 | tf_op jit(solution)/shard_map/all_gather | solution.py:246
  258.4 6.8 %copy-start.8 = (s32[128,8]{0,1:T(8,128)S(1)}, s32[128,8]{0,1:T(8,128)}, u32[]{:S(2)}) copy-start(s32[128,8]{0,1:T(8,128)} %param.17) | copy-start | bytes 12292
  262.1 77.8 %copy-start.7 = (f32[9]{0:T(128)S(1)}, f32[9]{0:T(128)}, u32[]{:S(2)}) copy-start(f32[9]{0:T(128)} %taps_ref.5) | copy-start | bytes 112
  393.2 16.2 %copy-start = (f32[2048,1024]{1,0:T(8,128)S(1)}, f32[2048,1024]{1,0:T(8,128)}, u32[]{:S(2)}) copy-start(f32[2048,1024]{1,0:T(8,128)} %fusion.8) | copy-start | bytes 25165828
  393.2 16.2 %copy-start.1 = (bf16[256,8,2048]{2,1,0:T(8,128)(2,1)S(1)}, bf16[256,8,2048]{2,1,0:T(8,128)(2,1)}, u32[]{:S(2)}) copy-start(bf16[256,8,2048]{2,1,0:T(8,128)(2,1)} %gather_fusion.1) | copy-start | bytes 25165828
  445.3 14.7 %collective-permute-start = (f32[4,64,1024]{2,1,0:T(8,128)S(1)}, f32[4,64,1024]{2,1,0:T(8,128)S(1)}, u32[]{:S(2)}, u32[]{:S(2)}) collective-permute-start(f32[4,64,1024]{2,1,0:T(8,128)S(1)} %bitcast.137), channel_id=1, source_target_pairs={{0,8},{8,16},{16,24},{1,9},{9,17},{17,25},{2,10},{10,18},{18,26},{... | collective-permute-start | bytes 3145736 | tf_op jit(solution)/shard_map/ppermute | solution.py:105
  448.3 16.4 %collective-permute-start.1 = (f32[4,64,1024]{2,1,0:T(8,128)S(1)}, f32[4,64,1024]{2,1,0:T(8,128)}, u32[]{:S(2)}, u32[]{:S(2)}) collective-permute-start(f32[4,64,1024]{2,1,0:T(8,128)S(1)} %bitcast.136), channel_id=1, source_target_pairs={{8,0},{16,8},{24,16},{9,1},{17,9},{25,17},{10,2},{18,10},{26,18},{... | collective-permute-start | bytes 3145736 | tf_op jit(solution)/shard_map/ppermute | solution.py:108
  460.1 4.7 copy-start.2
  471.2 15.5 %collective-permute-start.3 = (f32[32,4,1024]{2,1,0:T(4,128)}, f32[32,4,1024]{2,1,0:T(4,128)S(1)}, u32[]{:S(2)}, u32[]{:S(2)}) collective-permute-start(f32[32,4,1024]{2,1,0:T(4,128)} %get-tuple-element.32), channel_id=1, source_target_pairs={{1,0},{2,1},{3,2},{4,3},{5,4},{6,5},{7,6},{9,8},{10,9},{11,10},{12... | collective-permute-start | bytes 1572872 | tf_op jit(solution)/shard_map/ppermute | solution.py:108
  472.5 14.2 %collective-permute-start.2 = (f32[32,4,1024]{2,1,0:T(4,128)S(1)}, f32[32,4,1024]{2,1,0:T(4,128)S(1)}, u32[]{:S(2)}, u32[]{:S(2)}) collective-permute-start(f32[32,4,1024]{2,1,0:T(4,128)S(1)} %get-tuple-element.33), channel_id=1, source_target_pairs={{0,1},{1,2},{2,3},{3,4},{4,5},{5,6},{6,7},{8,9},{9,10},{10,11},{11... | collective-permute-start | bytes 1572872 | tf_op jit(solution)/shard_map/ppermute | solution.py:105
  486.7 0.8 copy-start.4
  487.5 0.8 copy-start.5
Sparse Core Ops, SparseCore 0:
  265.3 113.4 all-gather.1
